TPU v7x, 512 devices: a whole 4x4x16 slice. The times are simulated.
512 devices in a mesh: chan: 32 (over z, x_hi), seg: 16 (over y, x_lo, core).
Axes of the slice: x: 4 (x_hi: 2, x_lo: 2; x = x_hi * 2 + x_lo), y: 4, z: 16, core: 2. Of those that a mesh axis runs over, the one named last changes fastest.
Arguments:
- traces: bfloat16 [512, 16, 384], P('chan', 'seg')
- taper_len: int32 [512], P('chan'), may hold values from 1 to 192
- gather_id: int32 [512, 512], P('chan'), may hold values from 0 to 511, as said below
- offset_bin: int32 [512, 512], P('chan'), may hold values from 0 to 1, as said below
Outputs:
- stack: float32 [512, 2, 256], P(('chan', 'seg'))
Inputs may be any that keep to these rules, and one draw needn't show every extreme that they name: Channels lie on a fiber at integer positions p_0 < p_1 < ... with steps of 2 to 5; gather_id[i, j] = floor((p_i + p_j - 2 p_0) * 512 / (2 (p_last - p_0) + 1)). offset_bin[i, j] = floor(|p_i - p_j| * 2 / (p_last - p_0 + 1)) with the same positions.
All inputs are finite; a program needn't handle non-finite values.
Results may differ from a plain program's by a relative error of at most 0.0039.
Values may be sent and summed in bfloat16 or wider, within the bound.
No kernel may reach another device: no remote copies, remote signals or barrier semaphores. Data moves between devices by JAX's collectives and lax.ppermute only.
A program may use at most 64 MiB of HBM per device.

v0:
```python
import math

import jax
import jax.numpy as jnp
from jax import lax
from jax.sharding import PartitionSpec as P

LAGS = 256
OFFBINS = 2


def normalize(traces, taper_len):
    values = traces.astype(jnp.float32)
    sample_count = values.shape[2]
    power = jnp.mean(values * values, axis=2, keepdims=True)
    times = jnp.arange(sample_count).astype(jnp.float32)
    length = taper_len.astype(jnp.float32)[:, None, None]
    window = jnp.minimum(1.0, jnp.minimum((times + 1.0) / length, (sample_count - times) / length))
    return (window * values * lax.rsqrt(power + 1e-06)).astype(jnp.bfloat16)


def hankel(normed, lag_count):
    chan_count, seg_count, sample_count = normed.shape
    turned = jnp.transpose(normed, (1, 2, 0))
    padded = jnp.pad(turned, ((0, 0), (lag_count // 2, lag_count // 2), (0, 0)))
    slices = [padded[:, lag_count - k : lag_count - k + sample_count, :] for k in range(lag_count)]
    picked = jnp.stack(slices, axis=3)
    return picked.reshape(seg_count * sample_count, chan_count * lag_count)


def shards(traces, taper_len, gather_id, offset_bin):
    chan_count = traces.shape[0]
    chan_devices = lax.axis_size("chan")
    seg_devices = lax.axis_size("seg")
    bucket_count = chan_devices * seg_devices * OFFBINS
    normed = normalize(traces, taper_len)
    kernel = hankel(normed, LAGS)
    first_row = lax.axis_index("chan") * chan_count
    own_rows = first_row + jnp.arange(chan_count, dtype=jnp.int32)[None, :]
    empty = jnp.zeros((bucket_count, LAGS), jnp.float32)
    piece = lax.all_gather(normed, "chan", axis=0, tiled=True)
    row_count = piece.shape[0]
    product = jnp.dot(piece.reshape(row_count, -1), kernel, preferred_element_type=jnp.float32)
    product = product.reshape(row_count * chan_count, LAGS)
    labels = jnp.transpose(gather_id * OFFBINS + offset_bin)
    partner = jnp.arange(row_count, dtype=jnp.int32)[:, None]
    labels = jnp.where(partner == own_rows, bucket_count, labels).reshape(-1)
    total = empty.at[labels].add(product, mode="drop")
    scale = 1.0 / math.sqrt(traces.shape[2] * traces.shape[1] * seg_devices)
    stacked = (total * scale).reshape(chan_devices * seg_devices, OFFBINS, LAGS)
    result = lax.psum_scatter(stacked, ("chan", "seg"), scatter_dimension=0, tiled=True)
    return result


def solution(mesh):
    placed = (P("chan", "seg", None), P("chan"), P("chan", None), P("chan", None))
    return jax.shard_map(
        shards,
        mesh=mesh,
        in_specs=placed,
        out_specs=P(("chan", "seg"), None, None),
        check_vma=False,
    )
```

profile of v0, /device:TPU:1, one launch (start us, length us, event | category | flops | bytes accessed | tf_op | source)
XLA Modules:
  0.0 647.5 jit_solution(15832972223417551559)
XLA Ops:
  6.5 0.9 fusion.7
  7.4 0.7 convert_element_type.24
  8.1 0.8 fusion.264
  8.9 0.8 fusion.6
  10.2 0.1 constant_dynamic-update-slice_fusion.248
  10.3 0.1 constant_dynamic-update-slice_fusion.247
  10.4 0.1 constant_dynamic-update-slice_fusion.246
  10.4 0.1 constant_dynamic-update-slice_fusion.245
  10.5 0.1 constant_dynamic-update-slice_fusion.244
  10.6 0.1 constant_dynamic-update-slice_fusion.243
  10.7 0.1 constant_dynamic-update-slice_fusion.242
  10.8 0.1 constant_dynamic-update-slice_fusion.241
  20.1 0.1 constant_dynamic-update-slice_fusion.127
  30.5 0.8 copy.264
  31.3 71.5 %all_gather.3 = bf16[512,1,384]{2,0,1:T(8,128)(2,1)S(1)} all-gather(bf16[16,1,384]{2,0,1:T(8,128)(2,1)S(1)} %fusion.6), channel_id=1, replica_groups=mesh['chan'=32,'seg'=16] {'chan'}, dimensions={0}, use_global_device_ids=true | all-gather | bytes 405504 | tf_op jit(solution)/shard_map/all_gather | solution.py:41
  102.8 5.6 fusion.2
  108.4 9.3 %reshape.172 = f32[8192,256]{1,0:T(8,128)} reshape(f32[512,4096]{1,0:T(8,128)} %fusion.2) | data formatting | bytes 16777216 | tf_op jit(solution)/shard_map/reshape | solution.py:44
  117.8 0.1 copy.263
  117.9 0.2 reshape.163
  118.1 44.9 %scatter_custom_fusion = f32[1024,256]{1,0:T(8,128)S(1)} fusion(s32[8192]{0:T(1024)S(1)} %bitcast.1034, f32[8192,256]{1,0:T(8,128)} %reshape.172, f32[]{:T(128)} %constant.13.clone.1), kind=kCustom, calls=%fused_computation.258 | custom fusion | flops 2097152 | bytes 1049088 | tf_op jit(solution)/shard_map/scatter-add | solution.py:48
  163.0 0.1 broadcast_multiply_fusion
  163.1 1.7 reshape.167
  164.7 474.7 %all-reduce.4.cloned.1.call-done = f32[512,2,256]{2,1,0:T(2,128)} async-done(((f32[512,2,256]{2,1,0:T(2,128)}), f32[512,2,256]{2,1,0:T(2,128)}) %all-reduce.4.cloned.1.call-update) | async-done | bytes 1048592
  639.4 1.2 constant_dynamic-slice_fusion
  (260 shorter events, 20.1 us)
Async XLA Ops:
  6.5 13.5 %copy-start = (bf16[16,1,384]{2,0,1:T(8,128)(2,1)S(1)}, bf16[16,1,384]{2,0,1:T(8,128)(2,1)}, u32[]{:S(2)}) copy-start(bf16[16,1,384]{2,0,1:T(8,128)(2,1)} %param.4) | copy-start | bytes 36868
  6.5 632.9 %all-reduce.4.cloned.1.call-start = ((), (), s32[]{:S(2)}) async-start(), calls=%async_computation | async-start | bytes 2097152
  108.4 9.3 %copy-start.1 = (s32[16,512]{1,0:T(8,128)S(1)}, s32[16,512]{1,0:T(8,128)}, u32[]{:S(2)}) copy-start(s32[16,512]{1,0:T(8,128)} %param.7) | copy-start | bytes 98308
  108.4 9.3 %copy-start.2 = (s32[16,512]{1,0:T(8,128)S(1)}, s32[16,512]{1,0:T(8,128)}, u32[]{:S(2)}) copy-start(s32[16,512]{1,0:T(8,128)} %param.6) | copy-start | bytes 98308
Sparse Core Ops, SparseCore 0:
  164.9 474.5 all-reduce.3
where the time goes:
time: 648 us
  waiting for transfers between devices  475 us (73%)
  blocking collectives  71.5 us (11%)
  other arithmetic  48.3 us (7%)
  local copies, waits for them, and re-layouts  33.8 us (5%)
  between operations  13.6 us (2%)
    unnamed x2, waiting for transfers between devices  475 us
    all_gather x1, blocking collectives, shards(): piece = lax.all_gather(normed, 'chan', axis=0, tiled=True)  71.5 us
    scatter-add x1, other arithmetic, shards(): total = empty.at[labels].add(product, mode='drop')  44.9 us
    unnamed x261, local copies, waits for them, and re-layouts  21.8 us
  transfers between devices with their start and end apart: 1, of which 1 were waited for; matrix products, arithmetic and copies ran while one was open for 0% of the time, Pallas kernels for 0%

commit v1 on v0

--- a/solution.py
+++ b/solution.py
@@ -38,17 +38,21 @@
     first_row = lax.axis_index("chan") * chan_count
     own_rows = first_row + jnp.arange(chan_count, dtype=jnp.int32)[None, :]
     empty = jnp.zeros((bucket_count, LAGS), jnp.float32)
-    piece = lax.all_gather(normed, "chan", axis=0, tiled=True)
+    flat = lax.optimization_barrier(normed.reshape(chan_count, -1))
+    piece = lax.all_gather(flat, "chan", axis=0, tiled=True)
     row_count = piece.shape[0]
-    product = jnp.dot(piece.reshape(row_count, -1), kernel, preferred_element_type=jnp.float32)
+    product = jnp.dot(piece, kernel, preferred_element_type=jnp.float32)
     product = product.reshape(row_count * chan_count, LAGS)
     labels = jnp.transpose(gather_id * OFFBINS + offset_bin)
     partner = jnp.arange(row_count, dtype=jnp.int32)[:, None]
     labels = jnp.where(partner == own_rows, bucket_count, labels).reshape(-1)
     total = empty.at[labels].add(product, mode="drop")
     scale = 1.0 / math.sqrt(traces.shape[2] * traces.shape[1] * seg_devices)
-    stacked = (total * scale).reshape(chan_devices * seg_devices, OFFBINS, LAGS)
-    result = lax.psum_scatter(stacked, ("chan", "seg"), scatter_dimension=0, tiled=True)
+    stacked = (total * scale).reshape(chan_devices, seg_devices, OFFBINS, LAGS)
+    stacked = jnp.transpose(stacked, (1, 0, 2, 3))
+    part = lax.psum_scatter(stacked, "seg", scatter_dimension=0, tiled=True)
+    part = part.reshape(chan_devices, OFFBINS, LAGS)
+    result = lax.psum_scatter(part, "chan", scatter_dimension=0, tiled=True)
     return result
 
 

time: 648 us -> 546 us (0.84)
  the two profiles are of different devices: /device:TPU:1 before, /device:TPU:8 now
where the time goes in v1:
time: 546 us; the launch traced here: 545 us
  waiting for transfers between devices  355 us (65%)
  blocking collectives  84.6 us (15%)
  other arithmetic  48.3 us (9%)
  local copies, waits for them, and re-layouts  37.7 us (7%)
  between operations  13.6 us (2%)
  matrix products  5.6 us (1%)
    unnamed x3, waiting for transfers between devices  299 us
    all_gather x1, blocking collectives, shards(): piece = lax.all_gather(flat, 'chan', axis=0, tiled=True)  84.6 us
    reduce_scatter x1, waiting for transfers between devices, shards(): part = lax.psum_scatter(stacked, 'seg', scatter_dimension=0, tiled=True)  56 us
    scatter-add x1, other arithmetic, shards(): total = empty.at[labels].add(product, mode='drop')  44.9 us
    unnamed x262, local copies, waits for them, and re-layouts  23.6 us
  transfers between devices with their start and end apart: 2, of which 2 were waited for; matrix products, arithmetic and copies ran while one was open for 0% of the time, Pallas kernels for 0%

profile of v1, /device:TPU:8, one launch (start us, length us, event | category | flops | bytes accessed | tf_op | source)
XLA Modules:
  0.0 545.1 jit_solution(4039340912734101357)
XLA Ops:
  6.5 0.9 fusion.5
  7.4 0.7 convert_element_type.24
  8.1 0.8 fusion.264
  8.9 0.8 fusion.265
  10.4 0.1 constant_dynamic-update-slice_fusion.246
  10.4 0.1 constant_dynamic-update-slice_fusion.245
  10.5 0.1 constant_dynamic-update-slice_fusion.244
  10.6 0.1 constant_dynamic-update-slice_fusion.243
  20.1 0.1 constant_dynamic-update-slice_fusion.127
  30.5 0.8 copy.264
  31.3 84.6 %all_gather.3 = bf16[512,384]{1,0:T(8,128)(2,1)S(1)} all-gather(bf16[16,384]{1,0:T(8,128)(2,1)S(1)} %fusion.265), channel_id=1, replica_groups=mesh['chan'=32,'seg'=16] {'chan'}, dimensions={0}, use_global_device_ids=true | all-gather | bytes 405504 | tf_op jit(solution)/shard_map/all_gather | solution.py:42
  115.9 5.6 %fusion.261 = f32[512,4096]{1,0:T(8,128)} fusion(bf16[512,384]{1,0:T(8,128)(2,1)S(1)} %all_gather.3, bf16[384,4096]{0,1:T(8,128)(2,1)S(1)} %bitcast.1036), kind=kOutput, calls=%fused_computation.785 | convolution fusion | flops 1610612736 | bytes 11927552 | tf_op jit(solution)/shard_map/dot_general | solution.py:44
  121.5 9.3 %reshape.176 = f32[8192,256]{1,0:T(8,128)} reshape(f32[512,4096]{1,0:T(8,128)} %fusion.261) | data formatting | bytes 16777216 | tf_op jit(solution)/shard_map/reshape | solution.py:45
  130.9 0.1 copy.263
  131.0 0.2 reshape.166
  131.2 44.9 %scatter_custom_fusion = f32[1024,256]{1,0:T(8,128)S(1)} fusion(s32[8192]{0:T(1024)S(1)} %bitcast.1039, f32[8192,256]{1,0:T(8,128)} %reshape.176, f32[]{:T(128)} %constant.13.clone.1), kind=kCustom, calls=%fused_computation.258 | custom fusion | flops 2097152 | bytes 1049088 | tf_op jit(solution)/shard_map/scatter-add | solution.py:49
  176.1 0.1 broadcast_multiply_fusion
  176.2 0.6 reshape.170
  176.8 1.6 copy.265
  178.5 56.0 %reduce-scatter.2.cloned.1.call-done = f32[1,32,2,256]{3,1,2,0:T(8,128)} async-done(((f32[16,32,2,256]{3,1,2,0:T(8,128)}), f32[1,32,2,256]{3,1,2,0:T(8,128)}) %reduce-scatter.2.cloned.1.call-update) | async-done | bytes 65552 | tf_op jit(solution)/shard_map/reduce_scatter | solution.py:53
  234.5 1.5 copy.266
  236.0 1.3 dynamic-slice
  237.3 299.2 %all-reduce.4.cloned.1.call-done = f32[32,2,256]{2,1,0:T(2,128)} async-done(((f32[32,2,256]{2,1,0:T(2,128)}), f32[32,2,256]{2,1,0:T(2,128)}) %all-reduce.4.cloned.1.call-update) | async-done | bytes 65552
  536.5 1.8 constant_dynamic-slice_fusion
  (266 shorter events, 20.5 us)
Async XLA Ops:
  6.5 13.5 %copy-start = (bf16[16,1,384]{2,0,1:T(8,128)(2,1)S(1)}, bf16[16,1,384]{2,0,1:T(8,128)(2,1)}, u32[]{:S(2)}) copy-start(bf16[16,1,384]{2,0,1:T(8,128)(2,1)} %param.4) | copy-start | bytes 36868
  6.5 227.9 %reduce-scatter.2.cloned.1.call-start = ((), (), s32[]{:S(2)}) async-start(), calls=%async_computation.1 | async-start | bytes 1114112 | tf_op jit(solution)/shard_map/reduce_scatter | solution.py:53
  121.5 9.3 %copy-start.1 = (s32[16,512]{1,0:T(8,128)S(1)}, s32[16,512]{1,0:T(8,128)}, u32[]{:S(2)}) copy-start(s32[16,512]{1,0:T(8,128)} %param.7) | copy-start | bytes 98308
  121.5 9.3 %copy-start.2 = (s32[16,512]{1,0:T(8,128)S(1)}, s32[16,512]{1,0:T(8,128)}, u32[]{:S(2)}) copy-start(s32[16,512]{1,0:T(8,128)} %param.6) | copy-start | bytes 98308
  178.4 358.1 %all-reduce.4.cloned.1.call-start = ((), (), s32[]{:S(2)}) async-start(), calls=%async_computation.2 | async-start | bytes 131072
Sparse Core Ops, SparseCore 0:
  178.6 55.8 reduce-scatter.1
  237.6 298.8 all-reduce.3

commit v2 on v1

--- a/solution.py
+++ b/solution.py
@@ -39,7 +39,8 @@
     own_rows = first_row + jnp.arange(chan_count, dtype=jnp.int32)[None, :]
     empty = jnp.zeros((bucket_count, LAGS), jnp.float32)
     flat = lax.optimization_barrier(normed.reshape(chan_count, -1))
-    piece = lax.all_gather(flat, "chan", axis=0, tiled=True)
+    copies = jnp.broadcast_to(flat[None], (chan_devices,) + flat.shape)
+    piece = lax.all_to_all(copies, "chan", 0, 0, tiled=True).reshape(-1, flat.shape[1])
     row_count = piece.shape[0]
     product = jnp.dot(piece, kernel, preferred_element_type=jnp.float32)
     product = product.reshape(row_count * chan_count, LAGS)
@@ -52,8 +53,8 @@
     stacked = jnp.transpose(stacked, (1, 0, 2, 3))
     part = lax.psum_scatter(stacked, "seg", scatter_dimension=0, tiled=True)
     part = part.reshape(chan_devices, OFFBINS, LAGS)
-    result = lax.psum_scatter(part, "chan", scatter_dimension=0, tiled=True)
-    return result
+    pieces = lax.all_to_all(part, "chan", 0, 0, tiled=True)
+    return jnp.sum(pieces, axis=0, keepdims=True)
 
 
 def solution(mesh):

time: 546 us -> 226 us (0.41)
  the two profiles are of different devices: /device:TPU:8 before, /device:TPU:1 now
where the time goes in v2:
time: 226 us; the launch traced here: 223 us
  waiting for transfers between devices  68.4 us (30%)
  other arithmetic  51.7 us (23%)
  local copies, waits for them, and re-layouts  37.8 us (17%)
  blocking collectives  27.4 us (12%)
  starting transfers between devices  18.5 us (8%)
  between operations  13.6 us (6%)
  matrix products  5.59 us (2%)
    reduce_scatter x1, waiting for transfers between devices, shards(): part = lax.psum_scatter(stacked, 'seg', scatter_dimension=0, tiled=True)  68.3 us
    scatter-add x1, other arithmetic, shards(): total = empty.at[labels].add(product, mode='drop')  44.9 us
    all_to_all x1, blocking collectives, shards(): pieces = lax.all_to_all(part, 'chan', 0, 0, tiled=True)  27.4 us
    unnamed x256, local copies, waits for them, and re-layouts  20.5 us
    all_to_all x1, starting transfers between devices, shards(): lax.all_to_all(copies, 'chan', 0, 0, tiled=True).reshape(-1, flat.shape[1])  18.5 us
    reshape x1, local copies, waits for them, and re-layouts, shards(): product = product.reshape(row_count * chan_count, LAGS)  9.28 us
    dot_general x1, matrix products, shards(): product = jnp.dot(piece, kernel, preferred_element_type=jnp.float32)  5.59 us
  transfers between devices with their start and end apart: 2, of which 1 were waited for; matrix products, arithmetic and copies ran while one was open for 13% of the time, Pallas kernels for 0%

profile of v2, /device:TPU:1, one launch (start us, length us, event | category | flops | bytes accessed | tf_op | source)
XLA Modules:
  0.0 222.9 jit_solution(17874433438483889919)
XLA Ops:
  6.5 0.9 fusion.5
  7.4 0.7 convert_element_type.24
  8.1 0.8 fusion.265
  8.9 0.8 broadcast_in_dim.11
  9.7 18.5 %all-to-all-start = ((bf16[32,16,384]{2,1,0:T(8,128)(2,1)}), bf16[32,16,384]{2,1,0:T(8,128)(2,1)S(1)}, u32[]{:S(2)}, u32[]{:S(2)}) async-start(bf16[32,16,384]{2,1,0:T(8,128)(2,1)} %broadcast_in_dim.11), calls=%async_computation | async-start | bytes 786432 | tf_op jit(solution)/shard_map/all_to_all | solution.py:43
  28.2 0.8 fusion.264
  29.5 0.1 constant_dynamic-update-slice_fusion.248
  29.6 0.1 constant_dynamic-update-slice_fusion.247
  39.4 0.1 constant_dynamic-update-slice_fusion.127
  49.8 0.8 copy.269
  50.6 1.4 bitcast_select_fusion
  52.1 1.6 copy.268
  53.7 1.7 reshape.170
  55.4 1.4 compare_select_fusion
  56.7 5.6 %fusion.261 = f32[512,4096]{1,0:T(8,128)} fusion(bf16[512,384]{1,0:T(8,128)(2,1)S(1)} %bitcast.1039, bf16[384,4096]{0,1:T(8,128)(2,1)S(1)} %bitcast.1037), kind=kOutput, calls=%fused_computation.784 | convolution fusion | flops 1610612736 | bytes 11927552 | tf_op jit(solution)/shard_map/dot_general | solution.py:45
  62.3 9.3 %reshape.181 = f32[8192,256]{1,0:T(8,128)} reshape(f32[512,4096]{1,0:T(8,128)} %fusion.261) | data formatting | bytes 16777216 | tf_op jit(solution)/shard_map/reshape | solution.py:46
  71.6 44.9 %scatter_custom_fusion = f32[1024,256]{1,0:T(8,128)S(1)} fusion(s32[8192]{0:T(1024)} %bitcast.1041, f32[8192,256]{1,0:T(8,128)} %reshape.181, f32[]{:T(128)} %constant.13.clone.1), kind=kCustom, calls=%fused_computation.258 | custom fusion | flops 2097152 | bytes 1049088 | tf_op jit(solution)/shard_map/scatter-add | solution.py:50
  116.5 0.1 broadcast_multiply_fusion
  116.6 0.6 reshape.175
  117.2 1.6 copy.270
  118.8 68.3 %reduce-scatter.2.cloned.1.call-done = f32[1,32,2,256]{3,1,2,0:T(8,128)} async-done(((f32[16,32,2,256]{3,1,2,0:T(8,128)}), f32[1,32,2,256]{3,1,2,0:T(8,128)}) %reduce-scatter.2.cloned.1.call-update) | async-done | bytes 65552 | tf_op jit(solution)/shard_map/reduce_scatter | solution.py:54
  187.2 0.9 copy.271
  188.1 27.4 %all_to_all.10 = f32[32,2,256]{2,1,0:T(2,128)S(1)} all-to-all(f32[32,2,256]{2,1,0:T(2,128)S(1)} %copy.271), channel_id=1, replica_groups=mesh['chan'=32,'seg'=16] {'chan'}, dimensions={0} | all-to-all | bytes 131072 | tf_op jit(solution)/shard_map/all_to_all | solution.py:56
  215.4 0.6 reduce_sum.19
  (261 shorter events, 20.5 us)
Async XLA Ops:
  6.5 32.8 %copy-start = (bf16[16,1,384]{2,0,1:T(8,128)(2,1)S(1)}, bf16[16,1,384]{2,0,1:T(8,128)(2,1)}, u32[]{:S(2)}) copy-start(bf16[16,1,384]{2,0,1:T(8,128)(2,1)} %param.4) | copy-start | bytes 36868
  9.7 47.1 %all-to-all-start = ((bf16[32,16,384]{2,1,0:T(8,128)(2,1)}), bf16[32,16,384]{2,1,0:T(8,128)(2,1)S(1)}, u32[]{:S(2)}, u32[]{:S(2)}) async-start(bf16[32,16,384]{2,1,0:T(8,128)(2,1)} %broadcast_in_dim.11), calls=%async_computation | async-start | bytes 786432 | tf_op jit(solution)/shard_map/all_to_all | solution.py:43
  28.2 159.0 %reduce-scatter.2.cloned.1.call-start = ((), (), s32[]{:S(2)}) async-start(), calls=%async_computation.3 | async-start | bytes 1114112 | tf_op jit(solution)/shard_map/reduce_scatter | solution.py:54
Sparse Core Ops, SparseCore 0:
  119.0 68.1 reduce-scatter.1

commit v3 on v2

--- a/solution.py
+++ b/solution.py
@@ -37,7 +37,6 @@
     kernel = hankel(normed, LAGS)
     first_row = lax.axis_index("chan") * chan_count
     own_rows = first_row + jnp.arange(chan_count, dtype=jnp.int32)[None, :]
-    empty = jnp.zeros((bucket_count, LAGS), jnp.float32)
     flat = lax.optimization_barrier(normed.reshape(chan_count, -1))
     copies = jnp.broadcast_to(flat[None], (chan_devices,) + flat.shape)
     piece = lax.all_to_all(copies, "chan", 0, 0, tiled=True).reshape(-1, flat.shape[1])
@@ -46,14 +45,30 @@
     product = product.reshape(row_count * chan_count, LAGS)
     labels = jnp.transpose(gather_id * OFFBINS + offset_bin)
     partner = jnp.arange(row_count, dtype=jnp.int32)[:, None]
-    labels = jnp.where(partner == own_rows, bucket_count, labels).reshape(-1)
-    total = empty.at[labels].add(product, mode="drop")
+    labels = jnp.where(partner == own_rows, -1, labels).reshape(-1)
+    gathers = chan_devices * seg_devices
+    low_span = 2 * (row_count - 1)
+    reach = (low_span + 5 * (chan_count - 1)) * gathers // (2 * low_span + 1) + 2
+    depth = -(-(reach - 1) // seg_devices) + 1
+    depth = -(-depth // 8) * 8
+    start = gather_id[0, 0]
+    lanes = jnp.arange(seg_devices, dtype=jnp.int32)
+    first = jnp.minimum((start - lanes + seg_devices - 1) // seg_devices, chan_devices - depth)
+    first = jnp.maximum(first, 0)
+    window = (first[:, None] + jnp.arange(depth, dtype=jnp.int32)[None, :]) * seg_devices + lanes[:, None]
+    wanted = (window[:, :, None] * OFFBINS + jnp.arange(OFFBINS, dtype=jnp.int32)).reshape(-1)
+    onehot = (wanted[:, None] == labels[None, :]).astype(jnp.bfloat16)
+    high = product.astype(jnp.bfloat16)
+    low = (product - high.astype(jnp.float32)).astype(jnp.bfloat16)
+    both = jnp.dot(onehot, jnp.concatenate([high, low], axis=1), preferred_element_type=jnp.float32)
+    total = both[:, :LAGS] + both[:, LAGS:]
     scale = 1.0 / math.sqrt(traces.shape[2] * traces.shape[1] * seg_devices)
-    stacked = (total * scale).reshape(chan_devices, seg_devices, OFFBINS, LAGS)
-    stacked = jnp.transpose(stacked, (1, 0, 2, 3))
+    stacked = (total * scale).reshape(seg_devices, depth, OFFBINS, LAGS)
     part = lax.psum_scatter(stacked, "seg", scatter_dimension=0, tiled=True)
-    part = part.reshape(chan_devices, OFFBINS, LAGS)
-    pieces = lax.all_to_all(part, "chan", 0, 0, tiled=True)
+    own_first = first[lax.axis_index("seg")]
+    dense = jnp.zeros((chan_devices, OFFBINS, LAGS), jnp.float32)
+    dense = lax.dynamic_update_slice(dense, part.reshape(depth, OFFBINS, LAGS), (own_first, 0, 0))
+    pieces = lax.all_to_all(dense, "chan", 0, 0, tiled=True)
     return jnp.sum(pieces, axis=0, keepdims=True)
 
 

time: 226 us -> 201 us (0.89)
  other arithmetic: 51.7 us -> 16.2 us
  matrix products: 5.59 us -> 14.5 us
  waiting for transfers between devices: 68.4 us -> 65.4 us
    scatter-add x1 -> x0, other arithmetic: 44.9 us -> none  [shards(): total = empty.at[labels].add(product, mode='drop')]
    convert_element_type x0 -> x1, other arithmetic: none -> 9.27 us  [shards(): low = (product - high.astype(jnp.float32)).astype(jnp.bfloat16)]
    dot_general x0 -> x1, matrix products: none -> 8.87 us  [shards(): jnp.dot(onehot, jnp.concatenate([high, low], axis=1), preferred_element_t...]
    reduce_scatter x1, waiting for transfers between devices: 68.3 us -> 65.3 us  [shards(): part = lax.psum_scatter(stacked, 'seg', scatter_dimension=0, tiled=True)]
    unnamed x256 -> x258, local copies, waits for them, and re-layouts: 20.5 us -> 20.5 us
  transfers between devices with their start and end apart: 2 -> 2, of which waited for: 1 -> 1; matrix products, arithmetic and copies ran while one was open for 13% -> 16% of each run, Pallas kernels for 0% -> 0%
where the time goes in v3:
time: 201 us; the launch traced here: 197 us
  waiting for transfers between devices  65.4 us (33%)
  local copies, waits for them, and re-layouts  39.8 us (20%)
  blocking collectives  27.5 us (14%)
  starting transfers between devices  18.5 us (9%)
  other arithmetic  16.2 us (8%)
  between operations  15.6 us (8%)
  matrix products  14.5 us (7%)
    reduce_scatter x1, waiting for transfers between devices, shards(): part = lax.psum_scatter(stacked, 'seg', scatter_dimension=0, tiled=True)  65.3 us
    all_to_all x1, blocking collectives, shards(): pieces = lax.all_to_all(dense, 'chan', 0, 0, tiled=True)  27.5 us
    unnamed x258, local copies, waits for them, and re-layouts  20.5 us
    all_to_all x1, starting transfers between devices, shards(): lax.all_to_all(copies, 'chan', 0, 0, tiled=True).reshape(-1, flat.shape[1])  18.5 us
    reshape x1, local copies, waits for them, and re-layouts, shards(): product = product.reshape(row_count * chan_count, LAGS)  9.28 us
    convert_element_type x1, other arithmetic, shards(): low = (product - high.astype(jnp.float32)).astype(jnp.bfloat16)  9.27 us
    dot_general x1, matrix products, shards(): jnp.dot(onehot, jnp.concatenate([high, low], axis=1), preferred_element_t...  8.87 us
    dot_general x1, matrix products, shards(): product = jnp.dot(piece, kernel, preferred_element_type=jnp.float32)  5.59 us
  transfers between devices with their start and end apart: 2, of which 1 were waited for; matrix products, arithmetic and copies ran while one was open for 16% of the time, Pallas kernels for 0%

profile of v3, /device:TPU:1, one launch (start us, length us, event | category | flops | bytes accessed | tf_op | source)
XLA Modules:
  0.0 197.5 jit_solution(15349327057966076856)
XLA Ops:
  6.5 0.9 fusion.11
  7.4 0.7 convert_element_type.34
  8.1 0.8 fusion.273
  8.9 0.8 broadcast_in_dim.11
  9.7 18.5 %all-to-all-start = ((bf16[32,16,384]{2,1,0:T(8,128)(2,1)}), bf16[32,16,384]{2,1,0:T(8,128)(2,1)S(1)}, u32[]{:S(2)}, u32[]{:S(2)}) async-start(bf16[32,16,384]{2,1,0:T(8,128)(2,1)} %broadcast_in_dim.11), calls=%async_computation | async-start | bytes 786432 | tf_op jit(solution)/shard_map/all_to_all | solution.py:42
  28.2 0.8 fusion.272
  49.8 0.8 copy.267
  50.6 1.2 slice.775
  51.8 1.4 bitcast_select_fusion
  53.3 1.6 copy.266
  54.9 1.7 eq.32
  56.6 0.7 fusion.267
  57.3 0.8 iota_add_fusion
  58.1 1.1 add.118
  59.2 5.6 %fusion.269 = f32[512,4096]{1,0:T(8,128)} fusion(bf16[512,384]{1,0:T(8,128)(2,1)S(1)} %bitcast.1038, bf16[384,4096]{0,1:T(8,128)(2,1)S(1)} %bitcast.1037), kind=kOutput, calls=%fused_computation.798 | convolution fusion | flops 1610612736 | bytes 11927552 | tf_op jit(solution)/shard_map/dot_general | solution.py:44
  64.8 9.3 %reshape.208 = f32[8192,256]{1,0:T(8,128)} reshape(f32[512,4096]{1,0:T(8,128)} %fusion.269) | data formatting | bytes 16777216 | tf_op jit(solution)/shard_map/reshape | solution.py:45
  74.0 9.3 %subtract_convert_fusion = (bf16[8192,256]{1,0:T(8,128)(2,1)S(1)}, bf16[8192,256]{1,0:T(8,128)(2,1)}) fusion(f32[8192,256]{1,0:T(8,128)} %reshape.208), kind=kLoop, calls=%fused_computation.7 | loop fusion | flops 8388608 | bytes 16777216 | tf_op jit(solution)/shard_map/convert_element_type | solution.py:62
  83.3 8.9 %fusion = f32[768,512]{1,0:T(8,128)S(1)} fusion(s32[8192]{0:T(1024)S(1)} %copy-done.1, s32[768]{0:T(1024)S(1)} %add.118, bf16[8192,256]{1,0:T(8,128)(2,1)S(1)} %get-tuple-element.5, bf16[8192,256]{1,0:T(8,128)(2,1)} %get-tuple-element.6), kind=kOutput, calls=%fused_computation | convolution fusion | flops 6465519616 | bytes 9997312 | tf_op jit(solution)/shard_map/dot_general | solution.py:63
  92.8 0.9 copy.268
  93.7 0.6 dynamic_slice.3
  96.3 65.3 %reduce-scatter.2.cloned.1.call-done = f32[1,24,2,256]{3,1,2,0:T(8,128)} async-done(((f32[16,24,2,256]{3,1,2,0:T(8,128)}), f32[1,24,2,256]{3,1,2,0:T(8,128)}) %reduce-scatter.2.cloned.1.call-update) | async-done | bytes 49168 | tf_op jit(solution)/shard_map/reduce_scatter | solution.py:67
  161.6 0.8 copy_dynamic-update-slice_fusion
  162.5 27.5 %all_to_all.10 = f32[32,2,256]{2,1,0:T(2,128)S(1)} all-to-all(f32[32,2,256]{2,1,0:T(2,128)S(1)} %copy_dynamic-update-slice_fusion), channel_id=1, replica_groups=mesh['chan'=32,'seg'=16] {'chan'}, dimensions={0} | all-to-all | bytes 131072 | tf_op jit(solution)/shard_map/all_to_all | solution.py:71
  190.0 0.6 reduce_sum.19
  (270 shorter events, 21.4 us)
Async XLA Ops:
  6.5 32.8 %copy-start = (bf16[16,1,384]{2,0,1:T(8,128)(2,1)S(1)}, bf16[16,1,384]{2,0,1:T(8,128)(2,1)}, u32[]{:S(2)}) copy-start(bf16[16,1,384]{2,0,1:T(8,128)(2,1)} %param.4) | copy-start | bytes 36868
  9.7 49.5 %all-to-all-start = ((bf16[32,16,384]{2,1,0:T(8,128)(2,1)}), bf16[32,16,384]{2,1,0:T(8,128)(2,1)S(1)}, u32[]{:S(2)}, u32[]{:S(2)}) async-start(bf16[32,16,384]{2,1,0:T(8,128)(2,1)} %broadcast_in_dim.11), calls=%async_computation | async-start | bytes 786432 | tf_op jit(solution)/shard_map/all_to_all | solution.py:42
  28.2 133.4 %reduce-scatter.2.cloned.1.call-start = ((), (), s32[]{:S(2)}) async-start(), calls=%async_computation.3 | async-start | bytes 835584 | tf_op jit(solution)/shard_map/reduce_scatter | solution.py:67
  74.0 9.3 %copy-start.1 = (s32[8192]{0:T(1024)S(1)}, s32[8192]{0:T(1024)}, u32[]{:S(2)}) copy-start(s32[8192]{0:T(1024)} %eq.32) | copy-start | bytes 98308
Sparse Core Ops, SparseCore 0:
  93.8 67.7 reduce-scatter.1

commit v4 on v3

--- a/solution.py
+++ b/solution.py
@@ -50,7 +50,6 @@
     low_span = 2 * (row_count - 1)
     reach = (low_span + 5 * (chan_count - 1)) * gathers // (2 * low_span + 1) + 2
     depth = -(-(reach - 1) // seg_devices) + 1
-    depth = -(-depth // 8) * 8
     start = gather_id[0, 0]
     lanes = jnp.arange(seg_devices, dtype=jnp.int32)
     first = jnp.minimum((start - lanes + seg_devices - 1) // seg_devices, chan_devices - depth)
@@ -58,13 +57,14 @@
     window = (first[:, None] + jnp.arange(depth, dtype=jnp.int32)[None, :]) * seg_devices + lanes[:, None]
     wanted = (window[:, :, None] * OFFBINS + jnp.arange(OFFBINS, dtype=jnp.int32)).reshape(-1)
     onehot = (wanted[:, None] == labels[None, :]).astype(jnp.bfloat16)
-    high = product.astype(jnp.bfloat16)
-    low = (product - high.astype(jnp.float32)).astype(jnp.bfloat16)
-    both = jnp.dot(onehot, jnp.concatenate([high, low], axis=1), preferred_element_type=jnp.float32)
+    high = lax.reduce_precision(product, exponent_bits=8, mantissa_bits=7)
+    low = product - high
+    split = jnp.concatenate([high, low], axis=1).astype(jnp.bfloat16)
+    both = jnp.dot(onehot, split, preferred_element_type=jnp.float32)
     total = both[:, :LAGS] + both[:, LAGS:]
     scale = 1.0 / math.sqrt(traces.shape[2] * traces.shape[1] * seg_devices)
     stacked = (total * scale).reshape(seg_devices, depth, OFFBINS, LAGS)
-    part = lax.psum_scatter(stacked, "seg", scatter_dimension=0, tiled=True)
+    part = jnp.sum(lax.all_to_all(stacked, "seg", 0, 0, tiled=True), axis=0)
     own_first = first[lax.axis_index("seg")]
     dense = jnp.zeros((chan_devices, OFFBINS, LAGS), jnp.float32)
     dense = lax.dynamic_update_slice(dense, part.reshape(depth, OFFBINS, LAGS), (own_first, 0, 0))

time: 201 us -> 126 us (0.63); the launches traced: 197 us -> 125 us
  waiting for transfers between devices: 65.4 us -> 8.37 us
  between operations: 15.6 us -> 2.2 us
  starting transfers between devices: 18.5 us -> 24 us
  other arithmetic: 16.2 us -> 11.8 us
  matrix products: 14.5 us -> 10.9 us
    reduce_scatter x1 -> x0, waiting for transfers between devices: 65.3 us -> none  [shards(): part = lax.psum_scatter(stacked, 'seg', scatter_dimension=0, tiled=True)]
    convert_element_type x1 -> x0, other arithmetic: 9.27 us -> none  [shards(): low = (product - high.astype(jnp.float32)).astype(jnp.bfloat16)]
    all_to_all x0 -> x1, waiting for transfers between devices: none -> 8.36 us  [shards(): part = jnp.sum(lax.all_to_all(stacked, 'seg', 0, 0, tiled=True), axis=0)]
    all_to_all x0 -> x1, starting transfers between devices: none -> 5.46 us  [shards(): part = jnp.sum(lax.all_to_all(stacked, 'seg', 0, 0, tiled=True), axis=0)]
    another operation x0 -> x1, other arithmetic: none -> 4.68 us
    dot_general x1, matrix products: 8.87 us -> 5.34 us  [shards(): both = jnp.dot(onehot, split, preferred_element_type=jnp.float32)]
  transfers between devices with their start and end apart: 2 -> 2, of which waited for: 1 -> 1; matrix products, arithmetic and copies ran while one was open for 16% -> 25% of each run, Pallas kernels for 0% -> 0%
where the time goes in v4:
time: 126 us; the launch traced here: 125 us
  local copies, waits for them, and re-layouts  38.7 us (31%)
  blocking collectives  28.8 us (23%)
  starting transfers between devices  24 us (19%)
  other arithmetic  11.8 us (9%)
  matrix products  10.9 us (9%)
  waiting for transfers between devices  8.37 us (7%)
  between operations  2.2 us (2%)
    all_to_all x1, blocking collectives, shards(): pieces = lax.all_to_all(dense, 'chan', 0, 0, tiled=True)  28.8 us
    unnamed x258, local copies, waits for them, and re-layouts  20.5 us
    all_to_all x1, starting transfers between devices, shards(): lax.all_to_all(copies, 'chan', 0, 0, tiled=True).reshape(-1, flat.shape[1])  18.5 us
    reshape x1, local copies, waits for them, and re-layouts, shards(): product = product.reshape(row_count * chan_count, LAGS)  9.28 us
    all_to_all x1, waiting for transfers between devices, shards(): part = jnp.sum(lax.all_to_all(stacked, 'seg', 0, 0, tiled=True), axis=0)  8.36 us
    dot_general x1, matrix products, shards(): product = jnp.dot(piece, kernel, preferred_element_type=jnp.float32)  5.6 us
    all_to_all x1, starting transfers between devices, shards(): part = jnp.sum(lax.all_to_all(stacked, 'seg', 0, 0, tiled=True), axis=0)  5.46 us
    dot_general x1, matrix products, shards(): both = jnp.dot(onehot, split, preferred_element_type=jnp.float32)  5.34 us
  transfers between devices with their start and end apart: 2, of which 1 were waited for; matrix products, arithmetic and copies ran while one was open for 25% of the time, Pallas kernels for 0%

profile of v4, /device:TPU:1, one launch (start us, length us, event | category | flops | bytes accessed | tf_op | source)
XLA Modules:
  0.0 124.7 jit_solution(931328922291975222)
XLA Ops:
  0.0 0.9 fusion.12
  0.9 0.7 convert_element_type.26
  1.6 0.8 fusion.274
  2.4 0.8 broadcast_in_dim.11
  3.1 18.5 %all-to-all-start = ((bf16[32,16,384]{2,1,0:T(8,128)(2,1)}), bf16[32,16,384]{2,1,0:T(8,128)(2,1)S(1)}, u32[]{:S(2)}, u32[]{:S(2)}) async-start(bf16[32,16,384]{2,1,0:T(8,128)(2,1)} %broadcast_in_dim.11), calls=%async_computation | async-start | bytes 786432 | tf_op jit(solution)/shard_map/all_to_all | solution.py:42
  21.6 0.8 fusion.273
  43.3 0.8 copy.266
  44.0 1.2 slice.775
  45.2 1.4 %bitcast_select_fusion = s32[512,16]{0,1:T(8,128)} fusion(s32[16,512]{1,0:T(8,128)} %param.7, s32[16,512]{1,0:T(8,128)} %param.6, s32[16]{0:T(128)S(1)} %iota_add_fusion.1), kind=kLoop, calls=%fused_computation.524 | loop fusion | flops 32768 | bytes 98368 | tf_op jit(solution)/shard_map/jit(_where)/select_n | solution.py:48
  46.7 1.6 %copy.265 = s32[512,16]{1,0:T(8,128)} copy(s32[512,16]{0,1:T(8,128)} %bitcast_select_fusion) | data formatting | bytes 65536 | tf_op jit(solution)/shard_map/jit(_where)/select_n | solution.py:48
  48.3 1.7 %eq.32 = s32[8192]{0:T(1024)} reshape(s32[512,16]{1,0:T(8,128)} %copy.265) | data formatting | bytes 65536 | tf_op jit(solution)/shard_map/eq | solution.py:59
  49.9 0.7 fusion.268
  50.7 0.8 iota_add_fusion
  51.5 1.1 add.116
  52.5 5.6 %fusion.270 = f32[512,4096]{1,0:T(8,128)} fusion(bf16[512,384]{1,0:T(8,128)(2,1)S(1)} %bitcast.1037, bf16[384,4096]{0,1:T(8,128)(2,1)S(1)} %bitcast.1036), kind=kOutput, calls=%fused_computation.800 | convolution fusion | flops 1610612736 | bytes 11927552 | tf_op jit(solution)/shard_map/dot_general | solution.py:44
  58.1 9.3 %reshape.205 = f32[8192,256]{1,0:T(8,128)} reshape(f32[512,4096]{1,0:T(8,128)} %fusion.270) | data formatting | bytes 16777216 | tf_op jit(solution)/shard_map/reshape | solution.py:45
  67.4 4.7 %reduce-precision_convert_fusion = (bf16[8192,256]{1,0:T(8,128)(2,1)S(1)}, bf16[8192,256]{1,0:T(8,128)(2,1)S(1)}) fusion(f32[8192,256]{1,0:T(8,128)} %reshape.205), kind=kLoop, calls=%fused_computation.3 | loop fusion | flops 8388608 | bytes 16777216 | tf_op jit(solution)/shard_map/convert
  72.1 5.3 %fusion = f32[608,512]{1,0:T(8,128)S(1)} fusion(s32[8192]{0:T(1024)S(1)} %copy-done.1, s32[608]{0:T(1024)S(1)} %add.116, bf16[8192,256]{1,0:T(8,128)(2,1)S(1)} %get-tuple-element.6, bf16[8192,256]{1,0:T(8,128)(2,1)S(1)} %get-tuple-element.5), kind=kOutput, calls=%fused_computation | convolution fusion | flops 5122031616 | bytes 9668992 | tf_op jit(solution)/shard_map/dot_general | solution.py:63
  77.5 1.2 reshape.206
  78.7 5.5 %all-to-all-start.1 = ((f32[16,19,2,256]{3,2,1,0:T(2,128)}), f32[16,19,2,256]{3,2,1,0:T(2,128)S(1)}, u32[]{:S(2)}, u32[]{:S(2)}) async-start(f32[16,19,2,256]{3,2,1,0:T(2,128)} %reshape.206), calls=%async_computation.1 | async-start | bytes 1245184 | tf_op jit(solution)/shard_map/all_to_all | solution.py:67
  84.2 0.6 dynamic_slice.3
  86.7 8.4 %all-to-all-done.1 = f32[16,19,2,256]{3,2,1,0:T(2,128)S(1)} async-done(((f32[16,19,2,256]{3,2,1,0:T(2,128)}), f32[16,19,2,256]{3,2,1,0:T(2,128)S(1)}, u32[]{:S(2)}, u32[]{:S(2)}) %all-to-all-start.1) | async-done | bytes 622624 | tf_op jit(solution)/shard_map/all_to_all | solution.py:67
  95.3 28.8 %all_to_all.15 = f32[32,2,256]{2,1,0:T(2,128)S(1)} all-to-all(f32[32,2,256]{2,1,0:T(2,128)S(1)} %constant_dynamic-update-slice_fusion.256), channel_id=1, replica_groups=mesh['chan'=32,'seg'=16] {'chan'}, dimensions={0} | all-to-all | bytes 131072 | tf_op jit(solution)/shard_map/all_to_all | solution.py:71
  124.1 0.6 reduce_sum.29
  (269 shorter events, 21.1 us)
Async XLA Ops:
  0.0 32.8 %copy-start = (bf16[16,1,384]{2,0,1:T(8,128)(2,1)S(1)}, bf16[16,1,384]{2,0,1:T(8,128)(2,1)}, u32[]{:S(2)}) copy-start(bf16[16,1,384]{2,0,1:T(8,128)(2,1)} %param.4) | copy-start | bytes 36868
  3.1 49.4 %all-to-all-start = ((bf16[32,16,384]{2,1,0:T(8,128)(2,1)}), bf16[32,16,384]{2,1,0:T(8,128)(2,1)S(1)}, u32[]{:S(2)}, u32[]{:S(2)}) async-start(bf16[32,16,384]{2,1,0:T(8,128)(2,1)} %broadcast_in_dim.11), calls=%async_computation | async-start | bytes 786432 | tf_op jit(solution)/shard_map/all_to_all | solution.py:42
  67.4 4.7 %copy-start.1 = (s32[8192]{0:T(1024)S(1)}, s32[8192]{0:T(1024)}, u32[]{:S(2)}) copy-start(s32[8192]{0:T(1024)} %eq.32) | copy-start | bytes 98308
  78.7 16.4 %all-to-all-start.1 = ((f32[16,19,2,256]{3,2,1,0:T(2,128)}), f32[16,19,2,256]{3,2,1,0:T(2,128)S(1)}, u32[]{:S(2)}, u32[]{:S(2)}) async-start(f32[16,19,2,256]{3,2,1,0:T(2,128)} %reshape.206), calls=%async_computation.1 | async-start | bytes 1245184 | tf_op jit(solution)/shard_map/all_to_all | solution.py:67

commit v5 on v4

--- a/solution.py
+++ b/solution.py
@@ -19,13 +19,16 @@
     return (window * values * lax.rsqrt(power + 1e-06)).astype(jnp.bfloat16)
 
 
-def hankel(normed, lag_count):
+def toeplitz(normed, lag_count):
     chan_count, seg_count, sample_count = normed.shape
-    turned = jnp.transpose(normed, (1, 2, 0))
-    padded = jnp.pad(turned, ((0, 0), (lag_count // 2, lag_count // 2), (0, 0)))
-    slices = [padded[:, lag_count - k : lag_count - k + sample_count, :] for k in range(lag_count)]
-    picked = jnp.stack(slices, axis=3)
-    return picked.reshape(seg_count * sample_count, chan_count * lag_count)
+    flat = normed.reshape(chan_count, sample_count)
+    half = lag_count // 2
+    width = sample_count + lag_count
+    ring = jnp.concatenate(
+        [flat[:, half:], jnp.zeros((chan_count, width - sample_count), flat.dtype), flat[:, :half]], axis=1
+    )
+    tiled = jnp.tile(ring, (1, lag_count + 1))[:, : lag_count * (width - 1)]
+    return tiled.reshape(chan_count, lag_count, width - 1)[:, :, :sample_count]
 
 
 def shards(traces, taper_len, gather_id, offset_bin):
@@ -34,14 +37,14 @@
     seg_devices = lax.axis_size("seg")
     bucket_count = chan_devices * seg_devices * OFFBINS
     normed = normalize(traces, taper_len)
-    kernel = hankel(normed, LAGS)
+    kernel = toeplitz(normed, LAGS)
     first_row = lax.axis_index("chan") * chan_count
     own_rows = first_row + jnp.arange(chan_count, dtype=jnp.int32)[None, :]
     flat = lax.optimization_barrier(normed.reshape(chan_count, -1))
     copies = jnp.broadcast_to(flat[None], (chan_devices,) + flat.shape)
     piece = lax.all_to_all(copies, "chan", 0, 0, tiled=True).reshape(-1, flat.shape[1])
     row_count = piece.shape[0]
-    product = jnp.dot(piece, kernel, preferred_element_type=jnp.float32)
+    product = jnp.einsum("it,jkt->ijk", piece, kernel, preferred_element_type=jnp.float32)
     product = product.reshape(row_count * chan_count, LAGS)
     labels = jnp.transpose(gather_id * OFFBINS + offset_bin)
     partner = jnp.arange(row_count, dtype=jnp.int32)[:, None]

time: 126 us -> 113 us (0.90)
  local copies, waits for them, and re-layouts: 38.7 us -> 29.3 us
  blocking collectives: 28.8 us -> 24.2 us
  other arithmetic: 11.8 us -> 8.09 us
  waiting for transfers between devices: 8.37 us -> 11.1 us
  starting transfers between devices: 24 us -> 25.7 us
    unnamed x258 -> x5, local copies, waits for them, and re-layouts: 20.5 us -> 0.68 us
    reshape x1, local copies, waits for them, and re-layouts: 9.28 us -> 16.7 us  [toeplitz(): return tiled.reshape(chan_count, lag_count, width - 1)[:, :, :sample_count]]
    dot_general x0 -> x1, local copies, waits for them, and re-layouts: none -> 4.86 us  [shards(): jnp.einsum('it,jkt->ijk', piece, kernel, preferred_element_type=jnp.float32)]
    all_to_all x1, blocking collectives: 28.8 us -> 24.2 us  [shards(): pieces = lax.all_to_all(dense, 'chan', 0, 0, tiled=True)]
    all_to_all x1, waiting for transfers between devices: 0.01 us -> 2.78 us  [shards(): lax.all_to_all(copies, 'chan', 0, 0, tiled=True).reshape(-1, flat.shape[1])]
    slice x0 -> x3, local copies, waits for them, and re-layouts: none -> 2.51 us  [the longest x1 2.51 us: toeplitz(): tiled = jnp.tile(ring, (1, lag_count + 1))[:, :lag_count * (width - 1)]]
    dot_general x1, matrix products: 5.34 us -> 7.52 us  [shards(): both = jnp.dot(onehot, split, preferred_element_type=jnp.float32)]
    all_to_all x1, starting transfers between devices: 5.46 us -> 7.25 us  [shards(): part = jnp.sum(lax.all_to_all(stacked, 'seg', 0, 0, tiled=True), axis=0)]
  transfers between devices with their start and end apart: 2 -> 2, of which waited for: 1 -> 2; matrix products, arithmetic and copies ran while one was open for 25% -> 21% of each run, Pallas kernels for 0% -> 0%
where the time goes in v5:
time: 113 us; the launch traced here: 112 us
  local copies, waits for them, and re-layouts  29.3 us (26%)
  starting transfers between devices  25.7 us (23%)
  blocking collectives  24.2 us (21%)
  matrix products  11.8 us (10%)
  waiting for transfers between devices  11.1 us (10%)
  other arithmetic  8.09 us (7%)
  between operations  2.08 us (2%)
    all_to_all x1, blocking collectives, shards(): pieces = lax.all_to_all(dense, 'chan', 0, 0, tiled=True)  24.2 us
    all_to_all x1, starting transfers between devices, shards(): lax.all_to_all(copies, 'chan', 0, 0, tiled=True).reshape(-1, flat.shape[1])  18.5 us
    reshape x1, local copies, waits for them, and re-layouts, toeplitz(): return tiled.reshape(chan_count, lag_count, width - 1)[:, :, :sample_count]  16.7 us
    all_to_all x1, waiting for transfers between devices, shards(): part = jnp.sum(lax.all_to_all(stacked, 'seg', 0, 0, tiled=True), axis=0)  8.36 us
    dot_general x1, matrix products, shards(): both = jnp.dot(onehot, split, preferred_element_type=jnp.float32)  7.52 us
    all_to_all x1, starting transfers between devices, shards(): part = jnp.sum(lax.all_to_all(stacked, 'seg', 0, 0, tiled=True), axis=0)  7.25 us
    dot_general x1, local copies, waits for them, and re-layouts, shards(): jnp.einsum('it,jkt->ijk', piece, kernel, preferred_element_type=jnp.float32)  4.86 us
    dot_general x1, matrix products, shards(): jnp.einsum('it,jkt->ijk', piece, kernel, preferred_element_type=jnp.float32)  4.26 us
  transfers between devices with their start and end apart: 2, of which 2 were waited for; matrix products, arithmetic and copies ran while one was open for 21% of the time, Pallas kernels for 0%

profile of v5, /device:TPU:1, one launch (start us, length us, event | category | flops | bytes accessed | tf_op | source)
XLA Modules:
  0.0 112.4 jit_solution(12064974154029534242)
XLA Ops:
  0.0 0.8 fusion.14
  0.8 0.7 convert_element_type.24
  1.5 0.8 fusion.15
  2.3 0.8 broadcast_in_dim.14
  3.1 18.5 %all-to-all-start = ((bf16[32,16,384]{2,1,0:T(8,128)(2,1)}), bf16[32,16,384]{2,1,0:T(8,128)(2,1)S(1)}, u32[]{:S(2)}, u32[]{:S(2)}) async-start(bf16[32,16,384]{2,1,0:T(8,128)(2,1)} %broadcast_in_dim.14), calls=%async_computation | async-start | bytes 786432 | tf_op jit(solution)/shard_map/all_to_all | solution.py:45
  21.6 1.2 %slice.21 = s32[1,1]{1,0:T(1,128)} slice(s32[16,512]{1,0:T(8,128)} %param.6), slice={[0:1], [0:1]} | slice | bytes 8 | tf_op jit(solution)/shard_map/slice | solution.py:56
  22.8 0.4 tile.4
  23.2 0.7 copy.13
  23.9 2.5 %slice.30 = bf16[16,163584]{1,0:T(8,128)(2,1)} slice(bf16[16,164480]{1,0:T(8,128)(2,1)S(1)} %bitcast.17), slice={[0:16], [0:163584]} | slice | bytes 10469376 | tf_op jit(solution)/shard_map/slice | solution.py:30
  26.4 16.7 %reshape.209 = bf16[16,256,639]{2,1,0:T(8,128)(2,1)} reshape(bf16[16,163584]{1,0:T(8,128)(2,1)} %slice.30) | data formatting | bytes 10469376 | tf_op jit(solution)/shard_map/reshape | solution.py:31
  43.3 0.1 eq.32
  43.5 0.7 fusion.16
  44.5 2.8 %all-to-all-done = bf16[32,16,384]{2,1,0:T(8,128)(2,1)S(1)} async-done(((bf16[32,16,384]{2,1,0:T(8,128)(2,1)}), bf16[32,16,384]{2,1,0:T(8,128)(2,1)S(1)}, u32[]{:S(2)}, u32[]{:S(2)}) %all-to-all-start) | async-done | bytes 393248 | tf_op jit(solution)/shard_map/all_to_all | solution.py:45
  47.2 4.3 %fusion.8 = f32[512,16,256]{2,0,1:T(8,128)S(1)} fusion(bf16[512,384,1]{1,0,2:T(8,128)(2,1)S(1)} %bitcast.18, bf16[16,256,639]{2,1,0:T(8,128)(2,1)} %reshape.209), kind=kOutput, calls=%fused_computation.10 | convolution fusion | flops 1610612736 | bytes 11927552 | tf_op jit(solution)/shard_map/it,jkt->ijk/dot_general | solution.py:47
  51.5 4.9 %copy.10 = f32[512,16,256]{2,1,0:T(8,128)S(1)} copy(f32[512,16,256]{2,0,1:T(8,128)S(1)} %fusion.8) | data formatting | bytes 16777216 | tf_op jit(solution)/shard_map/it,jkt->ijk/dot_general | solution.py:47
  56.4 4.0 %reduce-precision_convert_fusion = (bf16[8192,256]{1,0:T(8,128)(2,1)S(1)}, bf16[8192,256]{1,0:T(8,128)(2,1)}) fusion(f32[512,16,256]{2,1,0:T(8,128)S(1)} %copy.10), kind=kLoop, calls=%fused_computation.3 | loop fusion | flops 8388608 | bytes 16777216 | tf_op jit(solution)/shard_map/convert
  60.3 7.5 %fusion = f32[608,512]{1,0:T(8,128)S(1)} fusion(s32[8192]{0:T(1024)S(1)} %eq.32, s32[608]{0:T(1024)S(1)} %add.114, bf16[8192,256]{1,0:T(8,128)(2,1)} %get-tuple-element.6, bf16[8192,256]{1,0:T(8,128)(2,1)S(1)} %get-tuple-element.5), kind=kOutput, calls=%fused_computation | convolution fusion | flops 5122031616 | bytes 9668992 | tf_op jit(solution)/shard_map/dot_general | solution.py:66
  68.0 1.2 %reshape.211 = f32[16,19,2,256]{3,2,1,0:T(2,128)} reshape(f32[608,256]{1,0:T(8,128)S(1)} %fusion.10) | data formatting | bytes 1245184 | tf_op jit(solution)/shard_map/reshape | solution.py:69
  69.1 7.2 %all-to-all-start.1 = ((f32[16,19,2,256]{3,2,1,0:T(2,128)}), f32[16,19,2,256]{3,2,1,0:T(2,128)S(1)}, u32[]{:S(2)}, u32[]{:S(2)}) async-start(f32[16,19,2,256]{3,2,1,0:T(2,128)} %reshape.211), calls=%async_computation.1 | async-start | bytes 1245184 | tf_op jit(solution)/shard_map/all_to_all | solution.py:70
  76.4 0.6 dynamic_slice.3
  78.9 8.4 %all-to-all-done.1 = f32[16,19,2,256]{3,2,1,0:T(2,128)S(1)} async-done(((f32[16,19,2,256]{3,2,1,0:T(2,128)}), f32[16,19,2,256]{3,2,1,0:T(2,128)S(1)}, u32[]{:S(2)}, u32[]{:S(2)}) %all-to-all-start.1) | async-done | bytes 622624 | tf_op jit(solution)/shard_map/all_to_all | solution.py:70
  87.3 0.2 reduce_sum.28
  87.5 24.2 %all_to_all.15 = f32[32,2,256]{2,1,0:T(2,128)S(1)} all-to-all(f32[32,2,256]{2,1,0:T(2,128)S(1)} %constant_dynamic-update-slice_fusion), channel_id=1, replica_groups=mesh['chan'=32,'seg'=16] {'chan'}, dimensions={0} | all-to-all | bytes 131072 | tf_op jit(solution)/shard_map/all_to_all | solution.py:74
  111.7 0.6 reduce_sum.29
  (20 shorter events, 0.7 us)
Async XLA Ops:
  3.1 44.2 %all-to-all-start = ((bf16[32,16,384]{2,1,0:T(8,128)(2,1)}), bf16[32,16,384]{2,1,0:T(8,128)(2,1)S(1)}, u32[]{:S(2)}, u32[]{:S(2)}) async-start(bf16[32,16,384]{2,1,0:T(8,128)(2,1)} %broadcast_in_dim.14), calls=%async_computation | async-start | bytes 786432 | tf_op jit(solution)/shard_map/all_to_all | solution.py:45
  26.4 16.7 %copy-start = (s32[16,512]{1,0:T(8,128)S(1)}, s32[16,512]{1,0:T(8,128)}, u32[]{:S(2)}) copy-start(s32[16,512]{1,0:T(8,128)} %param.7) | copy-start | bytes 98308
  26.4 16.7 %copy-start.1 = (s32[16,512]{1,0:T(8,128)S(1)}, s32[16,512]{1,0:T(8,128)}, u32[]{:S(2)}) copy-start(s32[16,512]{1,0:T(8,128)} %param.6) | copy-start | bytes 98308
  69.1 18.1 %all-to-all-start.1 = ((f32[16,19,2,256]{3,2,1,0:T(2,128)}), f32[16,19,2,256]{3,2,1,0:T(2,128)S(1)}, u32[]{:S(2)}, u32[]{:S(2)}) async-start(f32[16,19,2,256]{3,2,1,0:T(2,128)} %reshape.211), calls=%async_computation.1 | async-start | bytes 1245184 | tf_op jit(solution)/shard_map/all_to_all | solution.py:70

commit v6 on v5

--- a/solution.py
+++ b/solution.py
@@ -23,7 +23,7 @@
     chan_count, seg_count, sample_count = normed.shape
     flat = normed.reshape(chan_count, sample_count)
     half = lag_count // 2
-    width = sample_count + lag_count
+    width = sample_count + lag_count + 1
     ring = jnp.concatenate(
         [flat[:, half:], jnp.zeros((chan_count, width - sample_count), flat.dtype), flat[:, :half]], axis=1
     )

time: 113 us -> 110 us (0.973)
  local copies, waits for them, and re-layouts: 29.3 us -> 26.5 us
  waiting for transfers between devices: 11.1 us -> 13.9 us
  blocking collectives: 24.2 us -> 21.5 us
    reshape x1 -> x0, local copies, waits for them, and re-layouts: 16.7 us -> none  [toeplitz(): return tiled.reshape(chan_count, lag_count, width - 1)[:, :, :sample_count]]
    another operation x1 -> x2, local copies, waits for them, and re-layouts: 0.42 us -> 11.9 us  [toeplitz(): tiled = jnp.tile(ring, (1, lag_count + 1))[:, :lag_count * (width - 1)]]
    all_to_all x1, blocking collectives: 24.2 us -> 21.5 us  [shards(): pieces = lax.all_to_all(dense, 'chan', 0, 0, tiled=True)]
    all_to_all x1, waiting for transfers between devices: 2.78 us -> 5.49 us  [shards(): lax.all_to_all(copies, 'chan', 0, 0, tiled=True).reshape(-1, flat.shape[1])]
    unnamed x5, local copies, waits for them, and re-layouts: 0.68 us -> 3.17 us
    slice x1 -> x2, local copies, waits for them, and re-layouts: 2.51 us -> 2.49 us  [toeplitz(): tiled = jnp.tile(ring, (1, lag_count + 1))[:, :lag_count * (width - 1)]]
  transfers between devices with their start and end apart: 2 -> 2, of which waited for: 2 -> 2; matrix products, arithmetic and copies ran while one was open for 21% -> 17% of each run, Pallas kernels for 0% -> 0%
where the time goes in v6:
time: 110 us
  local copies, waits for them, and re-layouts  26.5 us (24%)
  starting transfers between devices  25.7 us (23%)
  blocking collectives  21.5 us (20%)
  waiting for transfers between devices  13.9 us (13%)
  matrix products  11.8 us (11%)
  other arithmetic  8.13 us (7%)
  between operations  2.07 us (2%)
    all_to_all x1, blocking collectives, shards(): pieces = lax.all_to_all(dense, 'chan', 0, 0, tiled=True)  21.5 us
    all_to_all x1, starting transfers between devices, shards(): lax.all_to_all(copies, 'chan', 0, 0, tiled=True).reshape(-1, flat.shape[1])  18.5 us
    another operation x2, local copies, waits for them, and re-layouts, toeplitz(): tiled = jnp.tile(ring, (1, lag_count + 1))[:, :lag_count * (width - 1)]  11.9 us
    all_to_all x1, waiting for transfers between devices, shards(): part = jnp.sum(lax.all_to_all(stacked, 'seg', 0, 0, tiled=True), axis=0)  8.36 us
    dot_general x1, matrix products, shards(): both = jnp.dot(onehot, split, preferred_element_type=jnp.float32)  7.52 us
    all_to_all x1, starting transfers between devices, shards(): part = jnp.sum(lax.all_to_all(stacked, 'seg', 0, 0, tiled=True), axis=0)  7.25 us
    all_to_all x1, waiting for transfers between devices, shards(): lax.all_to_all(copies, 'chan', 0, 0, tiled=True).reshape(-1, flat.shape[1])  5.49 us
    dot_general x1, local copies, waits for them, and re-layouts, shards(): jnp.einsum('it,jkt->ijk', piece, kernel, preferred_element_type=jnp.float32)  4.86 us
  transfers between devices with their start and end apart: 2, of which 2 were waited for; matrix products, arithmetic and copies ran while one was open for 17% of the time, Pallas kernels for 0%

profile of v6, /device:TPU:1, one launch (start us, length us, event | category | flops | bytes accessed | tf_op | source)
XLA Modules:
  0.0 109.6 jit_solution(1684752710054265199)
XLA Ops:
  0.0 0.8 fusion.14
  0.8 0.7 convert_element_type.24
  1.5 0.8 fusion.15
  2.3 0.8 broadcast_in_dim.14
  3.1 18.5 %all-to-all-start = ((bf16[32,16,384]{2,1,0:T(8,128)(2,1)}), bf16[32,16,384]{2,1,0:T(8,128)(2,1)S(1)}, u32[]{:S(2)}, u32[]{:S(2)}) async-start(bf16[32,16,384]{2,1,0:T(8,128)(2,1)} %broadcast_in_dim.14), calls=%async_computation | async-start | bytes 786432 | tf_op jit(solution)/shard_map/all_to_all | solution.py:45
  21.6 1.2 %slice.21 = s32[1,1]{1,0:T(1,128)} slice(s32[16,512]{1,0:T(8,128)} %param.6), slice={[0:1], [0:1]} | slice | bytes 8 | tf_op jit(solution)/shard_map/slice | solution.py:56
  22.9 3.1 %tile.4 = bf16[16,257,641]{2,1,0:T(8,128)(2,1)} broadcast(bf16[16,641]{1,0:T(8,128)(2,1)S(1)} %pad_maximum_fusion), dimensions={0,2} | broadcast | bytes 5292096 | tf_op jit(solution)/shard_map/tile | solution.py:30
  26.0 8.7 %tile.10 = bf16[16,164737]{1,0:T(8,128)(2,1)} reshape(bf16[16,257,641]{2,1,0:T(8,128)(2,1)} %tile.4) | data formatting | bytes 10543168 | tf_op jit(solution)/shard_map/tile | solution.py:30
  34.7 2.5 %slice-done = bf16[16,163840]{1,0:T(8,128)(2,1)S(1)} async-done(((bf16[16,164737]{1,0:T(8,128)(2,1)}), bf16[16,163840]{1,0:T(8,128)(2,1)S(1)}, s32[]{:S(2)}) %slice-start) | async-done | bytes 5242904 | tf_op jit(solution)/shard_map/slice | solution.py:30
  37.2 3.2 %copy.13 = bf16[2,8,256,640]{3,2,1,0:T(8,128)(2,1)} copy(bf16[2,8,256,640]{3,1,2,0:T(8,128)(2,1)S(1)} %bitcast.17) | data formatting | bytes 10485760
  40.6 0.1 eq.32
  40.8 0.7 fusion.16
  41.8 5.5 %all-to-all-done = bf16[32,16,384]{2,1,0:T(8,128)(2,1)S(1)} async-done(((bf16[32,16,384]{2,1,0:T(8,128)(2,1)}), bf16[32,16,384]{2,1,0:T(8,128)(2,1)S(1)}, u32[]{:S(2)}, u32[]{:S(2)}) %all-to-all-start) | async-done | bytes 393248 | tf_op jit(solution)/shard_map/all_to_all | solution.py:45
  47.2 4.3 %fusion.8 = f32[512,16,256]{2,0,1:T(8,128)S(1)} fusion(bf16[512,384,1]{1,0,2:T(8,128)(2,1)S(1)} %bitcast.18, bf16[16,256,640]{2,1,0:T(8,128)(2,1)} %bitcast.16), kind=kOutput, calls=%fused_computation.10 | convolution fusion | flops 1610612736 | bytes 11927552 | tf_op jit(solution)/shard_map/it,jkt->ijk/dot_general | solution.py:47
  51.5 4.9 %copy.10 = f32[512,16,256]{2,1,0:T(8,128)S(1)} copy(f32[512,16,256]{2,0,1:T(8,128)S(1)} %fusion.8) | data formatting | bytes 16777216 | tf_op jit(solution)/shard_map/it,jkt->ijk/dot_general | solution.py:47
  56.4 4.0 %reduce-precision_convert_fusion = (bf16[8192,256]{1,0:T(8,128)(2,1)S(1)}, bf16[8192,256]{1,0:T(8,128)(2,1)}) fusion(f32[512,16,256]{2,1,0:T(8,128)S(1)} %copy.10), kind=kLoop, calls=%fused_computation.3 | loop fusion | flops 8388608 | bytes 16777216 | tf_op jit(solution)/shard_map/convert
  60.3 7.5 %fusion = f32[608,512]{1,0:T(8,128)S(1)} fusion(s32[8192]{0:T(1024)S(1)} %eq.32, s32[608]{0:T(1024)S(1)} %add.114, bf16[8192,256]{1,0:T(8,128)(2,1)} %get-tuple-element.6, bf16[8192,256]{1,0:T(8,128)(2,1)S(1)} %get-tuple-element.5), kind=kOutput, calls=%fused_computation | convolution fusion | flops 5122031616 | bytes 9668992 | tf_op jit(solution)/shard_map/dot_general | solution.py:66
  67.9 1.2 %reshape.211 = f32[16,19,2,256]{3,2,1,0:T(2,128)} reshape(f32[608,256]{1,0:T(8,128)S(1)} %fusion.10) | data formatting | bytes 1245184 | tf_op jit(solution)/shard_map/reshape | solution.py:69
  69.1 7.3 %all-to-all-start.1 = ((f32[16,19,2,256]{3,2,1,0:T(2,128)}), f32[16,19,2,256]{3,2,1,0:T(2,128)S(1)}, u32[]{:S(2)}, u32[]{:S(2)}) async-start(f32[16,19,2,256]{3,2,1,0:T(2,128)} %reshape.211), calls=%async_computation.1 | async-start | bytes 1245184 | tf_op jit(solution)/shard_map/all_to_all | solution.py:70
  76.4 0.6 dynamic_slice.3
  78.9 8.4 %all-to-all-done.1 = f32[16,19,2,256]{3,2,1,0:T(2,128)S(1)} async-done(((f32[16,19,2,256]{3,2,1,0:T(2,128)}), f32[16,19,2,256]{3,2,1,0:T(2,128)S(1)}, u32[]{:S(2)}, u32[]{:S(2)}) %all-to-all-start.1) | async-done | bytes 622624 | tf_op jit(solution)/shard_map/all_to_all | solution.py:70
  87.3 0.2 reduce_sum.28
  87.5 21.5 %all_to_all.15 = f32[32,2,256]{2,1,0:T(2,128)S(1)} all-to-all(f32[32,2,256]{2,1,0:T(2,128)S(1)} %constant_dynamic-update-slice_fusion), channel_id=1, replica_groups=mesh['chan'=32,'seg'=16] {'chan'}, dimensions={0} | all-to-all | bytes 131072 | tf_op jit(solution)/shard_map/all_to_all | solution.py:74
  109.0 0.6 reduce_sum.29
  (21 shorter events, 0.8 us)
Async XLA Ops:
  3.1 44.2 %all-to-all-start = ((bf16[32,16,384]{2,1,0:T(8,128)(2,1)}), bf16[32,16,384]{2,1,0:T(8,128)(2,1)S(1)}, u32[]{:S(2)}, u32[]{:S(2)}) async-start(bf16[32,16,384]{2,1,0:T(8,128)(2,1)} %broadcast_in_dim.14), calls=%async_computation | async-start | bytes 786432 | tf_op jit(solution)/shard_map/all_to_all | solution.py:45
  34.7 2.5 %slice-start = ((bf16[16,164737]{1,0:T(8,128)(2,1)}), bf16[16,163840]{1,0:T(8,128)(2,1)S(1)}, s32[]{:S(2)}) async-start(bf16[16,164737]{1,0:T(8,128)(2,1)} %tile.10), calls=%async_computation.3 | async-start | bytes 10485760 | tf_op jit(solution)/shard_map/slice | solution.py:30
  37.2 3.2 %copy-start = (s32[16,512]{1,0:T(8,128)S(1)}, s32[16,512]{1,0:T(8,128)}, u32[]{:S(2)}) copy-start(s32[16,512]{1,0:T(8,128)} %param.7) | copy-start | bytes 98308
  37.2 3.2 %copy-start.1 = (s32[16,512]{1,0:T(8,128)S(1)}, s32[16,512]{1,0:T(8,128)}, u32[]{:S(2)}) copy-start(s32[16,512]{1,0:T(8,128)} %param.6) | copy-start | bytes 98308
  69.1 18.1 %all-to-all-start.1 = ((f32[16,19,2,256]{3,2,1,0:T(2,128)}), f32[16,19,2,256]{3,2,1,0:T(2,128)S(1)}, u32[]{:S(2)}, u32[]{:S(2)}) async-start(f32[16,19,2,256]{3,2,1,0:T(2,128)} %reshape.211), calls=%async_computation.1 | async-start | bytes 1245184 | tf_op jit(solution)/shard_map/all_to_all | solution.py:70

commit v7 on v6

--- a/solution.py
+++ b/solution.py
@@ -45,10 +45,10 @@
     piece = lax.all_to_all(copies, "chan", 0, 0, tiled=True).reshape(-1, flat.shape[1])
     row_count = piece.shape[0]
     product = jnp.einsum("it,jkt->ijk", piece, kernel, preferred_element_type=jnp.float32)
-    product = product.reshape(row_count * chan_count, LAGS)
-    labels = jnp.transpose(gather_id * OFFBINS + offset_bin)
-    partner = jnp.arange(row_count, dtype=jnp.int32)[:, None]
-    labels = jnp.where(partner == own_rows, -1, labels).reshape(-1)
+    product = jnp.transpose(product, (1, 0, 2)).reshape(row_count * chan_count, LAGS)
+    labels = gather_id * OFFBINS + offset_bin
+    partner = jnp.arange(row_count, dtype=jnp.int32)[None, :]
+    labels = jnp.where(partner == own_rows.reshape(-1, 1), -1, labels).reshape(-1)
     gathers = chan_devices * seg_devices
     low_span = 2 * (row_count - 1)
     reach = (low_span + 5 * (chan_count - 1)) * gathers // (2 * low_span + 1) + 2

time: 110 us -> 105 us (0.955)
  local copies, waits for them, and re-layouts: 26.5 us -> 21.4 us
    dot_general x1 -> x0, local copies, waits for them, and re-layouts: 4.86 us -> none  [shards(): jnp.einsum('it,jkt->ijk', piece, kernel, preferred_element_type=jnp.float32)]
    unnamed x5 -> x6, local copies, waits for them, and re-layouts: 3.17 us -> 3.18 us
where the time goes in v7:
time: 105 us
  starting transfers between devices  25.7 us (24%)
  local copies, waits for them, and re-layouts  21.4 us (20%)
  blocking collectives  21.3 us (20%)
  waiting for transfers between devices  14.1 us (13%)
  matrix products  11.8 us (11%)
  other arithmetic  8.13 us (8%)
  between operations  2.07 us (2%)
    all_to_all x1, blocking collectives, shards(): pieces = lax.all_to_all(dense, 'chan', 0, 0, tiled=True)  21.3 us
    all_to_all x1, starting transfers between devices, shards(): lax.all_to_all(copies, 'chan', 0, 0, tiled=True).reshape(-1, flat.shape[1])  18.5 us
    another operation x2, local copies, waits for them, and re-layouts, toeplitz(): tiled = jnp.tile(ring, (1, lag_count + 1))[:, :lag_count * (width - 1)]  11.9 us
    all_to_all x1, waiting for transfers between devices, shards(): part = jnp.sum(lax.all_to_all(stacked, 'seg', 0, 0, tiled=True), axis=0)  8.36 us
    dot_general x1, matrix products, shards(): both = jnp.dot(onehot, split, preferred_element_type=jnp.float32)  7.52 us
    all_to_all x1, starting transfers between devices, shards(): part = jnp.sum(lax.all_to_all(stacked, 'seg', 0, 0, tiled=True), axis=0)  7.25 us
    all_to_all x1, waiting for transfers between devices, shards(): lax.all_to_all(copies, 'chan', 0, 0, tiled=True).reshape(-1, flat.shape[1])  5.73 us
    dot_general x1, matrix products, shards(): jnp.einsum('it,jkt->ijk', piece, kernel, preferred_element_type=jnp.float32)  4.26 us
  transfers between devices with their start and end apart: 2, of which 2 were waited for; matrix products, arithmetic and copies ran while one was open for 17% of the time, Pallas kernels for 0%

profile of v7, /device:TPU:1, one launch (start us, length us, event | category | flops | bytes accessed | tf_op | source)
XLA Modules:
  0.0 104.5 jit_solution(4318458437201066351)
XLA Ops:
  0.0 0.8 fusion.14
  0.8 0.7 convert_element_type.24
  1.5 0.8 fusion.15
  2.3 0.8 broadcast_in_dim.14
  3.1 18.5 %all-to-all-start = ((bf16[32,16,384]{2,1,0:T(8,128)(2,1)}), bf16[32,16,384]{2,1,0:T(8,128)(2,1)S(1)}, u32[]{:S(2)}, u32[]{:S(2)}) async-start(bf16[32,16,384]{2,1,0:T(8,128)(2,1)} %broadcast_in_dim.14), calls=%async_computation | async-start | bytes 786432 | tf_op jit(solution)/shard_map/all_to_all | solution.py:45
  21.6 1.2 %slice.21 = s32[1,1]{1,0:T(1,128)} slice(s32[16,512]{1,0:T(8,128)} %param.6), slice={[0:1], [0:1]} | slice | bytes 8 | tf_op jit(solution)/shard_map/slice | solution.py:56
  22.9 3.1 %tile.4 = bf16[16,257,641]{2,1,0:T(8,128)(2,1)} broadcast(bf16[16,641]{1,0:T(8,128)(2,1)S(1)} %pad_maximum_fusion), dimensions={0,2} | broadcast | bytes 5292096 | tf_op jit(solution)/shard_map/tile | solution.py:30
  26.0 8.7 %tile.10 = bf16[16,164737]{1,0:T(8,128)(2,1)} reshape(bf16[16,257,641]{2,1,0:T(8,128)(2,1)} %tile.4) | data formatting | bytes 10543168 | tf_op jit(solution)/shard_map/tile | solution.py:30
  34.7 2.5 %slice-done = bf16[16,163840]{1,0:T(8,128)(2,1)S(1)} async-done(((bf16[16,164737]{1,0:T(8,128)(2,1)}), bf16[16,163840]{1,0:T(8,128)(2,1)S(1)}, s32[]{:S(2)}) %slice-start) | async-done | bytes 5242904 | tf_op jit(solution)/shard_map/slice | solution.py:30
  37.2 3.2 %copy.8 = bf16[2,8,256,640]{3,2,1,0:T(8,128)(2,1)} copy(bf16[2,8,256,640]{3,1,2,0:T(8,128)(2,1)S(1)} %bitcast.20) | data formatting | bytes 10485760
  40.4 0.7 fusion.16
  41.1 0.1 iota_add_fusion
  41.3 0.1 add.115
  41.5 5.7 %all-to-all-done = bf16[32,16,384]{2,1,0:T(8,128)(2,1)S(1)} async-done(((bf16[32,16,384]{2,1,0:T(8,128)(2,1)}), bf16[32,16,384]{2,1,0:T(8,128)(2,1)S(1)}, u32[]{:S(2)}, u32[]{:S(2)}) %all-to-all-start) | async-done | bytes 393248 | tf_op jit(solution)/shard_map/all_to_all | solution.py:45
  47.2 4.3 %fusion.8 = f32[512,16,256]{2,0,1:T(8,128)S(1)} fusion(bf16[512,384,1]{1,0,2:T(8,128)(2,1)S(1)} %bitcast.21, bf16[16,256,640]{2,1,0:T(8,128)(2,1)} %bitcast.19), kind=kOutput, calls=%fused_computation.10 | convolution fusion | flops 1610612736 | bytes 11927552 | tf_op jit(solution)/shard_map/it,jkt->ijk/dot_general | solution.py:47
  51.5 4.0 %reduce-precision_convert_fusion = (bf16[8192,256]{1,0:T(8,128)(2,1)S(1)}, bf16[8192,256]{1,0:T(8,128)(2,1)}) fusion(f32[512,16,256]{2,0,1:T(8,128)S(1)} %fusion.8), kind=kLoop, calls=%fused_computation.3 | loop fusion | flops 8388608 | bytes 16777216 | tf_op jit(solution)/shard_map/convert
  55.5 7.5 %fusion = f32[608,512]{1,0:T(8,128)S(1)} fusion(s32[8192]{0:T(1024)S(1)} %bitcast.22, s32[608]{0:T(1024)S(1)} %add.115, bf16[8192,256]{1,0:T(8,128)(2,1)} %get-tuple-element.6, bf16[8192,256]{1,0:T(8,128)(2,1)S(1)} %get-tuple-element.5), kind=kOutput, calls=%fused_computation | convolution fusion | flops 5122031616 | bytes 9668992 | tf_op jit(solution)/shard_map/dot_general | solution.py:66
  63.1 1.2 %reshape.213 = f32[16,19,2,256]{3,2,1,0:T(2,128)} reshape(f32[608,256]{1,0:T(8,128)S(1)} %fusion.10) | data formatting | bytes 1245184 | tf_op jit(solution)/shard_map/reshape | solution.py:69
  64.3 7.2 %all-to-all-start.1 = ((f32[16,19,2,256]{3,2,1,0:T(2,128)}), f32[16,19,2,256]{3,2,1,0:T(2,128)S(1)}, u32[]{:S(2)}, u32[]{:S(2)}) async-start(f32[16,19,2,256]{3,2,1,0:T(2,128)} %reshape.213), calls=%async_computation.1 | async-start | bytes 1245184 | tf_op jit(solution)/shard_map/all_to_all | solution.py:70
  71.5 0.6 dynamic_slice.3
  74.0 8.4 %all-to-all-done.1 = f32[16,19,2,256]{3,2,1,0:T(2,128)S(1)} async-done(((f32[16,19,2,256]{3,2,1,0:T(2,128)}), f32[16,19,2,256]{3,2,1,0:T(2,128)S(1)}, u32[]{:S(2)}, u32[]{:S(2)}) %all-to-all-start.1) | async-done | bytes 622624 | tf_op jit(solution)/shard_map/all_to_all | solution.py:70
  82.4 0.2 reduce_sum.28
  82.6 21.3 %all_to_all.15 = f32[32,2,256]{2,1,0:T(2,128)S(1)} all-to-all(f32[32,2,256]{2,1,0:T(2,128)S(1)} %constant_dynamic-update-slice_fusion), channel_id=1, replica_groups=mesh['chan'=32,'seg'=16] {'chan'}, dimensions={0} | all-to-all | bytes 131072 | tf_op jit(solution)/shard_map/all_to_all | solution.py:74
  103.9 0.6 reduce_sum.29
  (19 shorter events, 0.4 us)
Async XLA Ops:
  3.1 44.2 %all-to-all-start = ((bf16[32,16,384]{2,1,0:T(8,128)(2,1)}), bf16[32,16,384]{2,1,0:T(8,128)(2,1)S(1)}, u32[]{:S(2)}, u32[]{:S(2)}) async-start(bf16[32,16,384]{2,1,0:T(8,128)(2,1)} %broadcast_in_dim.14), calls=%async_computation | async-start | bytes 786432 | tf_op jit(solution)/shard_map/all_to_all | solution.py:45
  34.7 2.5 %slice-start = ((bf16[16,164737]{1,0:T(8,128)(2,1)}), bf16[16,163840]{1,0:T(8,128)(2,1)S(1)}, s32[]{:S(2)}) async-start(bf16[16,164737]{1,0:T(8,128)(2,1)} %tile.10), calls=%async_computation.3 | async-start | bytes 10485760 | tf_op jit(solution)/shard_map/slice | solution.py:30
  37.2 4.2 %copy-start = (s32[16,512]{1,0:T(8,128)S(1)}, s32[16,512]{1,0:T(8,128)}, u32[]{:S(2)}) copy-start(s32[16,512]{1,0:T(8,128)} %param.7) | copy-start | bytes 98308
  37.2 4.2 %copy-start.1 = (s32[16,512]{1,0:T(8,128)S(1)}, s32[16,512]{1,0:T(8,128)}, u32[]{:S(2)}) copy-start(s32[16,512]{1,0:T(8,128)} %param.6) | copy-start | bytes 98308
  64.3 18.1 %all-to-all-start.1 = ((f32[16,19,2,256]{3,2,1,0:T(2,128)}), f32[16,19,2,256]{3,2,1,0:T(2,128)S(1)}, u32[]{:S(2)}, u32[]{:S(2)}) async-start(f32[16,19,2,256]{3,2,1,0:T(2,128)} %reshape.213), calls=%async_computation.1 | async-start | bytes 1245184 | tf_op jit(solution)/shard_map/all_to_all | solution.py:70

commit v8 on v7

--- a/solution.py
+++ b/solution.py
@@ -3,6 +3,8 @@
 import jax
 import jax.numpy as jnp
 from jax import lax
+from jax.experimental import pallas as pl
+from jax.experimental.pallas import tpu as pltpu
 from jax.sharding import PartitionSpec as P
 
 LAGS = 256
@@ -31,6 +33,42 @@
     return tiled.reshape(chan_count, lag_count, width - 1)[:, :, :sample_count]
 
 
+def bucket_body(x_ref, t_ref, lab_ref, want_ref, o_ref):
+    @pl.when(pl.program_id(0) == 0)
+    def _():
+        o_ref[...] = jnp.zeros_like(o_ref)
+
+    pairs = lax.dot_general(
+        x_ref[...], t_ref[0], (((1,), (1,)), ((), ())), preferred_element_type=jnp.float32
+    )
+    high = pairs.astype(jnp.bfloat16)
+    low = (pairs - high.astype(jnp.float32)).astype(jnp.bfloat16)
+    hits = jnp.where(want_ref[...] == lab_ref[0], 1.0, 0.0).astype(jnp.bfloat16)
+    o_ref[...] += jnp.dot(hits, high, preferred_element_type=jnp.float32) + jnp.dot(
+        hits, low, preferred_element_type=jnp.float32
+    )
+
+
+def bucket_sums(piece, kernel, labels, wanted):
+    row_count, sample_count = piece.shape
+    chan_count, lag_count, _ = kernel.shape
+    rows = wanted.shape[0]
+    flops = 2 * chan_count * row_count * lag_count * (sample_count + 2 * rows)
+    return pl.pallas_call(
+        bucket_body,
+        grid=(chan_count,),
+        in_specs=[
+            pl.BlockSpec((row_count, sample_count), lambda j: (0, 0)),
+            pl.BlockSpec((1, lag_count, sample_count), lambda j: (j, 0, 0)),
+            pl.BlockSpec((1, 1, row_count), lambda j: (j, 0, 0)),
+            pl.BlockSpec((rows, 1), lambda j: (0, 0)),
+        ],
+        out_specs=pl.BlockSpec((rows, lag_count), lambda j: (0, 0)),
+        out_shape=jax.ShapeDtypeStruct((rows, lag_count), jnp.float32),
+        cost_estimate=pl.CostEstimate(flops=flops, transcendentals=0, bytes_accessed=4 * rows * lag_count),
+    )(piece, kernel, labels.reshape(chan_count, 1, row_count), wanted.reshape(rows, 1))
+
+
 def shards(traces, taper_len, gather_id, offset_bin):
     chan_count = traces.shape[0]
     chan_devices = lax.axis_size("chan")
@@ -44,11 +82,9 @@
     copies = jnp.broadcast_to(flat[None], (chan_devices,) + flat.shape)
     piece = lax.all_to_all(copies, "chan", 0, 0, tiled=True).reshape(-1, flat.shape[1])
     row_count = piece.shape[0]
-    product = jnp.einsum("it,jkt->ijk", piece, kernel, preferred_element_type=jnp.float32)
-    product = jnp.transpose(product, (1, 0, 2)).reshape(row_count * chan_count, LAGS)
     labels = gather_id * OFFBINS + offset_bin
     partner = jnp.arange(row_count, dtype=jnp.int32)[None, :]
-    labels = jnp.where(partner == own_rows.reshape(-1, 1), -1, labels).reshape(-1)
+    labels = jnp.where(partner == own_rows.reshape(-1, 1), -1, labels)
     gathers = chan_devices * seg_devices
     low_span = 2 * (row_count - 1)
     reach = (low_span + 5 * (chan_count - 1)) * gathers // (2 * low_span + 1) + 2
@@ -59,12 +95,7 @@
     first = jnp.maximum(first, 0)
     window = (first[:, None] + jnp.arange(depth, dtype=jnp.int32)[None, :]) * seg_devices + lanes[:, None]
     wanted = (window[:, :, None] * OFFBINS + jnp.arange(OFFBINS, dtype=jnp.int32)).reshape(-1)
-    onehot = (wanted[:, None] == labels[None, :]).astype(jnp.bfloat16)
-    high = lax.reduce_precision(product, exponent_bits=8, mantissa_bits=7)
-    low = product - high
-    split = jnp.concatenate([high, low], axis=1).astype(jnp.bfloat16)
-    both = jnp.dot(onehot, split, preferred_element_type=jnp.float32)
-    total = both[:, :LAGS] + both[:, LAGS:]
+    total = bucket_sums(piece, kernel, labels, wanted)
     scale = 1.0 / math.sqrt(traces.shape[2] * traces.shape[1] * seg_devices)
     stacked = (total * scale).reshape(seg_devices, depth, OFFBINS, LAGS)
     part = jnp.sum(lax.all_to_all(stacked, "seg", 0, 0, tiled=True), axis=0)

time: 105 us -> 112 us (1.067)
  Pallas kernels: 0 us -> 19.3 us
  matrix products: 11.8 us -> 0 us
  other arithmetic: 8.13 us -> 5.23 us
  local copies, waits for them, and re-layouts: 21.4 us -> 23.3 us
    pallas_call x0 -> x1, Pallas kernels: none -> 19.3 us  [bucket_sums(): pl.pallas_call(bucket_body, grid=(chan_count,), in_specs=[pl.BlockSpec((r...]
    dot_general x2 -> x0, matrix products: 11.8 us -> none  [the longest x1 7.52 us: shards(): both = jnp.dot(onehot, split, preferred_element_type=jnp.float32)]
    another operation x1 -> x0, other arithmetic: 3.95 us -> none
    slice x0 -> x1, local copies, waits for them, and re-layouts: none -> 2.04 us  [toeplitz(): return tiled.reshape(chan_count, lag_count, width - 1)[:, :, :sample_count]]
    unnamed x6 -> x7, local copies, waits for them, and re-layouts: 3.18 us -> 1.62 us
where the time goes in v8:
time: 112 us; the launch traced here: 111 us
  starting transfers between devices  25.7 us (23%)
  local copies, waits for them, and re-layouts  23.3 us (21%)
  blocking collectives  22.3 us (20%)
  Pallas kernels  19.3 us (17%)
  waiting for transfers between devices  13 us (12%)
  other arithmetic  5.23 us (5%)
  between operations  2.05 us (2%)
    all_to_all x1, blocking collectives, shards(): pieces = lax.all_to_all(dense, 'chan', 0, 0, tiled=True)  22.3 us
    pallas_call x1, Pallas kernels, bucket_sums(): pl.pallas_call(bucket_body, grid=(chan_count,), in_specs=[pl.BlockSpec((r...  19.3 us
    all_to_all x1, starting transfers between devices, shards(): lax.all_to_all(copies, 'chan', 0, 0, tiled=True).reshape(-1, flat.shape[1])  18.5 us
    another operation x2, local copies, waits for them, and re-layouts, toeplitz(): tiled = jnp.tile(ring, (1, lag_count + 1))[:, :lag_count * (width - 1)]  11.9 us
    all_to_all x1, waiting for transfers between devices, shards(): part = jnp.sum(lax.all_to_all(stacked, 'seg', 0, 0, tiled=True), axis=0)  8.36 us
    all_to_all x1, starting transfers between devices, shards(): part = jnp.sum(lax.all_to_all(stacked, 'seg', 0, 0, tiled=True), axis=0)  7.25 us
    all_to_all x1, waiting for transfers between devices, shards(): lax.all_to_all(copies, 'chan', 0, 0, tiled=True).reshape(-1, flat.shape[1])  4.68 us
    slice x2, local copies, waits for them, and re-layouts, toeplitz(): tiled = jnp.tile(ring, (1, lag_count + 1))[:, :lag_count * (width - 1)]  2.49 us
  transfers between devices with their start and end apart: 2, of which 2 were waited for; matrix products, arithmetic and copies ran while one was open for 17% of the time, Pallas kernels for 0%

profile of v8, /device:TPU:1, one launch (start us, length us, event | category | flops | bytes accessed | tf_op | source)
XLA Modules:
  0.0 111.0 jit_solution(17427571197477775568)
XLA Ops:
  0.0 0.8 fusion.3
  0.8 0.7 convert_element_type.22
  1.5 0.8 fusion.4
  2.3 0.8 broadcast_in_dim.12
  3.1 18.5 %all-to-all-start = ((bf16[32,16,384]{2,1,0:T(8,128)(2,1)}), bf16[32,16,384]{2,1,0:T(8,128)(2,1)S(1)}, u32[]{:S(2)}, u32[]{:S(2)}) async-start(bf16[32,16,384]{2,1,0:T(8,128)(2,1)} %broadcast_in_dim.12), calls=%async_computation | async-start | bytes 786432 | tf_op jit(solution)/shard_map/all_to_all | solution.py:83
  21.6 1.2 %slice.19 = s32[1,1]{1,0:T(1,128)} slice(s32[16,512]{1,0:T(8,128)} %param.6), slice={[0:1], [0:1]} | slice | bytes 8 | tf_op jit(solution)/shard_map/slice | solution.py:92
  22.9 3.1 %tile.4 = bf16[16,257,641]{2,1,0:T(8,128)(2,1)} broadcast(bf16[16,641]{1,0:T(8,128)(2,1)S(1)} %pad_maximum_fusion), dimensions={0,2} | broadcast | bytes 5292096 | tf_op jit(solution)/shard_map/tile | solution.py:32
  26.0 8.7 %tile.10 = bf16[16,164737]{1,0:T(8,128)(2,1)} reshape(bf16[16,257,641]{2,1,0:T(8,128)(2,1)} %tile.4) | data formatting | bytes 10543168 | tf_op jit(solution)/shard_map/tile | solution.py:32
  34.7 2.5 %slice-done = bf16[16,163840]{1,0:T(8,128)(2,1)S(1)} async-done(((bf16[16,164737]{1,0:T(8,128)(2,1)}), bf16[16,163840]{1,0:T(8,128)(2,1)S(1)}, s32[]{:S(2)}) %slice-start) | async-done | bytes 5242904 | tf_op jit(solution)/shard_map/slice | solution.py:32
  37.2 0.8 copy.10
  38.1 2.0 %slice.23.t_ref = bf16[16,256,384]{2,1,0:T(8,128)(2,1)} slice(bf16[16,256,640]{2,1,0:T(8,128)(2,1)S(1)} %bitcast.9), slice={[0:16], [0:256], [0:384]} | slice | bytes 6291456 | tf_op jit(solution)/shard_map/slice | solution.py:33
  40.1 0.7 fusion.5
  41.0 0.8 add.124.want_ref
  41.9 0.6 reshape.219.lab_ref
  42.6 4.7 %all-to-all-done = bf16[32,16,384]{2,1,0:T(8,128)(2,1)S(1)} async-done(((bf16[32,16,384]{2,1,0:T(8,128)(2,1)}), bf16[32,16,384]{2,1,0:T(8,128)(2,1)S(1)}, u32[]{:S(2)}, u32[]{:S(2)}) %all-to-all-start) | async-done | bytes 393248 | tf_op jit(solution)/shard_map/all_to_all | solution.py:83
  47.2 0.8 copy-done
  48.0 19.3 %shard_map.46 = f32[608,256]{1,0:T(8,128)} custom-call(bf16[512,384]{1,0:T(8,128)(2,1)} %bitcast.10, bf16[16,256,384]{2,1,0:T(8,128)(2,1)} %slice.23.t_ref, s32[16,1,512]{2,1,0:T(1,128)} %reshape.219.lab_ref, s32[608,1]{1,0:T(8,128)} %add.124.want_ref), custom_call_target="tpu_custom_call" | custom-call | flops 6710886400 | bytes 622592 | tf_op jit(solution)/shard_map/pallas_call | solution.py:57
  67.3 1.1 %broadcast_multiply_fusion = f32[608,256]{1,0:T(8,128)S(1)} fusion(f32[608,256]{1,0:T(8,128)} %shard_map.46), kind=kLoop, calls=%fused_computation | loop fusion | flops 155648 | bytes 1245184 | tf_op jit(solution)/shard_map/mul | solution.py:100
  68.5 1.2 %reshape.220 = f32[16,19,2,256]{3,2,1,0:T(2,128)} reshape(f32[608,256]{1,0:T(8,128)S(1)} %broadcast_multiply_fusion) | data formatting | bytes 1245184 | tf_op jit(solution)/shard_map/reshape | solution.py:100
  69.7 7.2 %all-to-all-start.1 = ((f32[16,19,2,256]{3,2,1,0:T(2,128)}), f32[16,19,2,256]{3,2,1,0:T(2,128)S(1)}, u32[]{:S(2)}, u32[]{:S(2)}) async-start(f32[16,19,2,256]{3,2,1,0:T(2,128)} %reshape.220), calls=%async_computation.1 | async-start | bytes 1245184 | tf_op jit(solution)/shard_map/all_to_all | solution.py:101
  76.9 0.6 dynamic_slice.3
  79.4 8.4 %all-to-all-done.1 = f32[16,19,2,256]{3,2,1,0:T(2,128)S(1)} async-done(((f32[16,19,2,256]{3,2,1,0:T(2,128)}), f32[16,19,2,256]{3,2,1,0:T(2,128)S(1)}, u32[]{:S(2)}, u32[]{:S(2)}) %all-to-all-start.1) | async-done | bytes 622624 | tf_op jit(solution)/shard_map/all_to_all | solution.py:101
  88.0 22.3 %all_to_all.15 = f32[32,2,256]{2,1,0:T(2,128)S(1)} all-to-all(f32[32,2,256]{2,1,0:T(2,128)S(1)} %constant_dynamic-update-slice_fusion), channel_id=1, replica_groups=mesh['chan'=32,'seg'=16] {'chan'}, dimensions={0} | all-to-all | bytes 131072 | tf_op jit(solution)/shard_map/all_to_all | solution.py:105
  110.4 0.6 reduce_sum.29
  (20 shorter events, 0.6 us)
Async XLA Ops:
  3.1 44.2 %all-to-all-start = ((bf16[32,16,384]{2,1,0:T(8,128)(2,1)}), bf16[32,16,384]{2,1,0:T(8,128)(2,1)S(1)}, u32[]{:S(2)}, u32[]{:S(2)}) async-start(bf16[32,16,384]{2,1,0:T(8,128)(2,1)} %broadcast_in_dim.12), calls=%async_computation | async-start | bytes 786432 | tf_op jit(solution)/shard_map/all_to_all | solution.py:83
  34.7 2.5 %slice-start = ((bf16[16,164737]{1,0:T(8,128)(2,1)}), bf16[16,163840]{1,0:T(8,128)(2,1)S(1)}, s32[]{:S(2)}) async-start(bf16[16,164737]{1,0:T(8,128)(2,1)} %tile.10), calls=%async_computation.3 | async-start | bytes 10485760 | tf_op jit(solution)/shard_map/slice | solution.py:32
  38.1 3.8 %copy-start.1 = (s32[16,512]{1,0:T(8,128)S(1)}, s32[16,512]{1,0:T(8,128)}, u32[]{:S(2)}) copy-start(s32[16,512]{1,0:T(8,128)} %param.7) | copy-start | bytes 98308
  38.1 3.7 %copy-start.2 = (s32[16,512]{1,0:T(8,128)S(1)}, s32[16,512]{1,0:T(8,128)}, u32[]{:S(2)}) copy-start(s32[16,512]{1,0:T(8,128)} %param.6) | copy-start | bytes 98308
  47.2 0.8 copy-start
  69.7 18.1 %all-to-all-start.1 = ((f32[16,19,2,256]{3,2,1,0:T(2,128)}), f32[16,19,2,256]{3,2,1,0:T(2,128)S(1)}, u32[]{:S(2)}, u32[]{:S(2)}) async-start(f32[16,19,2,256]{3,2,1,0:T(2,128)} %reshape.220), calls=%async_computation.1 | async-start | bytes 1245184 | tf_op jit(solution)/shard_map/all_to_all | solution.py:101

commit v9 on v8

--- a/solution.py
+++ b/solution.py
@@ -33,7 +33,7 @@
     return tiled.reshape(chan_count, lag_count, width - 1)[:, :, :sample_count]
 
 
-def bucket_body(x_ref, t_ref, lab_ref, want_ref, o_ref):
+def bucket_body(x_ref, t_ref, lab_ref, o_ref):
     @pl.when(pl.program_id(0) == 0)
     def _():
         o_ref[...] = jnp.zeros_like(o_ref)
@@ -43,7 +43,7 @@
     )
     high = pairs.astype(jnp.bfloat16)
     low = (pairs - high.astype(jnp.float32)).astype(jnp.bfloat16)
-    hits = jnp.where(want_ref[...] == lab_ref[0], 1.0, 0.0).astype(jnp.bfloat16)
+    hits = lab_ref[0]
     o_ref[...] += jnp.dot(hits, high, preferred_element_type=jnp.float32) + jnp.dot(
         hits, low, preferred_element_type=jnp.float32
     )
@@ -53,6 +53,7 @@
     row_count, sample_count = piece.shape
     chan_count, lag_count, _ = kernel.shape
     rows = wanted.shape[0]
+    hits = (wanted[None, :, None] == labels[:, None, :]).astype(jnp.bfloat16)
     flops = 2 * chan_count * row_count * lag_count * (sample_count + 2 * rows)
     return pl.pallas_call(
         bucket_body,
@@ -60,13 +61,12 @@
         in_specs=[
             pl.BlockSpec((row_count, sample_count), lambda j: (0, 0)),
             pl.BlockSpec((1, lag_count, sample_count), lambda j: (j, 0, 0)),
-            pl.BlockSpec((1, 1, row_count), lambda j: (j, 0, 0)),
-            pl.BlockSpec((rows, 1), lambda j: (0, 0)),
+            pl.BlockSpec((1, rows, row_count), lambda j: (j, 0, 0)),
         ],
         out_specs=pl.BlockSpec((rows, lag_count), lambda j: (0, 0)),
         out_shape=jax.ShapeDtypeStruct((rows, lag_count), jnp.float32),
         cost_estimate=pl.CostEstimate(flops=flops, transcendentals=0, bytes_accessed=4 * rows * lag_count),
-    )(piece, kernel, labels.reshape(chan_count, 1, row_count), wanted.reshape(rows, 1))
+    )(piece, kernel, hits)
 
 
 def shards(traces, taper_len, gather_id, offset_bin):

time: 112 us -> 118 us (1.054)
  other arithmetic: 5.23 us -> 11.8 us
  blocking collectives: 22.3 us -> 27.6 us
  waiting for transfers between devices: 13 us -> 8.37 us
  local copies, waits for them, and re-layouts: 23.3 us -> 22 us
    convert_element_type x0 -> x1, other arithmetic: none -> 6.59 us  [bucket_sums(): hits = (wanted[None, :, None] == labels[:, None, :]).astype(jnp.bfloat16)]
    all_to_all x1, blocking collectives: 22.3 us -> 27.6 us  [shards(): pieces = lax.all_to_all(dense, 'chan', 0, 0, tiled=True)]
    all_to_all x1, waiting for transfers between devices: 4.68 us -> 0.01 us  [shards(): lax.all_to_all(copies, 'chan', 0, 0, tiled=True).reshape(-1, flat.shape[1])]
  transfers between devices with their start and end apart: 2 -> 2, of which waited for: 2 -> 1; matrix products, arithmetic and copies ran while one was open for 17% -> 21% of each run, Pallas kernels for 0% -> 0%
where the time goes in v9:
time: 118 us; the launch traced here: 117 us
  blocking collectives  27.6 us (23%)
  starting transfers between devices  25.1 us (21%)
  local copies, waits for them, and re-layouts  22 us (19%)
  Pallas kernels  20.2 us (17%)
  other arithmetic  11.8 us (10%)
  waiting for transfers between devices  8.37 us (7%)
  between operations  2.08 us (2%)
    all_to_all x1, blocking collectives, shards(): pieces = lax.all_to_all(dense, 'chan', 0, 0, tiled=True)  27.6 us
    pallas_call x1, Pallas kernels, bucket_sums(): pl.pallas_call(bucket_body, grid=(chan_count,), in_specs=[pl.BlockSpec((r...  20.2 us
    all_to_all x1, starting transfers between devices, shards(): lax.all_to_all(copies, 'chan', 0, 0, tiled=True).reshape(-1, flat.shape[1])  18.5 us
    another operation x2, local copies, waits for them, and re-layouts, toeplitz(): tiled = jnp.tile(ring, (1, lag_count + 1))[:, :lag_count * (width - 1)]  11.9 us
    all_to_all x1, waiting for transfers between devices, shards(): part = jnp.sum(lax.all_to_all(stacked, 'seg', 0, 0, tiled=True), axis=0)  8.36 us
    all_to_all x1, starting transfers between devices, shards(): part = jnp.sum(lax.all_to_all(stacked, 'seg', 0, 0, tiled=True), axis=0)  6.62 us
    convert_element_type x1, other arithmetic, bucket_sums(): hits = (wanted[None, :, None] == labels[:, None, :]).astype(jnp.bfloat16)  6.59 us
    slice x2, local copies, waits for them, and re-layouts, toeplitz(): tiled = jnp.tile(ring, (1, lag_count + 1))[:, :lag_count * (width - 1)]  2.49 us
  transfers between devices with their start and end apart: 2, of which 1 were waited for; matrix products, arithmetic and copies ran while one was open for 21% of the time, Pallas kernels for 0%

profile of v9, /device:TPU:1, one launch (start us, length us, event | category | flops | bytes accessed | tf_op | source)
XLA Modules:
  0.0 117.1 jit_solution(663876190081459496)
XLA Ops:
  0.0 0.8 fusion.3
  0.8 0.7 convert_element_type.25
  1.5 0.8 fusion.4
  2.3 0.8 broadcast_in_dim.12
  3.1 18.5 %all-to-all-start = ((bf16[32,16,384]{2,1,0:T(8,128)(2,1)}), bf16[32,16,384]{2,1,0:T(8,128)(2,1)S(1)}, u32[]{:S(2)}, u32[]{:S(2)}) async-start(bf16[32,16,384]{2,1,0:T(8,128)(2,1)} %broadcast_in_dim.12), calls=%async_computation | async-start | bytes 786432 | tf_op jit(solution)/shard_map/all_to_all | solution.py:83
  21.6 1.2 %slice.19 = s32[1,1]{1,0:T(1,128)} slice(s32[16,512]{1,0:T(8,128)} %param.6), slice={[0:1], [0:1]} | slice | bytes 8 | tf_op jit(solution)/shard_map/slice | solution.py:92
  22.8 0.7 fusion.5
  23.6 3.1 %tile.4 = bf16[16,257,641]{2,1,0:T(8,128)(2,1)} broadcast(bf16[16,641]{1,0:T(8,128)(2,1)S(1)} %pad_maximum_fusion), dimensions={0,2} | broadcast | bytes 5292096 | tf_op jit(solution)/shard_map/tile | solution.py:32
  26.7 8.7 %tile.10 = bf16[16,164737]{1,0:T(8,128)(2,1)} reshape(bf16[16,257,641]{2,1,0:T(8,128)(2,1)} %tile.4) | data formatting | bytes 10543168 | tf_op jit(solution)/shard_map/tile | solution.py:32
  35.5 2.5 %slice-done = bf16[16,163840]{1,0:T(8,128)(2,1)S(1)} async-done(((bf16[16,164737]{1,0:T(8,128)(2,1)}), bf16[16,163840]{1,0:T(8,128)(2,1)S(1)}, s32[]{:S(2)}) %slice-start) | async-done | bytes 5242904 | tf_op jit(solution)/shard_map/slice | solution.py:32
  38.0 0.8 copy.7
  38.8 2.1 %slice.23.t_ref = bf16[16,256,384]{2,1,0:T(8,128)(2,1)} slice(bf16[16,256,640]{2,1,0:T(8,128)(2,1)S(1)} %bitcast.9), slice={[0:16], [0:256], [0:384]} | slice | bytes 6291456 | tf_op jit(solution)/shard_map/slice | solution.py:33
  41.1 0.1 add.115
  41.3 6.6 %compare_convert_fusion.lab_ref = bf16[16,608,512]{2,1,0:T(8,128)(2,1)} fusion(s32[16,512]{1,0:T(8,128)S(1)} %add_select_fusion, s32[608]{0:T(1024)S(1)} %add.115), kind=kLoop, calls=%fused_computation | loop fusion | flops 9961472 | bytes 9996672 | tf_op jit(solution)/shard_map/convert_element_type | solution.py:56
  47.9 0.7 copy-done
  48.7 20.2 %shard_map.46 = f32[608,256]{1,0:T(8,128)} custom-call(bf16[512,384]{1,0:T(8,128)(2,1)} %bitcast.10, bf16[16,256,384]{2,1,0:T(8,128)(2,1)} %slice.23.t_ref, bf16[16,608,512]{2,1,0:T(8,128)(2,1)} %compare_convert_fusion.lab_ref), custom_call_target="tpu_custom_call" | custom-call | flops 6710886400 | bytes 622592 | tf_op jit(solution)/shard_map/pallas_call | solution.py:58
  68.8 1.1 broadcast_multiply_fusion
  70.0 1.2 %reshape.209 = f32[16,19,2,256]{3,2,1,0:T(2,128)} reshape(f32[608,256]{1,0:T(8,128)S(1)} %broadcast_multiply_fusion) | data formatting | bytes 1245184 | tf_op jit(solution)/shard_map/reshape | solution.py:100
  71.1 6.6 %all-to-all-start.1 = ((f32[16,19,2,256]{3,2,1,0:T(2,128)}), f32[16,19,2,256]{3,2,1,0:T(2,128)S(1)}, u32[]{:S(2)}, u32[]{:S(2)}) async-start(f32[16,19,2,256]{3,2,1,0:T(2,128)} %reshape.209), calls=%async_computation.1 | async-start | bytes 1245184 | tf_op jit(solution)/shard_map/all_to_all | solution.py:101
  77.8 0.6 dynamic_slice.3
  80.3 8.4 %all-to-all-done.1 = f32[16,19,2,256]{3,2,1,0:T(2,128)S(1)} async-done(((f32[16,19,2,256]{3,2,1,0:T(2,128)}), f32[16,19,2,256]{3,2,1,0:T(2,128)S(1)}, u32[]{:S(2)}, u32[]{:S(2)}) %all-to-all-start.1) | async-done | bytes 622624 | tf_op jit(solution)/shard_map/all_to_all | solution.py:101
  88.7 0.2 reduce_sum.28
  88.9 27.6 %all_to_all.15 = f32[32,2,256]{2,1,0:T(2,128)S(1)} all-to-all(f32[32,2,256]{2,1,0:T(2,128)S(1)} %constant_dynamic-update-slice_fusion), channel_id=1, replica_groups=mesh['chan'=32,'seg'=16] {'chan'}, dimensions={0} | all-to-all | bytes 131072 | tf_op jit(solution)/shard_map/all_to_all | solution.py:105
  116.5 0.6 reduce_sum.29
  (20 shorter events, 0.4 us)
Async XLA Ops:
  3.1 44.8 %all-to-all-start = ((bf16[32,16,384]{2,1,0:T(8,128)(2,1)}), bf16[32,16,384]{2,1,0:T(8,128)(2,1)S(1)}, u32[]{:S(2)}, u32[]{:S(2)}) async-start(bf16[32,16,384]{2,1,0:T(8,128)(2,1)} %broadcast_in_dim.12), calls=%async_computation | async-start | bytes 786432 | tf_op jit(solution)/shard_map/all_to_all | solution.py:83
  35.5 2.5 %slice-start = ((bf16[16,164737]{1,0:T(8,128)(2,1)}), bf16[16,163840]{1,0:T(8,128)(2,1)S(1)}, s32[]{:S(2)}) async-start(bf16[16,164737]{1,0:T(8,128)(2,1)} %tile.10), calls=%async_computation.3 | async-start | bytes 10485760 | tf_op jit(solution)/shard_map/slice | solution.py:32
  38.0 3.3 %copy-start.1 = (s32[16,512]{1,0:T(8,128)S(1)}, s32[16,512]{1,0:T(8,128)}, u32[]{:S(2)}) copy-start(s32[16,512]{1,0:T(8,128)} %param.7) | copy-start | bytes 98308
  38.0 3.3 %copy-start.2 = (s32[16,512]{1,0:T(8,128)S(1)}, s32[16,512]{1,0:T(8,128)}, u32[]{:S(2)}) copy-start(s32[16,512]{1,0:T(8,128)} %param.6) | copy-start | bytes 98308
  47.9 0.7 copy-start
  71.1 17.5 %all-to-all-start.1 = ((f32[16,19,2,256]{3,2,1,0:T(2,128)}), f32[16,19,2,256]{3,2,1,0:T(2,128)S(1)}, u32[]{:S(2)}, u32[]{:S(2)}) async-start(f32[16,19,2,256]{3,2,1,0:T(2,128)} %reshape.209), calls=%async_computation.1 | async-start | bytes 1245184 | tf_op jit(solution)/shard_map/all_to_all | solution.py:101

commit v10 on v7

--- a/solution.py
+++ b/solution.py
@@ -59,7 +59,7 @@
     first = jnp.maximum(first, 0)
     window = (first[:, None] + jnp.arange(depth, dtype=jnp.int32)[None, :]) * seg_devices + lanes[:, None]
     wanted = (window[:, :, None] * OFFBINS + jnp.arange(OFFBINS, dtype=jnp.int32)).reshape(-1)
-    onehot = (wanted[:, None] == labels[None, :]).astype(jnp.bfloat16)
+    onehot = lax.optimization_barrier((wanted[:, None] == labels[None, :]).astype(jnp.bfloat16))
     high = lax.reduce_precision(product, exponent_bits=8, mantissa_bits=7)
     low = product - high
     split = jnp.concatenate([high, low], axis=1).astype(jnp.bfloat16)

time: 105 us -> 114 us (1.086)
  blocking collectives: 21.3 us -> 27.8 us
  other arithmetic: 8.13 us -> 14.5 us
  waiting for transfers between devices: 14.1 us -> 8.37 us
  matrix products: 11.8 us -> 13.9 us
    all_to_all x1, blocking collectives: 21.3 us -> 27.8 us  [shards(): pieces = lax.all_to_all(dense, 'chan', 0, 0, tiled=True)]
    convert_element_type x0 -> x1, other arithmetic: none -> 6.45 us  [shards(): (wanted[:, None] == labels[None, :]).astype(jnp.bfloat16)]
    all_to_all x1, waiting for transfers between devices: 5.73 us -> 0.01 us  [shards(): lax.all_to_all(copies, 'chan', 0, 0, tiled=True).reshape(-1, flat.shape[1])]
    dot_general x1, matrix products: 7.52 us -> 9.65 us  [shards(): both = jnp.dot(onehot, split, preferred_element_type=jnp.float32)]
  transfers between devices with their start and end apart: 2 -> 2, of which waited for: 2 -> 1; matrix products, arithmetic and copies ran while one was open for 17% -> 22% of each run, Pallas kernels for 0% -> 0%
where the time goes in v10:
time: 114 us; the launch traced here: 113 us
  blocking collectives  27.8 us (24%)
  starting transfers between devices  24.9 us (22%)
  local copies, waits for them, and re-layouts  21.5 us (19%)
  other arithmetic  14.5 us (13%)
  matrix products  13.9 us (12%)
  waiting for transfers between devices  8.37 us (7%)
  between operations  2.09 us (2%)
    all_to_all x1, blocking collectives, shards(): pieces = lax.all_to_all(dense, 'chan', 0, 0, tiled=True)  27.8 us
    all_to_all x1, starting transfers between devices, shards(): lax.all_to_all(copies, 'chan', 0, 0, tiled=True).reshape(-1, flat.shape[1])  18.5 us
    another operation x2, local copies, waits for them, and re-layouts, toeplitz(): tiled = jnp.tile(ring, (1, lag_count + 1))[:, :lag_count * (width - 1)]  11.9 us
    dot_general x1, matrix products, shards(): both = jnp.dot(onehot, split, preferred_element_type=jnp.float32)  9.65 us
    all_to_all x1, waiting for transfers between devices, shards(): part = jnp.sum(lax.all_to_all(stacked, 'seg', 0, 0, tiled=True), axis=0)  8.36 us
    all_to_all x1, starting transfers between devices, shards(): part = jnp.sum(lax.all_to_all(stacked, 'seg', 0, 0, tiled=True), axis=0)  6.45 us
    convert_element_type x1, other arithmetic, shards(): (wanted[:, None] == labels[None, :]).astype(jnp.bfloat16)  6.45 us
    dot_general x1, matrix products, shards(): jnp.einsum('it,jkt->ijk', piece, kernel, preferred_element_type=jnp.float32)  4.26 us
  transfers between devices with their start and end apart: 2, of which 1 were waited for; matrix products, arithmetic and copies ran while one was open for 22% of the time, Pallas kernels for 0%

profile of v10, /device:TPU:1, one launch (start us, length us, event | category | flops | bytes accessed | tf_op | source)
XLA Modules:
  0.0 113.1 jit_solution(14945233073575841701)
XLA Ops:
  0.0 0.8 fusion.11
  0.8 0.7 convert_element_type.27
  1.5 0.8 fusion.12
  2.3 0.8 broadcast_in_dim.14
  3.1 18.5 %all-to-all-start = ((bf16[32,16,384]{2,1,0:T(8,128)(2,1)}), bf16[32,16,384]{2,1,0:T(8,128)(2,1)S(1)}, u32[]{:S(2)}, u32[]{:S(2)}) async-start(bf16[32,16,384]{2,1,0:T(8,128)(2,1)} %broadcast_in_dim.14), calls=%async_computation | async-start | bytes 786432 | tf_op jit(solution)/shard_map/all_to_all | solution.py:45
  21.6 1.2 %slice.21 = s32[1,1]{1,0:T(1,128)} slice(s32[16,512]{1,0:T(8,128)} %param.6), slice={[0:1], [0:1]} | slice | bytes 8 | tf_op jit(solution)/shard_map/slice | solution.py:56
  22.8 0.7 fusion.13
  23.6 3.1 %tile.4 = bf16[16,257,641]{2,1,0:T(8,128)(2,1)} broadcast(bf16[16,641]{1,0:T(8,128)(2,1)S(1)} %pad_maximum_fusion), dimensions={0,2} | broadcast | bytes 5292096 | tf_op jit(solution)/shard_map/tile | solution.py:30
  26.7 8.7 %tile.10 = bf16[16,164737]{1,0:T(8,128)(2,1)} reshape(bf16[16,257,641]{2,1,0:T(8,128)(2,1)} %tile.4) | data formatting | bytes 10543168 | tf_op jit(solution)/shard_map/tile | solution.py:30
  35.4 2.5 %slice-done = bf16[16,163840]{1,0:T(8,128)(2,1)S(1)} async-done(((bf16[16,164737]{1,0:T(8,128)(2,1)}), bf16[16,163840]{1,0:T(8,128)(2,1)S(1)}, s32[]{:S(2)}) %slice-start) | async-done | bytes 5242904 | tf_op jit(solution)/shard_map/slice | solution.py:30
  37.9 3.2 %copy.8 = bf16[2,8,256,640]{3,2,1,0:T(8,128)(2,1)} copy(bf16[2,8,256,640]{3,1,2,0:T(8,128)(2,1)S(1)} %bitcast.21) | data formatting | bytes 10485760
  41.2 0.1 iota_add_fusion
  41.3 0.1 add.115
  41.6 6.5 %compare_convert_fusion = bf16[608,8192]{1,0:T(8,128)(2,1)} fusion(s32[8192]{0:T(1024)S(1)} %bitcast.23, s32[608]{0:T(1024)S(1)} %add.115), kind=kLoop, calls=%fused_computation | loop fusion | flops 9961472 | bytes 9996672 | tf_op jit(solution)/shard_map/convert_element_type | solution.py:62
  48.0 4.3 %fusion.5 = f32[512,16,256]{2,0,1:T(8,128)S(1)} fusion(bf16[512,384,1]{1,0,2:T(8,128)(2,1)S(1)} %bitcast.22, bf16[16,256,640]{2,1,0:T(8,128)(2,1)} %bitcast.20), kind=kOutput, calls=%fused_computation.8 | convolution fusion | flops 1610612736 | bytes 11927552 | tf_op jit(solution)/shard_map/it,jkt->ijk/dot_general | solution.py:47
  52.3 3.9 %reduce-precision_convert_fusion = (bf16[8192,256]{1,0:T(8,128)(2,1)S(1)}, bf16[8192,256]{1,0:T(8,128)(2,1)}) fusion(f32[512,16,256]{2,0,1:T(8,128)S(1)} %fusion.5), kind=kLoop, calls=%fused_computation.2 | loop fusion | flops 8388608 | bytes 16777216 | tf_op jit(solution)/shard_map/convert
  56.2 9.7 %fusion.1 = f32[608,512]{1,0:T(8,128)S(1)} fusion(bf16[608,8192]{1,0:T(8,128)(2,1)} %compare_convert_fusion, bf16[8192,256]{1,0:T(8,128)(2,1)} %get-tuple-element.6, bf16[8192,256]{1,0:T(8,128)(2,1)S(1)} %get-tuple-element.5), kind=kOutput, calls=%fused_computation.4 | convolution fusion | flops 5117050880 | bytes 19595264 | tf_op jit(solution)/shard_map/dot_general | solution.py:66
  66.0 1.2 %reshape.213 = f32[16,19,2,256]{3,2,1,0:T(2,128)} reshape(f32[608,256]{1,0:T(8,128)S(1)} %fusion.7) | data formatting | bytes 1245184 | tf_op jit(solution)/shard_map/reshape | solution.py:69
  67.2 6.5 %all-to-all-start.1 = ((f32[16,19,2,256]{3,2,1,0:T(2,128)}), f32[16,19,2,256]{3,2,1,0:T(2,128)S(1)}, u32[]{:S(2)}, u32[]{:S(2)}) async-start(f32[16,19,2,256]{3,2,1,0:T(2,128)} %reshape.213), calls=%async_computation.1 | async-start | bytes 1245184 | tf_op jit(solution)/shard_map/all_to_all | solution.py:70
  73.6 0.6 dynamic_slice.3
  76.1 8.4 %all-to-all-done.1 = f32[16,19,2,256]{3,2,1,0:T(2,128)S(1)} async-done(((f32[16,19,2,256]{3,2,1,0:T(2,128)}), f32[16,19,2,256]{3,2,1,0:T(2,128)S(1)}, u32[]{:S(2)}, u32[]{:S(2)}) %all-to-all-start.1) | async-done | bytes 622624 | tf_op jit(solution)/shard_map/all_to_all | solution.py:70
  84.5 0.2 reduce_sum.28
  84.7 27.8 %all_to_all.15 = f32[32,2,256]{2,1,0:T(2,128)S(1)} all-to-all(f32[32,2,256]{2,1,0:T(2,128)S(1)} %constant_dynamic-update-slice_fusion), channel_id=1, replica_groups=mesh['chan'=32,'seg'=16] {'chan'}, dimensions={0} | all-to-all | bytes 131072 | tf_op jit(solution)/shard_map/all_to_all | solution.py:74
  112.5 0.6 reduce_sum.29
  (20 shorter events, 0.4 us)
Async XLA Ops:
  3.1 45.0 %all-to-all-start = ((bf16[32,16,384]{2,1,0:T(8,128)(2,1)}), bf16[32,16,384]{2,1,0:T(8,128)(2,1)S(1)}, u32[]{:S(2)}, u32[]{:S(2)}) async-start(bf16[32,16,384]{2,1,0:T(8,128)(2,1)} %broadcast_in_dim.14), calls=%async_computation | async-start | bytes 786432 | tf_op jit(solution)/shard_map/all_to_all | solution.py:45
  35.4 2.5 %slice-start = ((bf16[16,164737]{1,0:T(8,128)(2,1)}), bf16[16,163840]{1,0:T(8,128)(2,1)S(1)}, s32[]{:S(2)}) async-start(bf16[16,164737]{1,0:T(8,128)(2,1)} %tile.10), calls=%async_computation.3 | async-start | bytes 10485760 | tf_op jit(solution)/shard_map/slice | solution.py:30
  35.4 6.0 %copy-start = (s32[16,512]{1,0:T(8,128)S(1)}, s32[16,512]{1,0:T(8,128)}, u32[]{:S(2)}) copy-start(s32[16,512]{1,0:T(8,128)} %param.7) | copy-start | bytes 98308
  35.4 6.1 %copy-start.1 = (s32[16,512]{1,0:T(8,128)S(1)}, s32[16,512]{1,0:T(8,128)}, u32[]{:S(2)}) copy-start(s32[16,512]{1,0:T(8,128)} %param.6) | copy-start | bytes 98308
  67.2 17.3 %all-to-all-start.1 = ((f32[16,19,2,256]{3,2,1,0:T(2,128)}), f32[16,19,2,256]{3,2,1,0:T(2,128)S(1)}, u32[]{:S(2)}, u32[]{:S(2)}) async-start(f32[16,19,2,256]{3,2,1,0:T(2,128)} %reshape.213), calls=%async_computation.1 | async-start | bytes 1245184 | tf_op jit(solution)/shard_map/all_to_all | solution.py:70

commit v11 on v7

--- a/solution.py
+++ b/solution.py
@@ -71,8 +71,17 @@
     own_first = first[lax.axis_index("seg")]
     dense = jnp.zeros((chan_devices, OFFBINS, LAGS), jnp.float32)
     dense = lax.dynamic_update_slice(dense, part.reshape(depth, OFFBINS, LAGS), (own_first, 0, 0))
-    pieces = lax.all_to_all(dense, "chan", 0, 0, tiled=True)
-    return jnp.sum(pieces, axis=0, keepdims=True)
+    me = lax.axis_index("chan")
+    reach_bit = chan_devices // 2
+    while reach_bit >= 1:
+        halves = dense.reshape(2, -1, OFFBINS, LAGS)
+        mine = (me // reach_bit) % 2
+        keep = jnp.where(mine == 0, halves[0], halves[1])
+        give = jnp.where(mine == 0, halves[1], halves[0])
+        pairs = [(c, c ^ reach_bit) for c in range(chan_devices)]
+        dense = keep + lax.ppermute(give, "chan", pairs)
+        reach_bit //= 2
+    return dense
 
 
 def solution(mesh):

time: 105 us -> 128 us (1.22)
  the two profiles are of different devices: /device:TPU:1 before, /device:TPU:6 now
where the time goes in v11:
time: 128 us
  waiting for transfers between devices  46.4 us (36%)
  starting transfers between devices  37.5 us (29%)
  local copies, waits for them, and re-layouts  21.5 us (17%)
  matrix products  11.8 us (9%)
  other arithmetic  8.22 us (6%)
  between operations  2.23 us (2%)
    ppermute x5, waiting for transfers between devices, shards(): dense = keep + lax.ppermute(give, 'chan', pairs)  30.9 us
    all_to_all x1, starting transfers between devices, shards(): lax.all_to_all(copies, 'chan', 0, 0, tiled=True).reshape(-1, flat.shape[1])  18.2 us
    ppermute x5, starting transfers between devices, shards(): dense = keep + lax.ppermute(give, 'chan', pairs)  13.4 us
    another operation x2, local copies, waits for them, and re-layouts, toeplitz(): tiled = jnp.tile(ring, (1, lag_count + 1))[:, :lag_count * (width - 1)]  11.9 us
    all_to_all x1, waiting for transfers between devices, shards(): part = jnp.sum(lax.all_to_all(stacked, 'seg', 0, 0, tiled=True), axis=0)  8.27 us
    dot_general x1, matrix products, shards(): both = jnp.dot(onehot, split, preferred_element_type=jnp.float32)  7.52 us
    all_to_all x1, waiting for transfers between devices, shards(): lax.all_to_all(copies, 'chan', 0, 0, tiled=True).reshape(-1, flat.shape[1])  7.2 us
    all_to_all x1, starting transfers between devices, shards(): part = jnp.sum(lax.all_to_all(stacked, 'seg', 0, 0, tiled=True), axis=0)  5.95 us
  transfers between devices with their start and end apart: 7, of which 7 were waited for; matrix products, arithmetic and copies ran while one was open for 14% of the time, Pallas kernels for 0%

profile of v11, /device:TPU:6, one launch (start us, length us, event | category | flops | bytes accessed | tf_op | source)
XLA Modules:
  0.0 127.6 jit_solution(10511395014302500925)
XLA Ops:
  0.0 0.8 fusion.14
  3.1 18.2 %all-to-all-start = ((bf16[32,16,384]{2,1,0:T(8,128)(2,1)}), bf16[32,16,384]{2,1,0:T(8,128)(2,1)S(1)}, u32[]{:S(2)}, u32[]{:S(2)}) async-start(bf16[32,16,384]{2,1,0:T(8,128)(2,1)} %broadcast_in_dim.11), calls=%async_computation | async-start | bytes 786432 | tf_op jit(solution)/shard_map/all_to_all | solution.py:45
  21.3 1.2 slice.71
  22.6 3.1 %tile.4 = bf16[16,257,641]{2,1,0:T(8,128)(2,1)} broadcast(bf16[16,641]{1,0:T(8,128)(2,1)S(1)} %pad_maximum_fusion), dimensions={0,2} | broadcast | bytes 5292096 | tf_op jit(solution)/shard_map/tile | solution.py:30
  25.8 8.7 %tile.10 = bf16[16,164737]{1,0:T(8,128)(2,1)} reshape(bf16[16,257,641]{2,1,0:T(8,128)(2,1)} %tile.4) | data formatting | bytes 10543168 | tf_op jit(solution)/shard_map/tile | solution.py:30
  34.5 2.5 %slice-done = bf16[16,163840]{1,0:T(8,128)(2,1)S(1)} async-done(((bf16[16,164737]{1,0:T(8,128)(2,1)}), bf16[16,163840]{1,0:T(8,128)(2,1)S(1)}, s32[]{:S(2)}) %slice-start) | async-done | bytes 5242904 | tf_op jit(solution)/shard_map/slice | solution.py:30
  37.0 3.1 %copy.6 = bf16[2,8,256,640]{3,2,1,0:T(8,128)(2,1)} copy(bf16[2,8,256,640]{3,1,2,0:T(8,128)(2,1)S(1)} %bitcast.19) | data formatting | bytes 10485760
  41.2 7.2 %all-to-all-done = bf16[32,16,384]{2,1,0:T(8,128)(2,1)S(1)} async-done(((bf16[32,16,384]{2,1,0:T(8,128)(2,1)}), bf16[32,16,384]{2,1,0:T(8,128)(2,1)S(1)}, u32[]{:S(2)}, u32[]{:S(2)}) %all-to-all-start) | async-done | bytes 393248 | tf_op jit(solution)/shard_map/all_to_all | solution.py:45
  48.4 4.3 %fusion.8 = f32[512,16,256]{2,0,1:T(8,128)S(1)} fusion(bf16[512,384,1]{1,0,2:T(8,128)(2,1)S(1)} %bitcast.20, bf16[16,256,640]{2,1,0:T(8,128)(2,1)} %bitcast.18), kind=kOutput, calls=%fused_computation.10 | convolution fusion | flops 1610612736 | bytes 11927552 | tf_op jit(solution)/shard_map/it,jkt->ijk/dot_general | solution.py:47
  52.7 4.0 %reduce-precision_convert_fusion = (bf16[8192,256]{1,0:T(8,128)(2,1)S(1)}, bf16[8192,256]{1,0:T(8,128)(2,1)}) fusion(f32[512,16,256]{2,0,1:T(8,128)S(1)} %fusion.8), kind=kLoop, calls=%fused_computation.3 | loop fusion | flops 8388608 | bytes 16777216 | tf_op jit(solution)/shard_map/convert
  56.7 7.5 %fusion = f32[608,512]{1,0:T(8,128)S(1)} fusion(s32[8192]{0:T(1024)S(1)} %bitcast.21, s32[608]{0:T(1024)S(1)} %add.156, bf16[8192,256]{1,0:T(8,128)(2,1)} %get-tuple-element.6, bf16[8192,256]{1,0:T(8,128)(2,1)S(1)} %get-tuple-element.5), kind=kOutput, calls=%fused_computation | convolution fusion | flops 5122031616 | bytes 9668992 | tf_op jit(solution)/shard_map/dot_general | solution.py:66
  64.3 1.2 reshape.238
  65.5 5.9 %all-to-all-start.1 = ((f32[16,19,2,256]{3,2,1,0:T(2,128)}), f32[16,19,2,256]{3,2,1,0:T(2,128)S(1)}, u32[]{:S(2)}, u32[]{:S(2)}) async-start(f32[16,19,2,256]{3,2,1,0:T(2,128)} %reshape.238), calls=%async_computation.1 | async-start | bytes 1245184 | tf_op jit(solution)/shard_map/all_to_all | solution.py:70
  73.9 8.3 %all-to-all-done.1 = f32[16,19,2,256]{3,2,1,0:T(2,128)S(1)} async-done(((f32[16,19,2,256]{3,2,1,0:T(2,128)}), f32[16,19,2,256]{3,2,1,0:T(2,128)S(1)}, u32[]{:S(2)}, u32[]{:S(2)}) %all-to-all-start.1) | async-done | bytes 622624 | tf_op jit(solution)/shard_map/all_to_all | solution.py:70
  82.5 4.9 %collective-permute-start = (f32[16,2,256]{2,1,0:T(2,128)S(1)}, f32[16,2,256]{2,1,0:T(2,128)S(1)}, u32[]{:S(2)}, u32[]{:S(2)}) collective-permute-start(f32[16,2,256]{2,1,0:T(2,128)S(1)} %broadcast_select_fusion), channel_id=1, source_target_pairs={{0,256},{16,272},{32,288},{48,304},{64,320},{80,336},{96,352},{112... | collective-permute-start | bytes 98312 | tf_op jit(solution)/shard_map/ppermute | solution.py:82
  87.4 11.0 %collective-permute-done = f32[16,2,256]{2,1,0:T(2,128)S(1)} collective-permute-done((f32[16,2,256]{2,1,0:T(2,128)S(1)}, f32[16,2,256]{2,1,0:T(2,128)S(1)}, u32[]{:S(2)}, u32[]{:S(2)}) %collective-permute-start) | collective-permute-done | bytes 32800 | tf_op jit(solution)/shard_map/ppermute | solution.py:82
  98.5 1.9 %collective-permute-start.1 = (f32[8,2,256]{2,1,0:T(2,128)S(1)}, f32[8,2,256]{2,1,0:T(2,128)S(1)}, u32[]{:S(2)}, u32[]{:S(2)}) collective-permute-start(f32[8,2,256]{2,1,0:T(2,128)S(1)} %broadcast_select_fusion.1), channel_id=1, source_target_pairs={{0,128},{16,144},{32,160},{48,176},{64,192},{80,208},{96,224},{112... | collective-permute-start | bytes 49160 | tf_op jit(solution)/shard_map/ppermute | solution.py:82
  100.5 7.6 %collective-permute-done.1 = f32[8,2,256]{2,1,0:T(2,128)S(1)} collective-permute-done((f32[8,2,256]{2,1,0:T(2,128)S(1)}, f32[8,2,256]{2,1,0:T(2,128)S(1)}, u32[]{:S(2)}, u32[]{:S(2)}) %collective-permute-start.1) | collective-permute-done | bytes 16416 | tf_op jit(solution)/shard_map/ppermute | solution.py:82
  108.1 1.9 %collective-permute-start.2 = (f32[4,2,256]{2,1,0:T(2,128)S(1)}, f32[4,2,256]{2,1,0:T(2,128)S(1)}, u32[]{:S(2)}, u32[]{:S(2)}) collective-permute-start(f32[4,2,256]{2,1,0:T(2,128)S(1)} %broadcast_select_fusion.2), channel_id=1, source_target_pairs={{0,64},{16,80},{32,96},{48,112},{64,0},{80,16},{96,32},{112,48},{1... | collective-permute-start | bytes 24584 | tf_op jit(solution)/shard_map/ppermute | solution.py:82
  110.0 4.5 %collective-permute-done.2 = f32[4,2,256]{2,1,0:T(2,128)S(1)} collective-permute-done((f32[4,2,256]{2,1,0:T(2,128)S(1)}, f32[4,2,256]{2,1,0:T(2,128)S(1)}, u32[]{:S(2)}, u32[]{:S(2)}) %collective-permute-start.2) | collective-permute-done | bytes 8224 | tf_op jit(solution)/shard_map/ppermute | solution.py:82
  114.5 2.1 %collective-permute-start.3 = (f32[2,2,256]{2,1,0:T(2,128)S(1)}, f32[2,2,256]{2,1,0:T(2,128)S(1)}, u32[]{:S(2)}, u32[]{:S(2)}) collective-permute-start(f32[2,2,256]{2,1,0:T(2,128)S(1)} %broadcast_select_fusion.3), channel_id=1, source_target_pairs={{0,32},{16,48},{32,0},{48,16},{64,96},{80,112},{96,64},{112,80},{1... | collective-permute-start | bytes 12296 | tf_op jit(solution)/shard_map/ppermute | solution.py:82
  116.7 3.3 %collective-permute-done.3 = f32[2,2,256]{2,1,0:T(2,128)S(1)} collective-permute-done((f32[2,2,256]{2,1,0:T(2,128)S(1)}, f32[2,2,256]{2,1,0:T(2,128)S(1)}, u32[]{:S(2)}, u32[]{:S(2)}) %collective-permute-start.3) | collective-permute-done | bytes 4128 | tf_op jit(solution)/shard_map/ppermute | solution.py:82
  120.0 2.5 %collective-permute-start.4 = (f32[1,2,256]{2,1,0:T(2,128)S(1)}, f32[1,2,256]{2,1,0:T(2,128)S(1)}, u32[]{:S(2)}, u32[]{:S(2)}) collective-permute-start(f32[1,2,256]{2,1,0:T(2,128)S(1)} %broadcast_select_fusion.4), channel_id=1, source_target_pairs={{0,16},{16,0},{32,48},{48,32},{64,80},{80,64},{96,112},{112,96},{1... | collective-permute-start | bytes 6152 | tf_op jit(solution)/shard_map/ppermute | solution.py:82
  122.5 4.5 %collective-permute-done.4 = f32[1,2,256]{2,1,0:T(2,128)S(1)} collective-permute-done((f32[1,2,256]{2,1,0:T(2,128)S(1)}, f32[1,2,256]{2,1,0:T(2,128)S(1)}, u32[]{:S(2)}, u32[]{:S(2)}) %collective-permute-start.4) | collective-permute-done | bytes 2080 | tf_op jit(solution)/shard_map/ppermute | solution.py:82
  (37 shorter events, 5.0 us)
Async XLA Ops:
  3.1 45.3 %all-to-all-start = ((bf16[32,16,384]{2,1,0:T(8,128)(2,1)}), bf16[32,16,384]{2,1,0:T(8,128)(2,1)S(1)}, u32[]{:S(2)}, u32[]{:S(2)}) async-start(bf16[32,16,384]{2,1,0:T(8,128)(2,1)} %broadcast_in_dim.11), calls=%async_computation | async-start | bytes 786432 | tf_op jit(solution)/shard_map/all_to_all | solution.py:45
  34.5 2.5 %slice-start = ((bf16[16,164737]{1,0:T(8,128)(2,1)}), bf16[16,163840]{1,0:T(8,128)(2,1)S(1)}, s32[]{:S(2)}) async-start(bf16[16,164737]{1,0:T(8,128)(2,1)} %tile.10), calls=%async_computation.2 | async-start | bytes 10485760 | tf_op jit(solution)/shard_map/slice | solution.py:30
  37.0 3.2 %copy-start = (s32[16,512]{1,0:T(8,128)S(1)}, s32[16,512]{1,0:T(8,128)}, u32[]{:S(2)}) copy-start(s32[16,512]{1,0:T(8,128)} %param.7) | copy-start | bytes 98308
  37.0 3.2 %copy-start.1 = (s32[16,512]{1,0:T(8,128)S(1)}, s32[16,512]{1,0:T(8,128)}, u32[]{:S(2)}) copy-start(s32[16,512]{1,0:T(8,128)} %param.6) | copy-start | bytes 98308
  65.5 16.7 %all-to-all-start.1 = ((f32[16,19,2,256]{3,2,1,0:T(2,128)}), f32[16,19,2,256]{3,2,1,0:T(2,128)S(1)}, u32[]{:S(2)}, u32[]{:S(2)}) async-start(f32[16,19,2,256]{3,2,1,0:T(2,128)} %reshape.238), calls=%async_computation.1 | async-start | bytes 1245184 | tf_op jit(solution)/shard_map/all_to_all | solution.py:70
  82.5 16.0 %collective-permute-start = (f32[16,2,256]{2,1,0:T(2,128)S(1)}, f32[16,2,256]{2,1,0:T(2,128)S(1)}, u32[]{:S(2)}, u32[]{:S(2)}) collective-permute-start(f32[16,2,256]{2,1,0:T(2,128)S(1)} %broadcast_select_fusion), channel_id=1, source_target_pairs={{0,256},{16,272},{32,288},{48,304},{64,320},{80,336},{96,352},{112... | collective-permute-start | bytes 98312 | tf_op jit(solution)/shard_map/ppermute | solution.py:82
  98.5 9.5 %collective-permute-start.1 = (f32[8,2,256]{2,1,0:T(2,128)S(1)}, f32[8,2,256]{2,1,0:T(2,128)S(1)}, u32[]{:S(2)}, u32[]{:S(2)}) collective-permute-start(f32[8,2,256]{2,1,0:T(2,128)S(1)} %broadcast_select_fusion.1), channel_id=1, source_target_pairs={{0,128},{16,144},{32,160},{48,176},{64,192},{80,208},{96,224},{112... | collective-permute-start | bytes 49160 | tf_op jit(solution)/shard_map/ppermute | solution.py:82
  108.1 6.4 %collective-permute-start.2 = (f32[4,2,256]{2,1,0:T(2,128)S(1)}, f32[4,2,256]{2,1,0:T(2,128)S(1)}, u32[]{:S(2)}, u32[]{:S(2)}) collective-permute-start(f32[4,2,256]{2,1,0:T(2,128)S(1)} %broadcast_select_fusion.2), channel_id=1, source_target_pairs={{0,64},{16,80},{32,96},{48,112},{64,0},{80,16},{96,32},{112,48},{1... | collective-permute-start | bytes 24584 | tf_op jit(solution)/shard_map/ppermute | solution.py:82
  114.5 5.5 %collective-permute-start.3 = (f32[2,2,256]{2,1,0:T(2,128)S(1)}, f32[2,2,256]{2,1,0:T(2,128)S(1)}, u32[]{:S(2)}, u32[]{:S(2)}) collective-permute-start(f32[2,2,256]{2,1,0:T(2,128)S(1)} %broadcast_select_fusion.3), channel_id=1, source_target_pairs={{0,32},{16,48},{32,0},{48,16},{64,96},{80,112},{96,64},{112,80},{1... | collective-permute-start | bytes 12296 | tf_op jit(solution)/shard_map/ppermute | solution.py:82
  120.0 7.0 %collective-permute-start.4 = (f32[1,2,256]{2,1,0:T(2,128)S(1)}, f32[1,2,256]{2,1,0:T(2,128)S(1)}, u32[]{:S(2)}, u32[]{:S(2)}) collective-permute-start(f32[1,2,256]{2,1,0:T(2,128)S(1)} %broadcast_select_fusion.4), channel_id=1, source_target_pairs={{0,16},{16,0},{32,48},{48,32},{64,80},{80,64},{96,112},{112,96},{1... | collective-permute-start | bytes 6152 | tf_op jit(solution)/shard_map/ppermute | solution.py:82

commit v12 on v7

--- a/solution.py
+++ b/solution.py
@@ -53,6 +53,7 @@
     low_span = 2 * (row_count - 1)
     reach = (low_span + 5 * (chan_count - 1)) * gathers // (2 * low_span + 1) + 2
     depth = -(-(reach - 1) // seg_devices) + 1
+    depth = -(-depth * OFFBINS // 8) * 8 // OFFBINS
     start = gather_id[0, 0]
     lanes = jnp.arange(seg_devices, dtype=jnp.int32)
     first = jnp.minimum((start - lanes + seg_devices - 1) // seg_devices, chan_devices - depth)
@@ -66,7 +67,7 @@
     both = jnp.dot(onehot, split, preferred_element_type=jnp.float32)
     total = both[:, :LAGS] + both[:, LAGS:]
     scale = 1.0 / math.sqrt(traces.shape[2] * traces.shape[1] * seg_devices)
-    stacked = (total * scale).reshape(seg_devices, depth, OFFBINS, LAGS)
+    stacked = (total * scale).reshape(seg_devices, depth * OFFBINS, LAGS)
     part = jnp.sum(lax.all_to_all(stacked, "seg", 0, 0, tiled=True), axis=0)
     own_first = first[lax.axis_index("seg")]
     dense = jnp.zeros((chan_devices, OFFBINS, LAGS), jnp.float32)

time: 105 us -> 105 us (level)
  local copies, waits for them, and re-layouts: 21.4 us -> 20.3 us
    reshape x1, local copies, waits for them, and re-layouts: 1.19 us -> 0.03 us  [shards(): part.reshape(depth, OFFBINS, LAGS)]
where the time goes in v12:
time: 105 us
  starting transfers between devices  25.7 us (24%)
  blocking collectives  21.3 us (20%)
  local copies, waits for them, and re-layouts  20.3 us (19%)
  waiting for transfers between devices  14.4 us (14%)
  matrix products  12.1 us (12%)
  other arithmetic  8.83 us (8%)
  between operations  2.07 us (2%)
    all_to_all x1, blocking collectives, shards(): pieces = lax.all_to_all(dense, 'chan', 0, 0, tiled=True)  21.3 us
    all_to_all x1, starting transfers between devices, shards(): lax.all_to_all(copies, 'chan', 0, 0, tiled=True).reshape(-1, flat.shape[1])  18.5 us
    another operation x2, local copies, waits for them, and re-layouts, toeplitz(): tiled = jnp.tile(ring, (1, lag_count + 1))[:, :lag_count * (width - 1)]  11.9 us
    all_to_all x1, waiting for transfers between devices, shards(): part = jnp.sum(lax.all_to_all(stacked, 'seg', 0, 0, tiled=True), axis=0)  8.71 us
    dot_general x1, matrix products, shards(): both = jnp.dot(onehot, split, preferred_element_type=jnp.float32)  7.79 us
    all_to_all x1, starting transfers between devices, shards(): part = jnp.sum(lax.all_to_all(stacked, 'seg', 0, 0, tiled=True), axis=0)  7.25 us
    all_to_all x1, waiting for transfers between devices, shards(): lax.all_to_all(copies, 'chan', 0, 0, tiled=True).reshape(-1, flat.shape[1])  5.72 us
    dot_general x1, matrix products, shards(): jnp.einsum('it,jkt->ijk', piece, kernel, preferred_element_type=jnp.float32)  4.26 us
  transfers between devices with their start and end apart: 2, of which 2 were waited for; matrix products, arithmetic and copies ran while one was open for 17% of the time, Pallas kernels for 0%

profile of v12, /device:TPU:1, one launch (start us, length us, event | category | flops | bytes accessed | tf_op | source)
XLA Modules:
  0.0 104.7 jit_solution(4148493440836143522)
XLA Ops:
  0.0 0.8 fusion.14
  0.8 0.7 convert_element_type.24
  1.5 0.8 fusion.15
  2.3 0.8 broadcast_in_dim.14
  3.1 18.5 %all-to-all-start = ((bf16[32,16,384]{2,1,0:T(8,128)(2,1)}), bf16[32,16,384]{2,1,0:T(8,128)(2,1)S(1)}, u32[]{:S(2)}, u32[]{:S(2)}) async-start(bf16[32,16,384]{2,1,0:T(8,128)(2,1)} %broadcast_in_dim.14), calls=%async_computation | async-start | bytes 786432 | tf_op jit(solution)/shard_map/all_to_all | solution.py:45
  21.6 1.2 %slice.21 = s32[1,1]{1,0:T(1,128)} slice(s32[16,512]{1,0:T(8,128)} %param.6), slice={[0:1], [0:1]} | slice | bytes 8 | tf_op jit(solution)/shard_map/slice | solution.py:57
  22.8 0.1 pad_maximum_fusion
  22.9 3.1 %tile.4 = bf16[16,257,641]{2,1,0:T(8,128)(2,1)} broadcast(bf16[16,641]{1,0:T(8,128)(2,1)S(1)} %pad_maximum_fusion), dimensions={0,2} | broadcast | bytes 5292096 | tf_op jit(solution)/shard_map/tile | solution.py:30
  26.0 8.7 %tile.10 = bf16[16,164737]{1,0:T(8,128)(2,1)} reshape(bf16[16,257,641]{2,1,0:T(8,128)(2,1)} %tile.4) | data formatting | bytes 10543168 | tf_op jit(solution)/shard_map/tile | solution.py:30
  34.7 2.5 %slice-done = bf16[16,163840]{1,0:T(8,128)(2,1)S(1)} async-done(((bf16[16,164737]{1,0:T(8,128)(2,1)}), bf16[16,163840]{1,0:T(8,128)(2,1)S(1)}, s32[]{:S(2)}) %slice-start) | async-done | bytes 5242904 | tf_op jit(solution)/shard_map/slice | solution.py:30
  37.2 3.2 %copy.9 = bf16[2,8,256,640]{3,2,1,0:T(8,128)(2,1)} copy(bf16[2,8,256,640]{3,1,2,0:T(8,128)(2,1)S(1)} %bitcast.21) | data formatting | bytes 10485760
  40.4 0.7 fusion.16
  41.1 0.1 iota_add_fusion
  41.3 0.1 add.115
  41.5 5.7 %all-to-all-done = bf16[32,16,384]{2,1,0:T(8,128)(2,1)S(1)} async-done(((bf16[32,16,384]{2,1,0:T(8,128)(2,1)}), bf16[32,16,384]{2,1,0:T(8,128)(2,1)S(1)}, u32[]{:S(2)}, u32[]{:S(2)}) %all-to-all-start) | async-done | bytes 393248 | tf_op jit(solution)/shard_map/all_to_all | solution.py:45
  47.2 4.3 %fusion.8 = f32[512,16,256]{2,0,1:T(8,128)S(1)} fusion(bf16[512,384,1]{1,0,2:T(8,128)(2,1)S(1)} %bitcast.22, bf16[16,256,640]{2,1,0:T(8,128)(2,1)} %bitcast.20), kind=kOutput, calls=%fused_computation.10 | convolution fusion | flops 1610612736 | bytes 11927552 | tf_op jit(solution)/shard_map/it,jkt->ijk/dot_general | solution.py:47
  51.5 4.0 %reduce-precision_convert_fusion = (bf16[8192,256]{1,0:T(8,128)(2,1)S(1)}, bf16[8192,256]{1,0:T(8,128)(2,1)}) fusion(f32[512,16,256]{2,0,1:T(8,128)S(1)} %fusion.8), kind=kLoop, calls=%fused_computation.3 | loop fusion | flops 8388608 | bytes 16777216 | tf_op jit(solution)/shard_map/convert
  55.5 7.8 %fusion = f32[640,512]{1,0:T(8,128)S(1)} fusion(s32[8192]{0:T(1024)S(1)} %bitcast.23, s32[640]{0:T(1024)S(1)} %add.115, bf16[8192,256]{1,0:T(8,128)(2,1)} %get-tuple-element.6, bf16[8192,256]{1,0:T(8,128)(2,1)S(1)} %get-tuple-element.5), kind=kOutput, calls=%fused_computation | convolution fusion | flops 5390729216 | bytes 9734656 | tf_op jit(solution)/shard_map/dot_general | solution.py:67
  63.3 0.9 fusion.10
  64.2 7.2 %all-to-all-start.1 = ((f32[16,40,256]{2,1,0:T(8,128)}), f32[16,40,256]{2,1,0:T(8,128)S(1)}, u32[]{:S(2)}, u32[]{:S(2)}) async-start(f32[16,40,256]{2,1,0:T(8,128)} %bitcast.7), calls=%async_computation.1 | async-start | bytes 1310720 | tf_op jit(solution)/shard_map/all_to_all | solution.py:71
  71.4 0.6 dynamic_slice.3
  74.0 8.7 %all-to-all-done.1 = f32[16,40,256]{2,1,0:T(8,128)S(1)} async-done(((f32[16,40,256]{2,1,0:T(8,128)}), f32[16,40,256]{2,1,0:T(8,128)S(1)}, u32[]{:S(2)}, u32[]{:S(2)}) %all-to-all-start.1) | async-done | bytes 655392 | tf_op jit(solution)/shard_map/all_to_all | solution.py:71
  82.8 21.3 %all_to_all.15 = f32[32,2,256]{2,1,0:T(2,128)S(1)} all-to-all(f32[32,2,256]{2,1,0:T(2,128)S(1)} %constant_dynamic-update-slice_fusion), channel_id=1, replica_groups=mesh['chan'=32,'seg'=16] {'chan'}, dimensions={0} | all-to-all | bytes 131072 | tf_op jit(solution)/shard_map/all_to_all | solution.py:75
  104.1 0.6 reduce_sum.29
  (19 shorter events, 0.3 us)
Async XLA Ops:
  3.1 44.2 %all-to-all-start = ((bf16[32,16,384]{2,1,0:T(8,128)(2,1)}), bf16[32,16,384]{2,1,0:T(8,128)(2,1)S(1)}, u32[]{:S(2)}, u32[]{:S(2)}) async-start(bf16[32,16,384]{2,1,0:T(8,128)(2,1)} %broadcast_in_dim.14), calls=%async_computation | async-start | bytes 786432 | tf_op jit(solution)/shard_map/all_to_all | solution.py:45
  34.7 2.5 %slice-start = ((bf16[16,164737]{1,0:T(8,128)(2,1)}), bf16[16,163840]{1,0:T(8,128)(2,1)S(1)}, s32[]{:S(2)}) async-start(bf16[16,164737]{1,0:T(8,128)(2,1)} %tile.10), calls=%async_computation.3 | async-start | bytes 10485760 | tf_op jit(solution)/shard_map/slice | solution.py:30
  37.2 4.2 %copy-start = (s32[16,512]{1,0:T(8,128)S(1)}, s32[16,512]{1,0:T(8,128)}, u32[]{:S(2)}) copy-start(s32[16,512]{1,0:T(8,128)} %param.7) | copy-start | bytes 98308
  37.2 4.2 %copy-start.1 = (s32[16,512]{1,0:T(8,128)S(1)}, s32[16,512]{1,0:T(8,128)}, u32[]{:S(2)}) copy-start(s32[16,512]{1,0:T(8,128)} %param.6) | copy-start | bytes 98308
  64.2 18.5 %all-to-all-start.1 = ((f32[16,40,256]{2,1,0:T(8,128)}), f32[16,40,256]{2,1,0:T(8,128)S(1)}, u32[]{:S(2)}, u32[]{:S(2)}) async-start(f32[16,40,256]{2,1,0:T(8,128)} %bitcast.7), calls=%async_computation.1 | async-start | bytes 1310720 | tf_op jit(solution)/shard_map/all_to_all | solution.py:71

commit v13 on v10

--- a/solution.py
+++ b/solution.py
@@ -44,11 +44,23 @@
     copies = jnp.broadcast_to(flat[None], (chan_devices,) + flat.shape)
     piece = lax.all_to_all(copies, "chan", 0, 0, tiled=True).reshape(-1, flat.shape[1])
     row_count = piece.shape[0]
-    product = jnp.einsum("it,jkt->ijk", piece, kernel, preferred_element_type=jnp.float32)
-    product = jnp.transpose(product, (1, 0, 2)).reshape(row_count * chan_count, LAGS)
+    sample_count = piece.shape[1]
+    me = lax.axis_index("chan")
+    half = chan_devices // 2
+    take = (half + 1) * chan_count
+    near = lax.dynamic_slice(jnp.concatenate([piece, piece], axis=0), (me * chan_count, 0), (take, sample_count))
+    block_of = jnp.arange(half + 1, dtype=jnp.int32)
+    weight = jnp.where(block_of == 0, 0.5, 1.0)
+    weight = jnp.where((block_of == half) & (me >= half), 0.0, weight)
+    weight = jnp.repeat(weight, chan_count)
+    product = jnp.einsum("it,jkt->ijk", near, kernel, preferred_element_type=jnp.float32)
+    product = jnp.transpose(product, (1, 0, 2)).reshape(take * chan_count, LAGS)
+    late = jnp.concatenate([jnp.zeros((chan_count, LAGS // 2), flat.dtype), flat[:, : sample_count - LAGS // 2]], axis=1)
+    edge = jnp.einsum("it,jt->ji", near, late, preferred_element_type=jnp.float32).reshape(-1, 1)
     labels = gather_id * OFFBINS + offset_bin
-    partner = jnp.arange(row_count, dtype=jnp.int32)[None, :]
-    labels = jnp.where(partner == own_rows.reshape(-1, 1), -1, labels).reshape(-1)
+    labels = lax.dynamic_slice(jnp.concatenate([labels, labels], axis=1), (0, me * chan_count), (chan_count, take))
+    partner = jnp.arange(take, dtype=jnp.int32)[None, :]
+    labels = jnp.where(partner == jnp.arange(chan_count, dtype=jnp.int32)[:, None], -1, labels).reshape(-1)
     gathers = chan_devices * seg_devices
     low_span = 2 * (row_count - 1)
     reach = (low_span + 5 * (chan_count - 1)) * gathers // (2 * low_span + 1) + 2
@@ -59,12 +71,18 @@
     first = jnp.maximum(first, 0)
     window = (first[:, None] + jnp.arange(depth, dtype=jnp.int32)[None, :]) * seg_devices + lanes[:, None]
     wanted = (window[:, :, None] * OFFBINS + jnp.arange(OFFBINS, dtype=jnp.int32)).reshape(-1)
-    onehot = lax.optimization_barrier((wanted[:, None] == labels[None, :]).astype(jnp.bfloat16))
-    high = lax.reduce_precision(product, exponent_bits=8, mantissa_bits=7)
-    low = product - high
-    split = jnp.concatenate([high, low], axis=1).astype(jnp.bfloat16)
+    hit = wanted[:, None] == labels[None, :]
+    onehot = jnp.where(hit, jnp.tile(weight, chan_count)[None, :], 0.0).astype(jnp.bfloat16)
+    extended = jnp.concatenate([product, edge], axis=1)
+    high = lax.reduce_precision(extended, exponent_bits=8, mantissa_bits=7)
+    low = extended - high
+    split = jnp.concatenate([high[:, :LAGS], low[:, :LAGS]], axis=1).astype(jnp.bfloat16)
     both = jnp.dot(onehot, split, preferred_element_type=jnp.float32)
-    total = both[:, :LAGS] + both[:, LAGS:]
+    ends = jnp.concatenate([high[:, LAGS:], low[:, LAGS:]], axis=1).astype(jnp.bfloat16)
+    tail = jnp.dot(onehot, ends, preferred_element_type=jnp.float32)
+    direct = both[:, :LAGS] + both[:, LAGS:]
+    mirror = jnp.concatenate([tail[:, :1] + tail[:, 1:], jnp.flip(direct[:, 1:], axis=1)], axis=1)
+    total = direct + mirror
     scale = 1.0 / math.sqrt(traces.shape[2] * traces.shape[1] * seg_devices)
     stacked = (total * scale).reshape(seg_devices, depth, OFFBINS, LAGS)
     part = jnp.sum(lax.all_to_all(stacked, "seg", 0, 0, tiled=True), axis=0)

time: 114 us -> 111 us (0.974)
  local copies, waits for them, and re-layouts: 21.5 us -> 29.2 us
  other arithmetic: 14.5 us -> 7.68 us
  blocking collectives: 27.8 us -> 21 us
  waiting for transfers between devices: 8.37 us -> 14.4 us
  matrix products: 13.9 us -> 9.99 us
    all_to_all x1, blocking collectives: 27.8 us -> 21 us  [shards(): pieces = lax.all_to_all(dense, 'chan', 0, 0, tiled=True)]
    dot_general x1, matrix products: 9.65 us -> 2.94 us  [shards(): both = jnp.dot(onehot, split, preferred_element_type=jnp.float32)]
    convert_element_type x1 -> x0, other arithmetic: 6.45 us -> none  [shards(): (wanted[:, None] == labels[None, :]).astype(jnp.bfloat16)]
    all_to_all x1, waiting for transfers between devices: 0.01 us -> 6 us  [shards(): lax.all_to_all(copies, 'chan', 0, 0, tiled=True).reshape(-1, flat.shape[1])]
    reshape x0 -> x2, local copies, waits for them, and re-layouts: none -> 5.88 us  [the longest x1 5.72 us: shards(): product = jnp.transpose(product, (1, 0, 2)).reshape(take * chan_count, LAGS)]
    dot_general x1 -> x3, matrix products: 4.26 us -> 7.05 us  [the longest x1 5.36 us: shards(): jnp.einsum('it,jkt->ijk', near, kernel, preferred_element_type=jnp.float32)]
    unnamed x6 -> x9, local copies, waits for them, and re-layouts: 3.23 us -> 4.81 us
    another operation x1, other arithmetic: 3.92 us -> 2.77 us
  transfers between devices with their start and end apart: 2 -> 2, of which waited for: 1 -> 2; matrix products, arithmetic and copies ran while one was open for 22% -> 16% of each run, Pallas kernels for 0% -> 0%
where the time goes in v13:
time: 111 us; the launch traced here: 110 us
  local copies, waits for them, and re-layouts  29.2 us (26%)
  starting transfers between devices  25.7 us (23%)
  blocking collectives  21 us (19%)
  waiting for transfers between devices  14.4 us (13%)
  matrix products  9.99 us (9%)
  other arithmetic  7.68 us (7%)
  between operations  2.17 us (2%)
    all_to_all x1, blocking collectives, shards(): pieces = lax.all_to_all(dense, 'chan', 0, 0, tiled=True)  21 us
    all_to_all x1, starting transfers between devices, shards(): lax.all_to_all(copies, 'chan', 0, 0, tiled=True).reshape(-1, flat.shape[1])  18.5 us
    another operation x2, local copies, waits for them, and re-layouts, toeplitz(): tiled = jnp.tile(ring, (1, lag_count + 1))[:, :lag_count * (width - 1)]  11.9 us
    all_to_all x1, waiting for transfers between devices, shards(): part = jnp.sum(lax.all_to_all(stacked, 'seg', 0, 0, tiled=True), axis=0)  8.36 us
    all_to_all x1, starting transfers between devices, shards(): part = jnp.sum(lax.all_to_all(stacked, 'seg', 0, 0, tiled=True), axis=0)  7.25 us
    all_to_all x1, waiting for transfers between devices, shards(): lax.all_to_all(copies, 'chan', 0, 0, tiled=True).reshape(-1, flat.shape[1])  6 us
    reshape x1, local copies, waits for them, and re-layouts, shards(): product = jnp.transpose(product, (1, 0, 2)).reshape(take * chan_count, LAGS)  5.72 us
    dot_general x1, matrix products, shards(): jnp.einsum('it,jkt->ijk', near, kernel, preferred_element_type=jnp.float32)  5.36 us
  transfers between devices with their start and end apart: 2, of which 2 were waited for; matrix products, arithmetic and copies ran while one was open for 16% of the time, Pallas kernels for 0%

profile of v13, /device:TPU:1, one launch (start us, length us, event | category | flops | bytes accessed | tf_op | source)
XLA Modules:
  0.0 110.2 jit_solution(314555066936495206)
XLA Ops:
  0.0 0.8 fusion.22
  0.8 0.7 convert_element_type.28
  1.5 0.8 fusion.28
  2.3 0.8 broadcast_in_dim.69
  3.1 18.5 %all-to-all-start = ((bf16[32,16,384]{2,1,0:T(8,128)(2,1)}), bf16[32,16,384]{2,1,0:T(8,128)(2,1)S(1)}, u32[]{:S(2)}, u32[]{:S(2)}) async-start(bf16[32,16,384]{2,1,0:T(8,128)(2,1)} %broadcast_in_dim.69), calls=%async_computation | async-start | bytes 786432 | tf_op jit(solution)/shard_map/all_to_all | solution.py:45
  21.7 3.1 %tile.18 = bf16[16,257,641]{2,1,0:T(8,128)(2,1)} broadcast(bf16[16,641]{1,0:T(8,128)(2,1)S(1)} %pad_maximum_fusion.1), dimensions={0,2} | broadcast | bytes 5292096 | tf_op jit(solution)/shard_map/tile | solution.py:30
  24.9 8.7 %tile.19 = bf16[16,164737]{1,0:T(8,128)(2,1)} reshape(bf16[16,257,641]{2,1,0:T(8,128)(2,1)} %tile.18) | data formatting | bytes 10543168 | tf_op jit(solution)/shard_map/tile | solution.py:30
  33.6 2.5 %slice-done = bf16[16,163840]{1,0:T(8,128)(2,1)S(1)} async-done(((bf16[16,164737]{1,0:T(8,128)(2,1)}), bf16[16,163840]{1,0:T(8,128)(2,1)S(1)}, s32[]{:S(2)}) %slice-start) | async-done | bytes 5242904 | tf_op jit(solution)/shard_map/slice | solution.py:30
  36.1 3.2 %copy.23 = bf16[2,8,256,640]{3,2,1,0:T(8,128)(2,1)} copy(bf16[2,8,256,640]{3,1,2,0:T(8,128)(2,1)S(1)} %bitcast.16) | data formatting | bytes 10485760
  39.2 0.5 slice.49
  40.2 0.7 fusion.31
  41.2 6.0 %all-to-all-done = bf16[32,16,384]{2,1,0:T(8,128)(2,1)S(1)} async-done(((bf16[32,16,384]{2,1,0:T(8,128)(2,1)}), bf16[32,16,384]{2,1,0:T(8,128)(2,1)S(1)}, u32[]{:S(2)}, u32[]{:S(2)}) %all-to-all-start) | async-done | bytes 393248 | tf_op jit(solution)/shard_map/all_to_all | solution.py:45
  47.6 5.4 %fusion.14 = f32[272,16,256]{2,0,1:T(8,128)} fusion(bf16[16,256,640]{2,1,0:T(8,128)(2,1)} %bitcast.18, bf16[272,384]{1,0:T(8,128)(2,1)S(1)} %fusion.17), kind=kOutput, calls=%fused_computation.18 | convolution fusion | flops 855638016 | bytes 7811072 | tf_op jit(solution)/shard_map/it,jkt->ijk/dot_general | solution.py:56
  52.9 5.7 %copy.17 = f32[4352,256]{0,1:T(8,128)} copy(f32[4352,256]{1,0:T(8,128)} %bitcast.17) | data formatting | bytes 8912896 | tf_op jit(solution)/shard_map/reshape | solution.py:57
  59.0 2.8 %reduce-precision_convert_fusion = (bf16[4352,257]{0,1:T(8,128)(2,1)S(1)}, bf16[4352,257]{0,1:T(8,128)(2,1)S(1)}) fusion(f32[4352,1]{0,1:T(1,128)S(1)} %reshape.211, f32[4352,256]{0,1:T(8,128)} %copy.17), kind=kLoop, calls=%fused_computation.4 | loop fusion | flops 5592320 | bytes 8947712 | tf_op jit(solution)/shard_map/convert.7
  62.1 1.6 %fusion = f32[608,2]{1,0:T(8,128)S(1)} fusion(bf16[4352]{0:T(1024)(128)(2,1)S(1)} %broadcast_in_dim.66, s32[4352]{0:T(1024)S(1)} %eq.38, s32[608]{0:T(1024)S(1)} %add.115, bf16[4352,1]{0,1:T(2,128)(2,1)S(1)} %slice.74, bf16[4352,1]{0,1:T(2,128)(2,1)S(1)} %slice.73), kind=kOutput, calls=%fused_computation.1 | convolution fusion | flops 15910912 | bytes 50816 | tf_op jit(solution)/shard_map/dot_general | solution.py:82
  63.8 2.9 %fusion.1 = f32[608,512]{1,0:T(8,128)S(1)} fusion(bf16[4352]{0:T(1024)(128)(2,1)S(1)} %broadcast_in_dim.66, s32[4352]{0:T(1024)S(1)} %eq.38, s32[608]{0:T(1024)S(1)} %add.115, bf16[4352,256]{0,1:T(8,128)(2,1)S(1)} %slice.70, bf16[4352,256]{0,1:T(8,128)(2,1)S(1)} %slice.69), kind=kOutput, calls=%fused_computation.2 | convolution fusion | flops 2723725312 | bytes 5730176 | tf_op jit(solution)/shard_map/dot_general | solution.py:80
  67.1 1.4 %reverse = f32[608,256]{1,0:T(8,128)S(1)} reverse(f32[608,256]{1,0:T(8,128)S(1)} %bitcast.19), dimensions={1} | reverse | bytes 1245184
  69.0 1.2 %reshape.212 = f32[16,19,2,256]{3,2,1,0:T(2,128)} reshape(f32[608,256]{1,0:T(8,128)S(1)} %fusion.16) | data formatting | bytes 1245184 | tf_op jit(solution)/shard_map/reshape | solution.py:87
  70.1 7.2 %all-to-all-start.1 = ((f32[16,19,2,256]{3,2,1,0:T(2,128)}), f32[16,19,2,256]{3,2,1,0:T(2,128)S(1)}, u32[]{:S(2)}, u32[]{:S(2)}) async-start(f32[16,19,2,256]{3,2,1,0:T(2,128)} %reshape.212), calls=%async_computation.1 | async-start | bytes 1245184 | tf_op jit(solution)/shard_map/all_to_all | solution.py:88
  77.4 0.6 dynamic_slice.11
  79.9 8.4 %all-to-all-done.1 = f32[16,19,2,256]{3,2,1,0:T(2,128)S(1)} async-done(((f32[16,19,2,256]{3,2,1,0:T(2,128)}), f32[16,19,2,256]{3,2,1,0:T(2,128)S(1)}, u32[]{:S(2)}, u32[]{:S(2)}) %all-to-all-start.1) | async-done | bytes 622624 | tf_op jit(solution)/shard_map/all_to_all | solution.py:88
  88.5 21.0 %all_to_all.15 = f32[32,2,256]{2,1,0:T(2,128)S(1)} all-to-all(f32[32,2,256]{2,1,0:T(2,128)S(1)} %constant_dynamic-update-slice_fusion), channel_id=1, replica_groups=mesh['chan'=32,'seg'=16] {'chan'}, dimensions={0} | all-to-all | bytes 131072 | tf_op jit(solution)/shard_map/all_to_all | solution.py:92
  109.5 0.6 reduce_sum.29
  (42 shorter events, 3.0 us)
Async XLA Ops:
  2.3 31.3 %copy-start = (bf16[16,384]{1,0:T(8,128)(2,1)}, bf16[16,384]{1,0:T(8,128)(2,1)S(1)}, u32[]{:S(2)}) copy-start(bf16[16,384]{1,0:T(8,128)(2,1)S(1)} %fusion.28) | copy-start | bytes 36868
  3.1 44.2 %all-to-all-start = ((bf16[32,16,384]{2,1,0:T(8,128)(2,1)}), bf16[32,16,384]{2,1,0:T(8,128)(2,1)S(1)}, u32[]{:S(2)}, u32[]{:S(2)}) async-start(bf16[32,16,384]{2,1,0:T(8,128)(2,1)} %broadcast_in_dim.69), calls=%async_computation | async-start | bytes 786432 | tf_op jit(solution)/shard_map/all_to_all | solution.py:45
  33.6 2.5 %slice-start = ((bf16[16,164737]{1,0:T(8,128)(2,1)}), bf16[16,163840]{1,0:T(8,128)(2,1)S(1)}, s32[]{:S(2)}) async-start(bf16[16,164737]{1,0:T(8,128)(2,1)} %tile.19), calls=%async_computation.3 | async-start | bytes 10485760 | tf_op jit(solution)/shard_map/slice | solution.py:30
  36.1 3.2 %copy-start.2 = (s32[16,512]{1,0:T(8,128)S(1)}, s32[16,512]{1,0:T(8,128)}, u32[]{:S(2)}) copy-start(s32[16,512]{1,0:T(8,128)} %param.6) | copy-start | bytes 98308
  36.1 3.7 %copy-start.1 = (s32[16,512]{1,0:T(8,128)S(1)}, s32[16,512]{1,0:T(8,128)}, u32[]{:S(2)}) copy-start(s32[16,512]{1,0:T(8,128)} %param.7) | copy-start | bytes 98308
  52.9 5.7 %slice-start.1 = ((bf16[16,384]{1,0:T(8,128)(2,1)}), bf16[16,256]{1,0:T(8,128)(2,1)S(1)}, s32[]{:S(2)}) async-start(bf16[16,384]{1,0:T(8,128)(2,1)} %copy-done), calls=%async_computation.4 | async-start | bytes 16384 | tf_op jit(solution)/shard_map/slice | solution.py:58
  70.1 18.1 %all-to-all-start.1 = ((f32[16,19,2,256]{3,2,1,0:T(2,128)}), f32[16,19,2,256]{3,2,1,0:T(2,128)S(1)}, u32[]{:S(2)}, u32[]{:S(2)}) async-start(f32[16,19,2,256]{3,2,1,0:T(2,128)} %reshape.212), calls=%async_computation.1 | async-start | bytes 1245184 | tf_op jit(solution)/shard_map/all_to_all | solution.py:88

commit v14 on v13

--- a/solution.py
+++ b/solution.py
@@ -73,12 +73,12 @@
     wanted = (window[:, :, None] * OFFBINS + jnp.arange(OFFBINS, dtype=jnp.int32)).reshape(-1)
     hit = wanted[:, None] == labels[None, :]
     onehot = jnp.where(hit, jnp.tile(weight, chan_count)[None, :], 0.0).astype(jnp.bfloat16)
-    extended = jnp.concatenate([product, edge], axis=1)
-    high = lax.reduce_precision(extended, exponent_bits=8, mantissa_bits=7)
-    low = extended - high
-    split = jnp.concatenate([high[:, :LAGS], low[:, :LAGS]], axis=1).astype(jnp.bfloat16)
+    high = lax.reduce_precision(product, exponent_bits=8, mantissa_bits=7)
+    low = product - high
+    split = jnp.concatenate([high, low], axis=1).astype(jnp.bfloat16)
     both = jnp.dot(onehot, split, preferred_element_type=jnp.float32)
-    ends = jnp.concatenate([high[:, LAGS:], low[:, LAGS:]], axis=1).astype(jnp.bfloat16)
+    edge_high = lax.reduce_precision(edge, exponent_bits=8, mantissa_bits=7)
+    ends = jnp.concatenate([edge_high, edge - edge_high], axis=1).astype(jnp.bfloat16)
     tail = jnp.dot(onehot, ends, preferred_element_type=jnp.float32)
     direct = both[:, :LAGS] + both[:, LAGS:]
     mirror = jnp.concatenate([tail[:, :1] + tail[:, 1:], jnp.flip(direct[:, 1:], axis=1)], axis=1)

time: 111 us -> 102 us (0.919)
  local copies, waits for them, and re-layouts: 29.2 us -> 23.9 us
  matrix products: 9.99 us -> 7.86 us
  waiting for transfers between devices: 14.4 us -> 12.9 us
  blocking collectives: 21 us -> 22.4 us
    reshape x1 -> x0, local copies, waits for them, and re-layouts: 5.72 us -> none  [shards(): product = jnp.transpose(product, (1, 0, 2)).reshape(take * chan_count, LAGS)]
    dot_general x1, matrix products: 5.36 us -> 3.24 us  [shards(): jnp.einsum('it,jkt->ijk', near, kernel, preferred_element_type=jnp.float32)]
    another operation x1 -> x2, other arithmetic: 2.77 us -> 1 us
    all_to_all x1, waiting for transfers between devices: 6 us -> 4.56 us  [shards(): lax.all_to_all(copies, 'chan', 0, 0, tiled=True).reshape(-1, flat.shape[1])]
    all_to_all x1, blocking collectives: 21 us -> 22.4 us  [shards(): pieces = lax.all_to_all(dense, 'chan', 0, 0, tiled=True)]
    unnamed x9 -> x5, local copies, waits for them, and re-layouts: 4.81 us -> 4.8 us
  transfers between devices with their start and end apart: 2 -> 2, of which waited for: 2 -> 2; matrix products, arithmetic and copies ran while one was open for 16% -> 19% of each run, Pallas kernels for 0% -> 0%
where the time goes in v14:
time: 102 us
  starting transfers between devices  25.7 us (25%)
  local copies, waits for them, and re-layouts  23.9 us (23%)
  blocking collectives  22.4 us (22%)
  waiting for transfers between devices  12.9 us (13%)
  matrix products  7.86 us (8%)
  other arithmetic  6.67 us (7%)
  between operations  2.16 us (2%)
    all_to_all x1, blocking collectives, shards(): pieces = lax.all_to_all(dense, 'chan', 0, 0, tiled=True)  22.4 us
    all_to_all x1, starting transfers between devices, shards(): lax.all_to_all(copies, 'chan', 0, 0, tiled=True).reshape(-1, flat.shape[1])  18.5 us
    another operation x2, local copies, waits for them, and re-layouts, toeplitz(): tiled = jnp.tile(ring, (1, lag_count + 1))[:, :lag_count * (width - 1)]  11.9 us
    all_to_all x1, waiting for transfers between devices, shards(): part = jnp.sum(lax.all_to_all(stacked, 'seg', 0, 0, tiled=True), axis=0)  8.36 us
    all_to_all x1, starting transfers between devices, shards(): part = jnp.sum(lax.all_to_all(stacked, 'seg', 0, 0, tiled=True), axis=0)  7.25 us
    unnamed x5, local copies, waits for them, and re-layouts  4.8 us
    all_to_all x1, waiting for transfers between devices, shards(): lax.all_to_all(copies, 'chan', 0, 0, tiled=True).reshape(-1, flat.shape[1])  4.56 us
    dot_general x1, matrix products, shards(): jnp.einsum('it,jkt->ijk', near, kernel, preferred_element_type=jnp.float32)  3.24 us
  transfers between devices with their start and end apart: 2, of which 2 were waited for; matrix products, arithmetic and copies ran while one was open for 19% of the time, Pallas kernels for 0%

profile of v14, /device:TPU:1, one launch (start us, length us, event | category | flops | bytes accessed | tf_op | source)
XLA Modules:
  0.0 101.6 jit_solution(16372790261286924297)
XLA Ops:
  0.0 0.8 fusion.22
  0.8 0.7 convert_element_type.28
  1.5 0.8 fusion.29
  2.3 0.8 broadcast_in_dim.69
  3.1 18.5 %all-to-all-start = ((bf16[32,16,384]{2,1,0:T(8,128)(2,1)}), bf16[32,16,384]{2,1,0:T(8,128)(2,1)S(1)}, u32[]{:S(2)}, u32[]{:S(2)}) async-start(bf16[32,16,384]{2,1,0:T(8,128)(2,1)} %broadcast_in_dim.69), calls=%async_computation | async-start | bytes 786432 | tf_op jit(solution)/shard_map/all_to_all | solution.py:45
  21.9 1.2 %slice.33 = s32[1,1]{1,0:T(1,128)} slice(s32[16,512]{1,0:T(8,128)} %param.6), slice={[0:1], [0:1]} | slice | bytes 8 | tf_op jit(solution)/shard_map/slice | solution.py:68
  23.1 0.8 multiply_add_fusion
  24.1 0.7 fusion.32
  25.2 3.1 %tile.18 = bf16[16,257,641]{2,1,0:T(8,128)(2,1)} broadcast(bf16[16,641]{1,0:T(8,128)(2,1)S(1)} %pad_maximum_fusion), dimensions={0,2} | broadcast | bytes 5292096 | tf_op jit(solution)/shard_map/tile | solution.py:30
  28.3 8.7 %tile.19 = bf16[16,164737]{1,0:T(8,128)(2,1)} reshape(bf16[16,257,641]{2,1,0:T(8,128)(2,1)} %tile.18) | data formatting | bytes 10543168 | tf_op jit(solution)/shard_map/tile | solution.py:30
  37.1 2.5 %slice-done = bf16[16,163840]{1,0:T(8,128)(2,1)S(1)} async-done(((bf16[16,164737]{1,0:T(8,128)(2,1)}), bf16[16,163840]{1,0:T(8,128)(2,1)S(1)}, s32[]{:S(2)}) %slice-start) | async-done | bytes 5242904 | tf_op jit(solution)/shard_map/slice | solution.py:30
  39.5 3.1 %copy.16 = bf16[2,8,256,640]{3,2,1,0:T(8,128)(2,1)} copy(bf16[2,8,256,640]{3,1,2,0:T(8,128)(2,1)S(1)} %bitcast.18) | data formatting | bytes 10485760
  42.7 4.6 %all-to-all-done = bf16[32,16,384]{2,1,0:T(8,128)(2,1)S(1)} async-done(((bf16[32,16,384]{2,1,0:T(8,128)(2,1)}), bf16[32,16,384]{2,1,0:T(8,128)(2,1)S(1)}, u32[]{:S(2)}, u32[]{:S(2)}) %all-to-all-start) | async-done | bytes 393248 | tf_op jit(solution)/shard_map/all_to_all | solution.py:45
  47.6 3.2 %fusion.14 = f32[272,16,256]{2,0,1:T(8,128)S(1)} fusion(bf16[16,256,640]{2,1,0:T(8,128)(2,1)} %bitcast.19, bf16[272,384]{1,0:T(8,128)(2,1)S(1)} %fusion.17), kind=kOutput, calls=%fused_computation.17 | convolution fusion | flops 855638016 | bytes 7811072 | tf_op jit(solution)/shard_map/it,jkt->ijk/dot_general | solution.py:56
  50.8 1.0 reduce-precision_convert_fusion
  51.8 2.9 %fusion.1 = f32[608,512]{1,0:T(8,128)S(1)} fusion(bf16[4352]{0:T(1024)(128)(2,1)S(1)} %broadcast_in_dim.66, s32[4352]{0:T(1024)S(1)} %eq.38, s32[608]{0:T(1024)S(1)} %add.115, bf16[4352,256]{1,0:T(8,128)(2,1)S(1)} %get-tuple-element.6, bf16[4352,256]{1,0:T(8,128)(2,1)S(1)} %get-tuple-element.5), kind=kOutput, calls=%fused_computation.2 | convolution fusion | flops 2723725312 | bytes 5730176 | tf_op jit(solution)/shard_map/dot_general | solution.py:79
  55.1 1.4 %reverse = f32[608,256]{1,0:T(8,128)S(1)} reverse(f32[608,256]{1,0:T(8,128)S(1)} %bitcast.20), dimensions={1} | reverse | bytes 1245184
  57.1 1.6 %fusion = f32[608,2]{1,0:T(8,128)S(1)} fusion(bf16[4352]{0:T(1024)(128)(2,1)S(1)} %broadcast_in_dim.66, s32[4352]{0:T(1024)S(1)} %eq.38, s32[608]{0:T(1024)S(1)} %add.115, bf16[4352,1]{0,1:T(2,128)(2,1)S(1)} %get-tuple-element.8, bf16[4352,1]{0,1:T(2,128)(2,1)S(1)} %get-tuple-element.7), kind=kOutput, calls=%fused_computation.1 | convolution fusion | flops 15910912 | bytes 50816 | tf_op jit(solution)/shard_map/dot_general | solution.py:82
  59.0 1.2 %reshape.240 = f32[16,19,2,256]{3,2,1,0:T(2,128)} reshape(f32[608,256]{1,0:T(8,128)S(1)} %fusion.16) | data formatting | bytes 1245184 | tf_op jit(solution)/shard_map/reshape | solution.py:87
  60.2 7.2 %all-to-all-start.1 = ((f32[16,19,2,256]{3,2,1,0:T(2,128)}), f32[16,19,2,256]{3,2,1,0:T(2,128)S(1)}, u32[]{:S(2)}, u32[]{:S(2)}) async-start(f32[16,19,2,256]{3,2,1,0:T(2,128)} %reshape.240), calls=%async_computation.1 | async-start | bytes 1245184 | tf_op jit(solution)/shard_map/all_to_all | solution.py:88
  67.5 0.6 dynamic_slice.11
  70.0 8.4 %all-to-all-done.1 = f32[16,19,2,256]{3,2,1,0:T(2,128)S(1)} async-done(((f32[16,19,2,256]{3,2,1,0:T(2,128)}), f32[16,19,2,256]{3,2,1,0:T(2,128)S(1)}, u32[]{:S(2)}, u32[]{:S(2)}) %all-to-all-start.1) | async-done | bytes 622624 | tf_op jit(solution)/shard_map/all_to_all | solution.py:88
  78.6 22.4 %all_to_all.15 = f32[32,2,256]{2,1,0:T(2,128)S(1)} all-to-all(f32[32,2,256]{2,1,0:T(2,128)S(1)} %constant_dynamic-update-slice_fusion), channel_id=1, replica_groups=mesh['chan'=32,'seg'=16] {'chan'}, dimensions={0} | all-to-all | bytes 131072 | tf_op jit(solution)/shard_map/all_to_all | solution.py:92
  101.0 0.6 reduce_sum.29
  (34 shorter events, 2.6 us)
Async XLA Ops:
  2.3 34.8 %copy-start = (bf16[16,384]{1,0:T(8,128)(2,1)}, bf16[16,384]{1,0:T(8,128)(2,1)S(1)}, u32[]{:S(2)}) copy-start(bf16[16,384]{1,0:T(8,128)(2,1)S(1)} %fusion.29) | copy-start | bytes 36868
  3.1 44.2 %all-to-all-start = ((bf16[32,16,384]{2,1,0:T(8,128)(2,1)}), bf16[32,16,384]{2,1,0:T(8,128)(2,1)S(1)}, u32[]{:S(2)}, u32[]{:S(2)}) async-start(bf16[32,16,384]{2,1,0:T(8,128)(2,1)} %broadcast_in_dim.69), calls=%async_computation | async-start | bytes 786432 | tf_op jit(solution)/shard_map/all_to_all | solution.py:45
  37.1 2.5 %slice-start = ((bf16[16,164737]{1,0:T(8,128)(2,1)}), bf16[16,163840]{1,0:T(8,128)(2,1)S(1)}, s32[]{:S(2)}) async-start(bf16[16,164737]{1,0:T(8,128)(2,1)} %tile.19), calls=%async_computation.3 | async-start | bytes 10485760 | tf_op jit(solution)/shard_map/slice | solution.py:30
  54.7 2.0 %slice-start.1 = ((bf16[16,384]{1,0:T(8,128)(2,1)}), bf16[16,256]{1,0:T(8,128)(2,1)S(1)}, s32[]{:S(2)}) async-start(bf16[16,384]{1,0:T(8,128)(2,1)} %copy-done), calls=%async_computation.4 | async-start | bytes 16384 | tf_op jit(solution)/shard_map/slice | solution.py:58
  60.2 18.1 %all-to-all-start.1 = ((f32[16,19,2,256]{3,2,1,0:T(2,128)}), f32[16,19,2,256]{3,2,1,0:T(2,128)S(1)}, u32[]{:S(2)}, u32[]{:S(2)}) async-start(f32[16,19,2,256]{3,2,1,0:T(2,128)} %reshape.240), calls=%async_computation.1 | async-start | bytes 1245184 | tf_op jit(solution)/shard_map/all_to_all | solution.py:88

commit v15 on v14

--- a/solution.py
+++ b/solution.py
@@ -65,6 +65,7 @@
     low_span = 2 * (row_count - 1)
     reach = (low_span + 5 * (chan_count - 1)) * gathers // (2 * low_span + 1) + 2
     depth = -(-(reach - 1) // seg_devices) + 1
+    depth = -(-depth * OFFBINS // 8) * 8 // OFFBINS
     start = gather_id[0, 0]
     lanes = jnp.arange(seg_devices, dtype=jnp.int32)
     first = jnp.minimum((start - lanes + seg_devices - 1) // seg_devices, chan_devices - depth)
@@ -84,7 +85,7 @@
     mirror = jnp.concatenate([tail[:, :1] + tail[:, 1:], jnp.flip(direct[:, 1:], axis=1)], axis=1)
     total = direct + mirror
     scale = 1.0 / math.sqrt(traces.shape[2] * traces.shape[1] * seg_devices)
-    stacked = (total * scale).reshape(seg_devices, depth, OFFBINS, LAGS)
+    stacked = (total * scale).reshape(seg_devices, depth * OFFBINS, LAGS)
     part = jnp.sum(lax.all_to_all(stacked, "seg", 0, 0, tiled=True), axis=0)
     own_first = first[lax.axis_index("seg")]
     dense = jnp.zeros((chan_devices, OFFBINS, LAGS), jnp.float32)

time: 102 us -> 102 us (level)
  local copies, waits for them, and re-layouts: 23.9 us -> 22.2 us
    reshape x1, local copies, waits for them, and re-layouts: 1.2 us -> 0.03 us  [shards(): part.reshape(depth, OFFBINS, LAGS)]
where the time goes in v15:
time: 102 us; the launch traced here: 101 us
  starting transfers between devices  25.7 us (25%)
  blocking collectives  22.4 us (22%)
  local copies, waits for them, and re-layouts  22.2 us (22%)
  waiting for transfers between devices  13.3 us (13%)
  matrix products  8.07 us (8%)
  other arithmetic  7.4 us (7%)
  between operations  2.16 us (2%)
    all_to_all x1, blocking collectives, shards(): pieces = lax.all_to_all(dense, 'chan', 0, 0, tiled=True)  22.4 us
    all_to_all x1, starting transfers between devices, shards(): lax.all_to_all(copies, 'chan', 0, 0, tiled=True).reshape(-1, flat.shape[1])  18.5 us
    another operation x2, local copies, waits for them, and re-layouts, toeplitz(): tiled = jnp.tile(ring, (1, lag_count + 1))[:, :lag_count * (width - 1)]  11.9 us
    all_to_all x1, waiting for transfers between devices, shards(): part = jnp.sum(lax.all_to_all(stacked, 'seg', 0, 0, tiled=True), axis=0)  8.71 us
    all_to_all x1, starting transfers between devices, shards(): part = jnp.sum(lax.all_to_all(stacked, 'seg', 0, 0, tiled=True), axis=0)  7.25 us
    all_to_all x1, waiting for transfers between devices, shards(): lax.all_to_all(copies, 'chan', 0, 0, tiled=True).reshape(-1, flat.shape[1])  4.56 us
    unnamed x5, local copies, waits for them, and re-layouts  4.3 us
    dot_general x1, matrix products, shards(): jnp.einsum('it,jkt->ijk', near, kernel, preferred_element_type=jnp.float32)  3.24 us
  transfers between devices with their start and end apart: 2, of which 2 were waited for; matrix products, arithmetic and copies ran while one was open for 19% of the time, Pallas kernels for 0%

profile of v15, /device:TPU:1, one launch (start us, length us, event | category | flops | bytes accessed | tf_op | source)
XLA Modules:
  0.0 101.3 jit_solution(945124860533118345)
XLA Ops:
  0.0 0.8 fusion.22
  0.8 0.7 convert_element_type.28
  1.5 0.8 fusion.29
  2.3 0.8 broadcast_in_dim.69
  3.1 18.5 %all-to-all-start = ((bf16[32,16,384]{2,1,0:T(8,128)(2,1)}), bf16[32,16,384]{2,1,0:T(8,128)(2,1)S(1)}, u32[]{:S(2)}, u32[]{:S(2)}) async-start(bf16[32,16,384]{2,1,0:T(8,128)(2,1)} %broadcast_in_dim.69), calls=%async_computation | async-start | bytes 786432 | tf_op jit(solution)/shard_map/all_to_all | solution.py:45
  21.9 1.2 %slice.33 = s32[1,1]{1,0:T(1,128)} slice(s32[16,512]{1,0:T(8,128)} %param.6), slice={[0:1], [0:1]} | slice | bytes 8 | tf_op jit(solution)/shard_map/slice | solution.py:69
  23.1 0.8 multiply_add_fusion
  24.1 0.7 fusion.32
  25.2 3.1 %tile.18 = bf16[16,257,641]{2,1,0:T(8,128)(2,1)} broadcast(bf16[16,641]{1,0:T(8,128)(2,1)S(1)} %pad_maximum_fusion), dimensions={0,2} | broadcast | bytes 5292096 | tf_op jit(solution)/shard_map/tile | solution.py:30
  28.3 8.7 %tile.19 = bf16[16,164737]{1,0:T(8,128)(2,1)} reshape(bf16[16,257,641]{2,1,0:T(8,128)(2,1)} %tile.18) | data formatting | bytes 10543168 | tf_op jit(solution)/shard_map/tile | solution.py:30
  37.1 2.5 %slice-done = bf16[16,163840]{1,0:T(8,128)(2,1)S(1)} async-done(((bf16[16,164737]{1,0:T(8,128)(2,1)}), bf16[16,163840]{1,0:T(8,128)(2,1)S(1)}, s32[]{:S(2)}) %slice-start) | async-done | bytes 5242904 | tf_op jit(solution)/shard_map/slice | solution.py:30
  39.5 3.1 %copy.19 = bf16[2,8,256,640]{3,2,1,0:T(8,128)(2,1)} copy(bf16[2,8,256,640]{3,1,2,0:T(8,128)(2,1)S(1)} %bitcast.19) | data formatting | bytes 10485760
  42.7 4.6 %all-to-all-done = bf16[32,16,384]{2,1,0:T(8,128)(2,1)S(1)} async-done(((bf16[32,16,384]{2,1,0:T(8,128)(2,1)}), bf16[32,16,384]{2,1,0:T(8,128)(2,1)S(1)}, u32[]{:S(2)}, u32[]{:S(2)}) %all-to-all-start) | async-done | bytes 393248 | tf_op jit(solution)/shard_map/all_to_all | solution.py:45
  47.6 3.2 %fusion.14 = f32[272,16,256]{2,0,1:T(8,128)S(1)} fusion(bf16[16,256,640]{2,1,0:T(8,128)(2,1)} %bitcast.20, bf16[272,384]{1,0:T(8,128)(2,1)S(1)} %fusion.17), kind=kOutput, calls=%fused_computation.17 | convolution fusion | flops 855638016 | bytes 7811072 | tf_op jit(solution)/shard_map/it,jkt->ijk/dot_general | solution.py:56
  50.8 1.0 reduce-precision_convert_fusion
  51.8 3.1 %fusion.1 = f32[640,512]{1,0:T(8,128)S(1)} fusion(bf16[4352]{0:T(1024)(128)(2,1)S(1)} %broadcast_in_dim.66, s32[4352]{0:T(1024)S(1)} %eq.38, s32[640]{0:T(1024)S(1)} %add.115, bf16[4352,256]{1,0:T(8,128)(2,1)S(1)} %get-tuple-element.6, bf16[4352,256]{1,0:T(8,128)(2,1)S(1)} %get-tuple-element.5), kind=kOutput, calls=%fused_computation.2 | convolution fusion | flops 2866610176 | bytes 5795840 | tf_op jit(solution)/shard_map/dot_general | solution.py:80
  55.2 0.9 reverse
  56.7 1.6 %fusion = f32[640,2]{1,0:T(8,128)S(1)} fusion(bf16[4352]{0:T(1024)(128)(2,1)S(1)} %broadcast_in_dim.66, s32[4352]{0:T(1024)S(1)} %eq.38, s32[640]{0:T(1024)S(1)} %add.115, bf16[4352,1]{0,1:T(2,128)(2,1)S(1)} %get-tuple-element.8, bf16[4352,1]{0,1:T(2,128)(2,1)S(1)} %get-tuple-element.7), kind=kOutput, calls=%fused_computation.1 | convolution fusion | flops 16746496 | bytes 51200 | tf_op jit(solution)/shard_map/dot_general | solution.py:83
  58.5 1.1 %fusion.16 = f32[640,256]{1,0:T(8,128)} fusion(f32[640,255]{1,0:T(8,128)S(1)} %slice.60, f32[640,1]{1,0:T(8,128)S(1)} %slice_add_fusion.1, f32[640,512]{1,0:T(8,128)S(1)} %fusion.1), kind=kLoop, calls=%fused_computation.23 | loop fusion | flops 655360 | bytes 2621440 | tf_op jit(solution)/shard_map/mul | solution.py:88
  59.6 7.2 %all-to-all-start.1 = ((f32[16,40,256]{2,1,0:T(8,128)}), f32[16,40,256]{2,1,0:T(8,128)S(1)}, u32[]{:S(2)}, u32[]{:S(2)}) async-start(f32[16,40,256]{2,1,0:T(8,128)} %bitcast.7), calls=%async_computation.1 | async-start | bytes 1310720 | tf_op jit(solution)/shard_map/all_to_all | solution.py:89
  66.8 0.6 dynamic_slice.11
  69.4 8.7 %all-to-all-done.1 = f32[16,40,256]{2,1,0:T(8,128)S(1)} async-done(((f32[16,40,256]{2,1,0:T(8,128)}), f32[16,40,256]{2,1,0:T(8,128)S(1)}, u32[]{:S(2)}, u32[]{:S(2)}) %all-to-all-start.1) | async-done | bytes 655392 | tf_op jit(solution)/shard_map/all_to_all | solution.py:89
  78.2 22.4 %all_to_all.15 = f32[32,2,256]{2,1,0:T(2,128)S(1)} all-to-all(f32[32,2,256]{2,1,0:T(2,128)S(1)} %constant_dynamic-update-slice_fusion), channel_id=1, replica_groups=mesh['chan'=32,'seg'=16] {'chan'}, dimensions={0} | all-to-all | bytes 131072 | tf_op jit(solution)/shard_map/all_to_all | solution.py:93
  100.7 0.6 reduce_sum.29
  (34 shorter events, 2.3 us)
Async XLA Ops:
  2.3 34.8 %copy-start = (bf16[16,384]{1,0:T(8,128)(2,1)}, bf16[16,384]{1,0:T(8,128)(2,1)S(1)}, u32[]{:S(2)}) copy-start(bf16[16,384]{1,0:T(8,128)(2,1)S(1)} %fusion.29) | copy-start | bytes 36868
  3.1 44.2 %all-to-all-start = ((bf16[32,16,384]{2,1,0:T(8,128)(2,1)}), bf16[32,16,384]{2,1,0:T(8,128)(2,1)S(1)}, u32[]{:S(2)}, u32[]{:S(2)}) async-start(bf16[32,16,384]{2,1,0:T(8,128)(2,1)} %broadcast_in_dim.69), calls=%async_computation | async-start | bytes 786432 | tf_op jit(solution)/shard_map/all_to_all | solution.py:45
  37.1 2.5 %slice-start = ((bf16[16,164737]{1,0:T(8,128)(2,1)}), bf16[16,163840]{1,0:T(8,128)(2,1)S(1)}, s32[]{:S(2)}) async-start(bf16[16,164737]{1,0:T(8,128)(2,1)} %tile.19), calls=%async_computation.3 | async-start | bytes 10485760 | tf_op jit(solution)/shard_map/slice | solution.py:30
  54.9 1.5 %slice-start.1 = ((bf16[16,384]{1,0:T(8,128)(2,1)}), bf16[16,256]{1,0:T(8,128)(2,1)S(1)}, s32[]{:S(2)}) async-start(bf16[16,384]{1,0:T(8,128)(2,1)} %copy-done), calls=%async_computation.4 | async-start | bytes 16384 | tf_op jit(solution)/shard_map/slice | solution.py:58
  59.6 18.5 %all-to-all-start.1 = ((f32[16,40,256]{2,1,0:T(8,128)}), f32[16,40,256]{2,1,0:T(8,128)S(1)}, u32[]{:S(2)}, u32[]{:S(2)}) async-start(f32[16,40,256]{2,1,0:T(8,128)} %bitcast.7), calls=%async_computation.1 | async-start | bytes 1310720 | tf_op jit(solution)/shard_map/all_to_all | solution.py:89

commit v16 on v15

--- a/solution.py
+++ b/solution.py
@@ -82,8 +82,8 @@
     ends = jnp.concatenate([edge_high, edge - edge_high], axis=1).astype(jnp.bfloat16)
     tail = jnp.dot(onehot, ends, preferred_element_type=jnp.float32)
     direct = both[:, :LAGS] + both[:, LAGS:]
-    mirror = jnp.concatenate([tail[:, :1] + tail[:, 1:], jnp.flip(direct[:, 1:], axis=1)], axis=1)
-    total = direct + mirror
+    first_lag = jnp.arange(LAGS, dtype=jnp.int32)[None, :] == 0
+    total = direct + jnp.where(first_lag, tail[:, :1] + tail[:, 1:], 0.0)
     scale = 1.0 / math.sqrt(traces.shape[2] * traces.shape[1] * seg_devices)
     stacked = (total * scale).reshape(seg_devices, depth * OFFBINS, LAGS)
     part = jnp.sum(lax.all_to_all(stacked, "seg", 0, 0, tiled=True), axis=0)
@@ -91,7 +91,9 @@
     dense = jnp.zeros((chan_devices, OFFBINS, LAGS), jnp.float32)
     dense = lax.dynamic_update_slice(dense, part.reshape(depth, OFFBINS, LAGS), (own_first, 0, 0))
     pieces = lax.all_to_all(dense, "chan", 0, 0, tiled=True)
-    return jnp.sum(pieces, axis=0, keepdims=True)
+    summed = jnp.sum(pieces, axis=0, keepdims=True)
+    flipped = jnp.flip(summed[:, :, 1:], axis=2)
+    return summed + jnp.concatenate([jnp.zeros_like(summed[:, :, :1]), flipped], axis=2)
 
 
 def solution(mesh):

time: 102 us -> 102 us (level)
  other arithmetic: 7.4 us -> 8.58 us
  local copies, waits for them, and re-layouts: 22.2 us -> 21.1 us
    another operation x2, other arithmetic: 1 us -> 2.38 us
    unnamed x5 -> x7, local copies, waits for them, and re-layouts: 4.3 us -> 3.42 us
where the time goes in v16:
time: 102 us; the launch traced here: 101 us
  starting transfers between devices  25.7 us (25%)
  blocking collectives  22.4 us (22%)
  local copies, waits for them, and re-layouts  21.1 us (21%)
  waiting for transfers between devices  13.3 us (13%)
  other arithmetic  8.58 us (8%)
  matrix products  8.07 us (8%)
  between operations  2.15 us (2%)
    all_to_all x1, blocking collectives, shards(): pieces = lax.all_to_all(dense, 'chan', 0, 0, tiled=True)  22.4 us
    all_to_all x1, starting transfers between devices, shards(): lax.all_to_all(copies, 'chan', 0, 0, tiled=True).reshape(-1, flat.shape[1])  18.5 us
    another operation x2, local copies, waits for them, and re-layouts, toeplitz(): tiled = jnp.tile(ring, (1, lag_count + 1))[:, :lag_count * (width - 1)]  11.9 us
    all_to_all x1, waiting for transfers between devices, shards(): part = jnp.sum(lax.all_to_all(stacked, 'seg', 0, 0, tiled=True), axis=0)  8.71 us
    all_to_all x1, starting transfers between devices, shards(): part = jnp.sum(lax.all_to_all(stacked, 'seg', 0, 0, tiled=True), axis=0)  7.25 us
    all_to_all x1, waiting for transfers between devices, shards(): lax.all_to_all(copies, 'chan', 0, 0, tiled=True).reshape(-1, flat.shape[1])  4.56 us
    unnamed x7, local copies, waits for them, and re-layouts  3.42 us
    dot_general x1, matrix products, shards(): jnp.einsum('it,jkt->ijk', near, kernel, preferred_element_type=jnp.float32)  3.27 us
  transfers between devices with their start and end apart: 2, of which 2 were waited for; matrix products, arithmetic and copies ran while one was open for 19% of the time, Pallas kernels for 0%

profile of v16, /device:TPU:1, one launch (start us, length us, event | category | flops | bytes accessed | tf_op | source)
XLA Modules:
  0.0 101.4 jit_solution(11596149972979173515)
XLA Ops:
  0.0 0.8 fusion.23
  0.8 0.7 convert_element_type.28
  1.5 0.8 fusion.30
  2.3 0.8 broadcast_in_dim.92
  3.1 18.5 %all-to-all-start = ((bf16[32,16,384]{2,1,0:T(8,128)(2,1)}), bf16[32,16,384]{2,1,0:T(8,128)(2,1)S(1)}, u32[]{:S(2)}, u32[]{:S(2)}) async-start(bf16[32,16,384]{2,1,0:T(8,128)(2,1)} %broadcast_in_dim.92), calls=%async_computation | async-start | bytes 786432 | tf_op jit(solution)/shard_map/all_to_all | solution.py:45
  21.9 1.2 %slice.33 = s32[1,1]{1,0:T(1,128)} slice(s32[16,512]{1,0:T(8,128)} %param.6), slice={[0:1], [0:1]} | slice | bytes 8 | tf_op jit(solution)/shard_map/slice | solution.py:69
  23.1 0.8 multiply_add_fusion
  24.1 0.7 fusion.34
  25.2 3.1 %tile.18 = bf16[16,257,641]{2,1,0:T(8,128)(2,1)} broadcast(bf16[16,641]{1,0:T(8,128)(2,1)S(1)} %pad_maximum_fusion), dimensions={0,2} | broadcast | bytes 5292096 | tf_op jit(solution)/shard_map/tile | solution.py:30
  28.3 8.7 %tile.19 = bf16[16,164737]{1,0:T(8,128)(2,1)} reshape(bf16[16,257,641]{2,1,0:T(8,128)(2,1)} %tile.18) | data formatting | bytes 10543168 | tf_op jit(solution)/shard_map/tile | solution.py:30
  37.0 2.5 %slice-done = bf16[16,163840]{1,0:T(8,128)(2,1)S(1)} async-done(((bf16[16,164737]{1,0:T(8,128)(2,1)}), bf16[16,163840]{1,0:T(8,128)(2,1)S(1)}, s32[]{:S(2)}) %slice-start) | async-done | bytes 5242904 | tf_op jit(solution)/shard_map/slice | solution.py:30
  39.5 3.2 %copy.8 = bf16[2,8,256,640]{3,2,1,0:T(8,128)(2,1)} copy(bf16[2,8,256,640]{3,1,2,0:T(8,128)(2,1)S(1)} %bitcast.20) | data formatting | bytes 10485760
  42.7 4.6 %all-to-all-done = bf16[32,16,384]{2,1,0:T(8,128)(2,1)S(1)} async-done(((bf16[32,16,384]{2,1,0:T(8,128)(2,1)}), bf16[32,16,384]{2,1,0:T(8,128)(2,1)S(1)}, u32[]{:S(2)}, u32[]{:S(2)}) %all-to-all-start) | async-done | bytes 393248 | tf_op jit(solution)/shard_map/all_to_all | solution.py:45
  47.2 0.3 fusion.18
  47.6 3.3 %fusion.14 = f32[272,16,256]{2,0,1:T(8,128)S(1)} fusion(bf16[16,256,640]{2,1,0:T(8,128)(2,1)} %bitcast.21, bf16[272,384]{1,0:T(8,128)(2,1)S(1)} %fusion.18), kind=kOutput, calls=%fused_computation.17 | convolution fusion | flops 855638016 | bytes 7811072 | tf_op jit(solution)/shard_map/it,jkt->ijk/dot_general | solution.py:56
  50.9 2.4 %reduce-precision_convert_fusion = (bf16[4352,256]{1,0:T(8,128)(2,1)S(1)}, bf16[4352,256]{1,0:T(8,128)(2,1)}) fusion(f32[272,16,256]{2,0,1:T(8,128)S(1)} %fusion.14), kind=kLoop, calls=%fused_computation.4 | loop fusion | flops 4456448 | bytes 8912896 | tf_op jit(solution)/shard_map/convert.2
  53.6 1.6 %fusion = f32[640,2]{0,1:T(2,128)S(1)} fusion(bf16[4352]{0:T(1024)(128)(2,1)S(1)} %broadcast_in_dim.89, s32[4352]{0:T(1024)S(1)} %eq.49, s32[640]{0:T(1024)S(1)} %add.120, bf16[4352,1]{0,1:T(2,128)(2,1)S(1)} %get-tuple-element.8, bf16[4352,1]{0,1:T(2,128)(2,1)S(1)} %get-tuple-element.7), kind=kOutput, calls=%fused_computation.1 | convolution fusion | flops 16746496 | bytes 51200 | tf_op jit(solution)/shard_map/dot_general | solution.py:83
  55.2 3.1 %fusion.1 = f32[640,512]{1,0:T(8,128)S(1)} fusion(bf16[4352]{0:T(1024)(128)(2,1)S(1)} %broadcast_in_dim.89, s32[4352]{0:T(1024)S(1)} %eq.49, s32[640]{0:T(1024)S(1)} %add.120, bf16[4352,256]{1,0:T(8,128)(2,1)S(1)} %copy-done, bf16[4352,256]{1,0:T(8,128)(2,1)S(1)} %get-tuple-element.5), kind=kOutput, calls=%fused_computation.2 | convolution fusion | flops 2866610176 | bytes 5795840 | tf_op jit(solution)/shard_map/dot_general | solution.py:80
  58.3 1.0 fusion.17
  59.3 7.2 %all-to-all-start.1 = ((f32[16,40,256]{2,1,0:T(8,128)}), f32[16,40,256]{2,1,0:T(8,128)S(1)}, u32[]{:S(2)}, u32[]{:S(2)}) async-start(f32[16,40,256]{2,1,0:T(8,128)} %bitcast.7), calls=%async_computation.1 | async-start | bytes 1310720 | tf_op jit(solution)/shard_map/all_to_all | solution.py:89
  66.5 0.6 dynamic_slice.11
  69.1 8.7 %all-to-all-done.1 = f32[16,40,256]{2,1,0:T(8,128)S(1)} async-done(((f32[16,40,256]{2,1,0:T(8,128)}), f32[16,40,256]{2,1,0:T(8,128)S(1)}, u32[]{:S(2)}, u32[]{:S(2)}) %all-to-all-start.1) | async-done | bytes 655392 | tf_op jit(solution)/shard_map/all_to_all | solution.py:89
  77.9 22.4 %all_to_all.15 = f32[32,2,256]{2,1,0:T(2,128)S(1)} all-to-all(f32[32,2,256]{2,1,0:T(2,128)S(1)} %constant_dynamic-update-slice_fusion), channel_id=1, replica_groups=mesh['chan'=32,'seg'=16] {'chan'}, dimensions={0} | all-to-all | bytes 131072 | tf_op jit(solution)/shard_map/all_to_all | solution.py:93
  100.7 0.7 pad_add_fusion
  (37 shorter events, 1.7 us)
Async XLA Ops:
  2.3 34.7 %copy-start.1 = (bf16[16,384]{1,0:T(8,128)(2,1)}, bf16[16,384]{1,0:T(8,128)(2,1)S(1)}, u32[]{:S(2)}) copy-start(bf16[16,384]{1,0:T(8,128)(2,1)S(1)} %fusion.30) | copy-start | bytes 36868
  3.1 44.2 %all-to-all-start = ((bf16[32,16,384]{2,1,0:T(8,128)(2,1)}), bf16[32,16,384]{2,1,0:T(8,128)(2,1)S(1)}, u32[]{:S(2)}, u32[]{:S(2)}) async-start(bf16[32,16,384]{2,1,0:T(8,128)(2,1)} %broadcast_in_dim.92), calls=%async_computation | async-start | bytes 786432 | tf_op jit(solution)/shard_map/all_to_all | solution.py:45
  37.0 2.5 %slice-start = ((bf16[16,164737]{1,0:T(8,128)(2,1)}), bf16[16,163840]{1,0:T(8,128)(2,1)S(1)}, s32[]{:S(2)}) async-start(bf16[16,164737]{1,0:T(8,128)(2,1)} %tile.19), calls=%async_computation.3 | async-start | bytes 10485760 | tf_op jit(solution)/shard_map/slice | solution.py:30
  50.9 2.4 %slice-start.1 = ((bf16[16,384]{1,0:T(8,128)(2,1)}), bf16[16,256]{1,0:T(8,128)(2,1)S(1)}, s32[]{:S(2)}) async-start(bf16[16,384]{1,0:T(8,128)(2,1)} %copy-done.1), calls=%async_computation.4 | async-start | bytes 16384 | tf_op jit(solution)/shard_map/slice | solution.py:58
  53.5 1.7 %copy-start = (bf16[4352,256]{1,0:T(8,128)(2,1)S(1)}, bf16[4352,256]{1,0:T(8,128)(2,1)}, u32[]{:S(2)}) copy-start(bf16[4352,256]{1,0:T(8,128)(2,1)} %get-tuple-element.6) | copy-start | bytes 6684676
  59.3 18.5 %all-to-all-start.1 = ((f32[16,40,256]{2,1,0:T(8,128)}), f32[16,40,256]{2,1,0:T(8,128)S(1)}, u32[]{:S(2)}, u32[]{:S(2)}) async-start(f32[16,40,256]{2,1,0:T(8,128)} %bitcast.7), calls=%async_computation.1 | async-start | bytes 1310720 | tf_op jit(solution)/shard_map/all_to_all | solution.py:89

commit v17 on v16

--- a/solution.py
+++ b/solution.py
@@ -40,9 +40,13 @@
     kernel = toeplitz(normed, LAGS)
     first_row = lax.axis_index("chan") * chan_count
     own_rows = first_row + jnp.arange(chan_count, dtype=jnp.int32)[None, :]
-    flat = lax.optimization_barrier(normed.reshape(chan_count, -1))
-    copies = jnp.broadcast_to(flat[None], (chan_devices,) + flat.shape)
-    piece = lax.all_to_all(copies, "chan", 0, 0, tiled=True).reshape(-1, flat.shape[1])
+    flat = normed.reshape(chan_count, -1)
+    raw = traces.reshape(chan_count, -1)
+    lengths = jnp.zeros((chan_count, 128), raw.dtype).at[:, 0].set(taper_len.astype(raw.dtype))
+    packed = jnp.concatenate([raw, lengths], axis=1)
+    copies = jnp.broadcast_to(packed[None], (chan_devices,) + packed.shape)
+    got = lax.all_to_all(copies, "chan", 0, 0, tiled=True).reshape(-1, packed.shape[1])
+    piece = normalize(got[:, None, : raw.shape[1]], got[:, raw.shape[1]]).reshape(-1, raw.shape[1])
     row_count = piece.shape[0]
     sample_count = piece.shape[1]
     me = lax.axis_index("chan")

time: 102 us -> 106 us (1.039)
  other arithmetic: 8.58 us -> 11.8 us
  blocking collectives: 22.4 us -> 19.2 us
  waiting for transfers between devices: 13.3 us -> 16.3 us
    all_to_all x1, blocking collectives: 22.4 us -> 19.2 us  [shards(): pieces = lax.all_to_all(dense, 'chan', 0, 0, tiled=True)]
    all_to_all x1, waiting for transfers between devices: 4.56 us -> 7.55 us  [shards(): lax.all_to_all(copies, 'chan', 0, 0, tiled=True)]
    another operation x2 -> x4, other arithmetic: 2.38 us -> 4.33 us
    unnamed x7 -> x6, local copies, waits for them, and re-layouts: 3.42 us -> 3.53 us
  transfers between devices with their start and end apart: 2 -> 2, of which waited for: 2 -> 2; matrix products, arithmetic and copies ran while one was open for 19% -> 20% of each run, Pallas kernels for 0% -> 0%
where the time goes in v17:
time: 106 us; the launch traced here: 105 us
  starting transfers between devices  26 us (25%)
  local copies, waits for them, and re-layouts  21.3 us (20%)
  blocking collectives  19.2 us (18%)
  waiting for transfers between devices  16.3 us (15%)
  other arithmetic  11.8 us (11%)
  matrix products  8.07 us (8%)
  between operations  2.15 us (2%)
    all_to_all x1, blocking collectives, shards(): pieces = lax.all_to_all(dense, 'chan', 0, 0, tiled=True)  19.2 us
    all_to_all x1, starting transfers between devices, shards(): lax.all_to_all(copies, 'chan', 0, 0, tiled=True)  18.5 us
    another operation x2, local copies, waits for them, and re-layouts, toeplitz(): tiled = jnp.tile(ring, (1, lag_count + 1))[:, :lag_count * (width - 1)]  11.9 us
    all_to_all x1, waiting for transfers between devices, shards(): part = jnp.sum(lax.all_to_all(stacked, 'seg', 0, 0, tiled=True), axis=0)  8.71 us
    all_to_all x1, waiting for transfers between devices, shards(): lax.all_to_all(copies, 'chan', 0, 0, tiled=True)  7.55 us
    all_to_all x1, starting transfers between devices, shards(): part = jnp.sum(lax.all_to_all(stacked, 'seg', 0, 0, tiled=True), axis=0)  7.52 us
    another operation x4, other arithmetic  4.33 us
    unnamed x6, local copies, waits for them, and re-layouts  3.53 us
  transfers between devices with their start and end apart: 2, of which 2 were waited for; matrix products, arithmetic and copies ran while one was open for 20% of the time, Pallas kernels for 0%

profile of v17, /device:TPU:1, one launch (start us, length us, event | category | flops | bytes accessed | tf_op | source)
XLA Modules:
  0.0 104.8 jit_solution(18014302607853911342)
XLA Ops:
  0.6 1.3 %fusion.40 = bf16[16,1]{0,1:T(2,128)(2,1)S(1)} fusion(pred[]{:T(512)} %compare_reduce_fusion, s32[16]{0:T(128)} %param.7), kind=kLoop, calls=%fused_computation.78 | loop fusion | flops 32 | bytes 97 | tf_op jit(solution)/shard_map/reshape.47
  2.0 0.7 fusion.35
  2.8 0.9 broadcast_in_dim.96
  3.6 18.5 %all-to-all-start = ((bf16[32,16,512]{2,1,0:T(8,128)(2,1)}), bf16[32,16,512]{2,1,0:T(8,128)(2,1)S(1)}, u32[]{:S(2)}, u32[]{:S(2)}) async-start(bf16[32,16,512]{2,1,0:T(8,128)(2,1)} %broadcast_in_dim.96), calls=%async_computation | async-start | bytes 1048576 | tf_op jit(solution)/shard_map/all_to_all | solution.py:48
  22.1 0.7 convert_element_type.59
  23.1 1.2 %slice.53 = s32[1,1]{1,0:T(1,128)} slice(s32[16,512]{1,0:T(8,128)} %param.8), slice={[0:1], [0:1]} | slice | bytes 8 | tf_op jit(solution)/shard_map/slice | solution.py:73
  24.3 0.8 multiply_add_fusion
  25.3 0.7 fusion.41
  26.3 0.8 fusion.28
  27.1 0.8 fusion.36
  28.0 3.1 %tile.18 = bf16[16,257,641]{2,1,0:T(8,128)(2,1)} broadcast(bf16[16,641]{1,0:T(8,128)(2,1)S(1)} %pad_maximum_fusion), dimensions={0,2} | broadcast | bytes 5292096 | tf_op jit(solution)/shard_map/tile | solution.py:30
  31.2 8.7 %tile.19 = bf16[16,164737]{1,0:T(8,128)(2,1)} reshape(bf16[16,257,641]{2,1,0:T(8,128)(2,1)} %tile.18) | data formatting | bytes 10543168 | tf_op jit(solution)/shard_map/tile | solution.py:30
  39.9 2.5 %slice-done = bf16[16,163840]{1,0:T(8,128)(2,1)S(1)} async-done(((bf16[16,164737]{1,0:T(8,128)(2,1)}), bf16[16,163840]{1,0:T(8,128)(2,1)S(1)}, s32[]{:S(2)}) %slice-start) | async-done | bytes 5242904 | tf_op jit(solution)/shard_map/slice | solution.py:30
  42.4 3.2 %copy.14 = bf16[2,8,256,640]{3,2,1,0:T(8,128)(2,1)} copy(bf16[2,8,256,640]{3,1,2,0:T(8,128)(2,1)S(1)} %bitcast.23) | data formatting | bytes 10485760
  45.5 7.5 %all-to-all-done = bf16[32,16,512]{2,1,0:T(8,128)(2,1)S(1)} async-done(((bf16[32,16,512]{2,1,0:T(8,128)(2,1)}), bf16[32,16,512]{2,1,0:T(8,128)(2,1)S(1)}, u32[]{:S(2)}, u32[]{:S(2)}) %all-to-all-start) | async-done | bytes 524320 | tf_op jit(solution)/shard_map/all_to_all | solution.py:48
  54.0 3.3 %fusion.14 = f32[272,16,256]{2,0,1:T(8,128)S(1)} fusion(bf16[16,256,640]{2,1,0:T(8,128)(2,1)} %bitcast.24, bf16[272,384]{1,0:T(8,128)(2,1)S(1)} %fusion.22), kind=kOutput, calls=%fused_computation.17 | convolution fusion | flops 855638016 | bytes 7811072 | tf_op jit(solution)/shard_map/it,jkt->ijk/dot_general | solution.py:60
  57.3 2.4 %reduce-precision_convert_fusion = (bf16[4352,256]{1,0:T(8,128)(2,1)S(1)}, bf16[4352,256]{1,0:T(8,128)(2,1)}) fusion(f32[272,16,256]{2,0,1:T(8,128)S(1)} %fusion.14), kind=kLoop, calls=%fused_computation.4 | loop fusion | flops 4456448 | bytes 8912896 | tf_op jit(solution)/shard_map/convert.3
  60.0 1.6 %fusion = f32[640,2]{0,1:T(2,128)S(1)} fusion(bf16[4352]{0:T(1024)(128)(2,1)S(1)} %broadcast_in_dim.93, s32[4352]{0:T(1024)S(1)} %eq.49, s32[640]{0:T(1024)S(1)} %add.135, bf16[4352,1]{0,1:T(2,128)(2,1)S(1)} %get-tuple-element.20, bf16[4352,1]{0,1:T(2,128)(2,1)S(1)} %get-tuple-element.19), kind=kOutput, calls=%fused_computation.1 | convolution fusion | flops 16746496 | bytes 51200 | tf_op jit(solution)/shard_map/dot_general | solution.py:87
  61.7 3.1 %fusion.1 = f32[640,512]{1,0:T(8,128)S(1)} fusion(bf16[4352]{0:T(1024)(128)(2,1)S(1)} %broadcast_in_dim.93, s32[4352]{0:T(1024)S(1)} %eq.49, s32[640]{0:T(1024)S(1)} %add.135, bf16[4352,256]{1,0:T(8,128)(2,1)S(1)} %copy-done, bf16[4352,256]{1,0:T(8,128)(2,1)S(1)} %get-tuple-element.17), kind=kOutput, calls=%fused_computation.2 | convolution fusion | flops 2866610176 | bytes 5795840 | tf_op jit(solution)/shard_map/dot_general | solution.py:84
  64.7 1.0 fusion.21
  65.7 7.5 %all-to-all-start.1 = ((f32[16,40,256]{2,1,0:T(8,128)}), f32[16,40,256]{2,1,0:T(8,128)S(1)}, u32[]{:S(2)}, u32[]{:S(2)}) async-start(f32[16,40,256]{2,1,0:T(8,128)} %bitcast.9), calls=%async_computation.1 | async-start | bytes 1310720 | tf_op jit(solution)/shard_map/all_to_all | solution.py:93
  75.8 8.7 %all-to-all-done.1 = f32[16,40,256]{2,1,0:T(8,128)S(1)} async-done(((f32[16,40,256]{2,1,0:T(8,128)}), f32[16,40,256]{2,1,0:T(8,128)S(1)}, u32[]{:S(2)}, u32[]{:S(2)}) %all-to-all-start.1) | async-done | bytes 655392 | tf_op jit(solution)/shard_map/all_to_all | solution.py:93
  84.6 19.2 %all_to_all.15 = f32[32,2,256]{2,1,0:T(2,128)S(1)} all-to-all(f32[32,2,256]{2,1,0:T(2,128)S(1)} %constant_dynamic-update-slice_fusion), channel_id=1, replica_groups=mesh['chan'=32,'seg'=16] {'chan'}, dimensions={0} | all-to-all | bytes 131072 | tf_op jit(solution)/shard_map/all_to_all | solution.py:97
  104.2 0.7 pad_add_fusion
  (41 shorter events, 4.0 us)
Async XLA Ops:
  3.6 49.5 %all-to-all-start = ((bf16[32,16,512]{2,1,0:T(8,128)(2,1)}), bf16[32,16,512]{2,1,0:T(8,128)(2,1)S(1)}, u32[]{:S(2)}, u32[]{:S(2)}) async-start(bf16[32,16,512]{2,1,0:T(8,128)(2,1)} %broadcast_in_dim.96), calls=%async_computation | async-start | bytes 1048576 | tf_op jit(solution)/shard_map/all_to_all | solution.py:48
  39.9 2.5 %slice-start = ((bf16[16,164737]{1,0:T(8,128)(2,1)}), bf16[16,163840]{1,0:T(8,128)(2,1)S(1)}, s32[]{:S(2)}) async-start(bf16[16,164737]{1,0:T(8,128)(2,1)} %tile.19), calls=%async_computation.3 | async-start | bytes 10485760 | tf_op jit(solution)/shard_map/slice | solution.py:30
  60.0 1.7 %copy-start = (bf16[4352,256]{1,0:T(8,128)(2,1)S(1)}, bf16[4352,256]{1,0:T(8,128)(2,1)}, u32[]{:S(2)}) copy-start(bf16[4352,256]{1,0:T(8,128)(2,1)} %get-tuple-element.18) | copy-start | bytes 6684676
  65.7 18.8 %all-to-all-start.1 = ((f32[16,40,256]{2,1,0:T(8,128)}), f32[16,40,256]{2,1,0:T(8,128)S(1)}, u32[]{:S(2)}, u32[]{:S(2)}) async-start(f32[16,40,256]{2,1,0:T(8,128)} %bitcast.9), calls=%async_computation.1 | async-start | bytes 1310720 | tf_op jit(solution)/shard_map/all_to_all | solution.py:93

commit v18 on v15

--- a/solution.py
+++ b/solution.py
@@ -73,16 +73,10 @@
     window = (first[:, None] + jnp.arange(depth, dtype=jnp.int32)[None, :]) * seg_devices + lanes[:, None]
     wanted = (window[:, :, None] * OFFBINS + jnp.arange(OFFBINS, dtype=jnp.int32)).reshape(-1)
     hit = wanted[:, None] == labels[None, :]
-    onehot = jnp.where(hit, jnp.tile(weight, chan_count)[None, :], 0.0).astype(jnp.bfloat16)
-    high = lax.reduce_precision(product, exponent_bits=8, mantissa_bits=7)
-    low = product - high
-    split = jnp.concatenate([high, low], axis=1).astype(jnp.bfloat16)
-    both = jnp.dot(onehot, split, preferred_element_type=jnp.float32)
-    edge_high = lax.reduce_precision(edge, exponent_bits=8, mantissa_bits=7)
-    ends = jnp.concatenate([edge_high, edge - edge_high], axis=1).astype(jnp.bfloat16)
-    tail = jnp.dot(onehot, ends, preferred_element_type=jnp.float32)
-    direct = both[:, :LAGS] + both[:, LAGS:]
-    mirror = jnp.concatenate([tail[:, :1] + tail[:, 1:], jnp.flip(direct[:, 1:], axis=1)], axis=1)
+    onehot = jnp.where(hit, jnp.tile(weight, chan_count)[None, :], 0.0)
+    direct = jnp.dot(onehot, product, precision=lax.Precision.HIGH, preferred_element_type=jnp.float32)
+    tail = jnp.dot(onehot, edge, precision=lax.Precision.HIGH, preferred_element_type=jnp.float32)
+    mirror = jnp.concatenate([tail, jnp.flip(direct[:, 1:], axis=1)], axis=1)
     total = direct + mirror
     scale = 1.0 / math.sqrt(traces.shape[2] * traces.shape[1] * seg_devices)
     stacked = (total * scale).reshape(seg_devices, depth * OFFBINS, LAGS)

time: 102 us -> 104 us (1.020)
  matrix products: 8.07 us -> 13 us
  other arithmetic: 7.4 us -> 5.4 us
  blocking collectives: 22.4 us -> 21 us
  waiting for transfers between devices: 13.3 us -> 14.7 us
    dot_general x2, matrix products: 4.71 us -> 9.59 us  [the longest x1 4.9 us: shards(): jnp.dot(onehot, product, precision=lax.Precision.HIGH, preferred_element_...]
    all_to_all x1, waiting for transfers between devices: 4.56 us -> 6.01 us  [shards(): lax.all_to_all(copies, 'chan', 0, 0, tiled=True).reshape(-1, flat.shape[1])]
    all_to_all x1, blocking collectives: 22.4 us -> 21 us  [shards(): pieces = lax.all_to_all(dense, 'chan', 0, 0, tiled=True)]
    unnamed x5 -> x9, local copies, waits for them, and re-layouts: 4.3 us -> 4.46 us
  transfers between devices with their start and end apart: 2 -> 2, of which waited for: 2 -> 2; matrix products, arithmetic and copies ran while one was open for 19% -> 17% of each run, Pallas kernels for 0% -> 0%
where the time goes in v18:
time: 104 us
  starting transfers between devices  25.7 us (25%)
  local copies, waits for them, and re-layouts  21.8 us (21%)
  blocking collectives  21 us (20%)
  waiting for transfers between devices  14.7 us (14%)
  matrix products  13 us (12%)
  other arithmetic  5.4 us (5%)
  between operations  2.16 us (2%)
    all_to_all x1, blocking collectives, shards(): pieces = lax.all_to_all(dense, 'chan', 0, 0, tiled=True)  21 us
    all_to_all x1, starting transfers between devices, shards(): lax.all_to_all(copies, 'chan', 0, 0, tiled=True).reshape(-1, flat.shape[1])  18.5 us
    another operation x2, local copies, waits for them, and re-layouts, toeplitz(): tiled = jnp.tile(ring, (1, lag_count + 1))[:, :lag_count * (width - 1)]  11.9 us
    all_to_all x1, waiting for transfers between devices, shards(): part = jnp.sum(lax.all_to_all(stacked, 'seg', 0, 0, tiled=True), axis=0)  8.71 us
    all_to_all x1, starting transfers between devices, shards(): part = jnp.sum(lax.all_to_all(stacked, 'seg', 0, 0, tiled=True), axis=0)  7.25 us
    all_to_all x1, waiting for transfers between devices, shards(): lax.all_to_all(copies, 'chan', 0, 0, tiled=True).reshape(-1, flat.shape[1])  6.01 us
    dot_general x1, matrix products, shards(): jnp.dot(onehot, product, precision=lax.Precision.HIGH, preferred_element_...  4.9 us
    dot_general x1, matrix products, shards(): jnp.dot(onehot, edge, precision=lax.Precision.HIGH, preferred_element_typ...  4.7 us
  transfers between devices with their start and end apart: 2, of which 2 were waited for; matrix products, arithmetic and copies ran while one was open for 17% of the time, Pallas kernels for 0%

profile of v18, /device:TPU:1, one launch (start us, length us, event | category | flops | bytes accessed | tf_op | source)
XLA Modules:
  0.0 103.8 jit_solution(11085525054079840639)
XLA Ops:
  0.0 0.8 fusion.25
  0.8 0.7 convert_element_type.22
  1.5 0.8 fusion.28
  2.3 0.8 broadcast_in_dim.69
  3.1 18.5 %all-to-all-start = ((bf16[32,16,384]{2,1,0:T(8,128)(2,1)}), bf16[32,16,384]{2,1,0:T(8,128)(2,1)S(1)}, u32[]{:S(2)}, u32[]{:S(2)}) async-start(bf16[32,16,384]{2,1,0:T(8,128)(2,1)} %broadcast_in_dim.69), calls=%async_computation | async-start | bytes 786432 | tf_op jit(solution)/shard_map/all_to_all | solution.py:45
  21.7 3.1 %tile.18 = bf16[16,257,641]{2,1,0:T(8,128)(2,1)} broadcast(bf16[16,641]{1,0:T(8,128)(2,1)S(1)} %pad_maximum_fusion), dimensions={0,2} | broadcast | bytes 5292096 | tf_op jit(solution)/shard_map/tile | solution.py:30
  24.8 8.7 %tile.19 = bf16[16,164737]{1,0:T(8,128)(2,1)} reshape(bf16[16,257,641]{2,1,0:T(8,128)(2,1)} %tile.18) | data formatting | bytes 10543168 | tf_op jit(solution)/shard_map/tile | solution.py:30
  33.6 2.5 %slice-done = bf16[16,163840]{1,0:T(8,128)(2,1)S(1)} async-done(((bf16[16,164737]{1,0:T(8,128)(2,1)}), bf16[16,163840]{1,0:T(8,128)(2,1)S(1)}, s32[]{:S(2)}) %slice-start) | async-done | bytes 5242904 | tf_op jit(solution)/shard_map/slice | solution.py:30
  36.1 3.2 %copy.12 = bf16[2,8,256,640]{3,2,1,0:T(8,128)(2,1)} copy(bf16[2,8,256,640]{3,1,2,0:T(8,128)(2,1)S(1)} %bitcast.19) | data formatting | bytes 10485760
  39.5 0.5 slice.21
  40.2 0.7 fusion.31
  41.2 6.0 %all-to-all-done = bf16[32,16,384]{2,1,0:T(8,128)(2,1)S(1)} async-done(((bf16[32,16,384]{2,1,0:T(8,128)(2,1)}), bf16[32,16,384]{2,1,0:T(8,128)(2,1)S(1)}, u32[]{:S(2)}, u32[]{:S(2)}) %all-to-all-start) | async-done | bytes 393248 | tf_op jit(solution)/shard_map/all_to_all | solution.py:45
  47.2 0.3 fusion.20
  47.6 3.2 %fusion.14 = f32[272,16,256]{2,0,1:T(8,128)S(1)} fusion(bf16[16,256,640]{2,1,0:T(8,128)(2,1)} %bitcast.20, bf16[272,384]{1,0:T(8,128)(2,1)S(1)} %fusion.20), kind=kOutput, calls=%fused_computation.14 | convolution fusion | flops 855638016 | bytes 7811072 | tf_op jit(solution)/shard_map/it,jkt->ijk/dot_general | solution.py:56
  50.8 4.9 %fusion.2 = f32[640,256]{1,0:T(8,128)S(1)} fusion(f32[4352,256]{1,0:T(8,128)S(1)} %bitcast.21, f32[4352]{0:T(1024)S(1)} %broadcast_in_dim.66, s32[4352]{0:T(1024)S(1)} %eq.38, s32[640]{0:T(1024)S(1)} %add.109), kind=kOutput, calls=%fused_computation.2 | convolution fusion | flops 4283760640 | bytes 5149184 | tf_op jit(solution)/shard_map/dot_general | solution.py:77
  55.7 0.2 slice.33
  56.0 1.1 %reverse = f32[640,256]{1,0:T(8,128)S(1)} reverse(f32[640,256]{1,0:T(8,128)S(1)} %bitcast.22), dimensions={1} | reverse | bytes 1310720
  57.6 4.7 %fusion.16 = f32[640]{0:T(1024)S(1)} fusion(f32[4352,1]{0,1:T(1,128)S(1)} %reshape.221, f32[4352]{0:T(1024)S(1)} %broadcast_in_dim.66, s32[4352]{0:T(1024)S(1)} %eq.38, s32[640]{0:T(1024)S(1)} %add.109), kind=kOutput, calls=%fused_computation.16 | convolution fusion | flops 22282240 | bytes 57344 | tf_op jit(solution)/shard_map/dot_general | solution.py:78
  62.4 1.1 %fusion.19 = f32[640,256]{1,0:T(8,128)} fusion(f32[640,256]{1,0:T(8,128)S(1)} %fusion.2, f32[640,255]{1,0:T(8,128)S(1)} %slice.36, f32[640,1]{1,0:T(8,128)S(1)} %dot_general.19), kind=kLoop, calls=%fused_computation.20 | loop fusion | flops 491520 | bytes 1966080 | tf_op jit(solution)/shard_map/mul | solution.py:82
  63.5 7.2 %all-to-all-start.1 = ((f32[16,40,256]{2,1,0:T(8,128)}), f32[16,40,256]{2,1,0:T(8,128)S(1)}, u32[]{:S(2)}, u32[]{:S(2)}) async-start(f32[16,40,256]{2,1,0:T(8,128)} %bitcast.6), calls=%async_computation.1 | async-start | bytes 1310720 | tf_op jit(solution)/shard_map/all_to_all | solution.py:83
  70.8 0.6 dynamic_slice.11
  73.3 8.7 %all-to-all-done.1 = f32[16,40,256]{2,1,0:T(8,128)S(1)} async-done(((f32[16,40,256]{2,1,0:T(8,128)}), f32[16,40,256]{2,1,0:T(8,128)S(1)}, u32[]{:S(2)}, u32[]{:S(2)}) %all-to-all-start.1) | async-done | bytes 655392 | tf_op jit(solution)/shard_map/all_to_all | solution.py:83
  82.1 21.0 %all_to_all.15 = f32[32,2,256]{2,1,0:T(2,128)S(1)} all-to-all(f32[32,2,256]{2,1,0:T(2,128)S(1)} %constant_dynamic-update-slice_fusion), channel_id=1, replica_groups=mesh['chan'=32,'seg'=16] {'chan'}, dimensions={0} | all-to-all | bytes 131072 | tf_op jit(solution)/shard_map/all_to_all | solution.py:87
  103.1 0.6 reduce_sum.29
  (35 shorter events, 1.6 us)
Async XLA Ops:
  2.3 31.3 %copy-start = (bf16[16,384]{1,0:T(8,128)(2,1)}, bf16[16,384]{1,0:T(8,128)(2,1)S(1)}, u32[]{:S(2)}) copy-start(bf16[16,384]{1,0:T(8,128)(2,1)S(1)} %fusion.28) | copy-start | bytes 36868
  3.1 44.2 %all-to-all-start = ((bf16[32,16,384]{2,1,0:T(8,128)(2,1)}), bf16[32,16,384]{2,1,0:T(8,128)(2,1)S(1)}, u32[]{:S(2)}, u32[]{:S(2)}) async-start(bf16[32,16,384]{2,1,0:T(8,128)(2,1)} %broadcast_in_dim.69), calls=%async_computation | async-start | bytes 786432 | tf_op jit(solution)/shard_map/all_to_all | solution.py:45
  33.6 2.5 %slice-start = ((bf16[16,164737]{1,0:T(8,128)(2,1)}), bf16[16,163840]{1,0:T(8,128)(2,1)S(1)}, s32[]{:S(2)}) async-start(bf16[16,164737]{1,0:T(8,128)(2,1)} %tile.19), calls=%async_computation.3 | async-start | bytes 10485760 | tf_op jit(solution)/shard_map/slice | solution.py:30
  36.1 3.4 %copy-start.2 = (s32[16,512]{1,0:T(8,128)S(1)}, s32[16,512]{1,0:T(8,128)}, u32[]{:S(2)}) copy-start(s32[16,512]{1,0:T(8,128)} %param.6) | copy-start | bytes 98308
  36.1 4.0 %copy-start.1 = (s32[16,512]{1,0:T(8,128)S(1)}, s32[16,512]{1,0:T(8,128)}, u32[]{:S(2)}) copy-start(s32[16,512]{1,0:T(8,128)} %param.7) | copy-start | bytes 98308
  50.8 6.4 %slice-start.1 = ((bf16[16,384]{1,0:T(8,128)(2,1)}), bf16[16,256]{1,0:T(8,128)(2,1)S(1)}, s32[]{:S(2)}) async-start(bf16[16,384]{1,0:T(8,128)(2,1)} %copy-done), calls=%async_computation.4 | async-start | bytes 16384 | tf_op jit(solution)/shard_map/slice | solution.py:58
  63.5 18.5 %all-to-all-start.1 = ((f32[16,40,256]{2,1,0:T(8,128)}), f32[16,40,256]{2,1,0:T(8,128)S(1)}, u32[]{:S(2)}, u32[]{:S(2)}) async-start(f32[16,40,256]{2,1,0:T(8,128)} %bitcast.6), calls=%async_computation.1 | async-start | bytes 1310720 | tf_op jit(solution)/shard_map/all_to_all | solution.py:83

commit v19 on v15

--- a/solution.py
+++ b/solution.py
@@ -90,8 +90,9 @@
     own_first = first[lax.axis_index("seg")]
     dense = jnp.zeros((chan_devices, OFFBINS, LAGS), jnp.float32)
     dense = lax.dynamic_update_slice(dense, part.reshape(depth, OFFBINS, LAGS), (own_first, 0, 0))
-    pieces = lax.all_to_all(dense, "chan", 0, 0, tiled=True)
-    return jnp.sum(pieces, axis=0, keepdims=True)
+    tiles = dense.reshape(chan_devices, OFFBINS * LAGS // 128, 128)
+    pieces = lax.all_to_all(tiles, "chan", 0, 0, tiled=True)
+    return jnp.sum(pieces, axis=0).reshape(1, OFFBINS, LAGS)
 
 
 def solution(mesh):

time: 102 us -> 102 us (level)
  no operation moved by 1% of the time
where the time goes in v19:
time: 102 us; the launch traced here: 101 us
  starting transfers between devices  25.7 us (25%)
  local copies, waits for them, and re-layouts  22.9 us (22%)
  blocking collectives  22.4 us (22%)
  waiting for transfers between devices  13.3 us (13%)
  matrix products  8.07 us (8%)
  other arithmetic  6.82 us (7%)
  between operations  2.17 us (2%)
    all_to_all x1, blocking collectives, shards(): pieces = lax.all_to_all(tiles, 'chan', 0, 0, tiled=True)  22.4 us
    all_to_all x1, starting transfers between devices, shards(): lax.all_to_all(copies, 'chan', 0, 0, tiled=True).reshape(-1, flat.shape[1])  18.5 us
    another operation x2, local copies, waits for them, and re-layouts, toeplitz(): tiled = jnp.tile(ring, (1, lag_count + 1))[:, :lag_count * (width - 1)]  11.9 us
    all_to_all x1, waiting for transfers between devices, shards(): part = jnp.sum(lax.all_to_all(stacked, 'seg', 0, 0, tiled=True), axis=0)  8.71 us
    all_to_all x1, starting transfers between devices, shards(): part = jnp.sum(lax.all_to_all(stacked, 'seg', 0, 0, tiled=True), axis=0)  7.25 us
    all_to_all x1, waiting for transfers between devices, shards(): lax.all_to_all(copies, 'chan', 0, 0, tiled=True).reshape(-1, flat.shape[1])  4.56 us
    unnamed x5, local copies, waits for them, and re-layouts  4.3 us
    dot_general x1, matrix products, shards(): jnp.einsum('it,jkt->ijk', near, kernel, preferred_element_type=jnp.float32)  3.24 us
  transfers between devices with their start and end apart: 2, of which 2 were waited for; matrix products, arithmetic and copies ran while one was open for 19% of the time, Pallas kernels for 0%

profile of v19, /device:TPU:1, one launch (start us, length us, event | category | flops | bytes accessed | tf_op | source)
XLA Modules:
  0.0 101.4 jit_solution(14066597452877341013)
XLA Ops:
  0.0 0.8 fusion.22
  0.8 0.7 convert_element_type.28
  1.5 0.8 fusion.29
  2.3 0.8 broadcast_in_dim.66
  3.1 18.5 %all-to-all-start = ((bf16[32,16,384]{2,1,0:T(8,128)(2,1)}), bf16[32,16,384]{2,1,0:T(8,128)(2,1)S(1)}, u32[]{:S(2)}, u32[]{:S(2)}) async-start(bf16[32,16,384]{2,1,0:T(8,128)(2,1)} %broadcast_in_dim.66), calls=%async_computation | async-start | bytes 786432 | tf_op jit(solution)/shard_map/all_to_all | solution.py:45
  21.9 1.2 %slice.33 = s32[1,1]{1,0:T(1,128)} slice(s32[16,512]{1,0:T(8,128)} %param.6), slice={[0:1], [0:1]} | slice | bytes 8 | tf_op jit(solution)/shard_map/slice | solution.py:69
  23.1 0.8 multiply_add_fusion
  24.1 0.7 fusion.32
  25.2 3.1 %tile.18 = bf16[16,257,641]{2,1,0:T(8,128)(2,1)} broadcast(bf16[16,641]{1,0:T(8,128)(2,1)S(1)} %pad_maximum_fusion), dimensions={0,2} | broadcast | bytes 5292096 | tf_op jit(solution)/shard_map/tile | solution.py:30
  28.3 8.7 %tile.19 = bf16[16,164737]{1,0:T(8,128)(2,1)} reshape(bf16[16,257,641]{2,1,0:T(8,128)(2,1)} %tile.18) | data formatting | bytes 10543168 | tf_op jit(solution)/shard_map/tile | solution.py:30
  37.1 2.5 %slice-done = bf16[16,163840]{1,0:T(8,128)(2,1)S(1)} async-done(((bf16[16,164737]{1,0:T(8,128)(2,1)}), bf16[16,163840]{1,0:T(8,128)(2,1)S(1)}, s32[]{:S(2)}) %slice-start) | async-done | bytes 5242904 | tf_op jit(solution)/shard_map/slice | solution.py:30
  39.5 3.1 %copy.16 = bf16[2,8,256,640]{3,2,1,0:T(8,128)(2,1)} copy(bf16[2,8,256,640]{3,1,2,0:T(8,128)(2,1)S(1)} %bitcast.18) | data formatting | bytes 10485760
  42.7 4.6 %all-to-all-done = bf16[32,16,384]{2,1,0:T(8,128)(2,1)S(1)} async-done(((bf16[32,16,384]{2,1,0:T(8,128)(2,1)}), bf16[32,16,384]{2,1,0:T(8,128)(2,1)S(1)}, u32[]{:S(2)}, u32[]{:S(2)}) %all-to-all-start) | async-done | bytes 393248 | tf_op jit(solution)/shard_map/all_to_all | solution.py:45
  47.6 3.2 %fusion.14 = f32[272,16,256]{2,0,1:T(8,128)S(1)} fusion(bf16[16,256,640]{2,1,0:T(8,128)(2,1)} %bitcast.19, bf16[272,384]{1,0:T(8,128)(2,1)S(1)} %fusion.17), kind=kOutput, calls=%fused_computation.17 | convolution fusion | flops 855638016 | bytes 7811072 | tf_op jit(solution)/shard_map/it,jkt->ijk/dot_general | solution.py:56
  50.8 1.0 reduce-precision_convert_fusion
  51.8 3.1 %fusion.1 = f32[640,512]{1,0:T(8,128)S(1)} fusion(bf16[4352]{0:T(1024)(128)(2,1)S(1)} %broadcast_in_dim.63, s32[4352]{0:T(1024)S(1)} %eq.38, s32[640]{0:T(1024)S(1)} %add.115, bf16[4352,256]{1,0:T(8,128)(2,1)S(1)} %get-tuple-element.6, bf16[4352,256]{1,0:T(8,128)(2,1)S(1)} %get-tuple-element.5), kind=kOutput, calls=%fused_computation.2 | convolution fusion | flops 2866610176 | bytes 5795840 | tf_op jit(solution)/shard_map/dot_general | solution.py:80
  55.2 0.9 reverse
  56.7 1.6 %fusion = f32[640,2]{1,0:T(8,128)S(1)} fusion(bf16[4352]{0:T(1024)(128)(2,1)S(1)} %broadcast_in_dim.63, s32[4352]{0:T(1024)S(1)} %eq.38, s32[640]{0:T(1024)S(1)} %add.115, bf16[4352,1]{0,1:T(2,128)(2,1)S(1)} %get-tuple-element.8, bf16[4352,1]{0,1:T(2,128)(2,1)S(1)} %get-tuple-element.7), kind=kOutput, calls=%fused_computation.1 | convolution fusion | flops 16746496 | bytes 51200 | tf_op jit(solution)/shard_map/dot_general | solution.py:83
  58.5 1.1 %fusion.16 = f32[640,256]{1,0:T(8,128)} fusion(f32[640,255]{1,0:T(8,128)S(1)} %slice.60, f32[640,1]{1,0:T(8,128)S(1)} %slice_add_fusion.1, f32[640,512]{1,0:T(8,128)S(1)} %fusion.1), kind=kLoop, calls=%fused_computation.23 | loop fusion | flops 655360 | bytes 2621440 | tf_op jit(solution)/shard_map/mul | solution.py:88
  59.6 7.2 %all-to-all-start.1 = ((f32[16,40,256]{2,1,0:T(8,128)}), f32[16,40,256]{2,1,0:T(8,128)S(1)}, u32[]{:S(2)}, u32[]{:S(2)}) async-start(f32[16,40,256]{2,1,0:T(8,128)} %bitcast.7), calls=%async_computation.1 | async-start | bytes 1310720 | tf_op jit(solution)/shard_map/all_to_all | solution.py:89
  66.8 0.6 dynamic_slice.11
  69.4 8.7 %all-to-all-done.1 = f32[16,40,256]{2,1,0:T(8,128)S(1)} async-done(((f32[16,40,256]{2,1,0:T(8,128)}), f32[16,40,256]{2,1,0:T(8,128)S(1)}, u32[]{:S(2)}, u32[]{:S(2)}) %all-to-all-start.1) | async-done | bytes 655392 | tf_op jit(solution)/shard_map/all_to_all | solution.py:89
  78.3 22.4 %all_to_all.15 = f32[32,4,128]{2,1,0:T(4,128)S(1)} all-to-all(f32[32,4,128]{2,1,0:T(4,128)S(1)} %reshape.251), channel_id=1, replica_groups=mesh['chan'=32,'seg'=16] {'chan'}, dimensions={0} | all-to-all | bytes 131072 | tf_op jit(solution)/shard_map/all_to_all | solution.py:94
  100.8 0.6 reshape.252
  (36 shorter events, 2.5 us)
Async XLA Ops:
  2.3 34.8 %copy-start = (bf16[16,384]{1,0:T(8,128)(2,1)}, bf16[16,384]{1,0:T(8,128)(2,1)S(1)}, u32[]{:S(2)}) copy-start(bf16[16,384]{1,0:T(8,128)(2,1)S(1)} %fusion.29) | copy-start | bytes 36868
  3.1 44.2 %all-to-all-start = ((bf16[32,16,384]{2,1,0:T(8,128)(2,1)}), bf16[32,16,384]{2,1,0:T(8,128)(2,1)S(1)}, u32[]{:S(2)}, u32[]{:S(2)}) async-start(bf16[32,16,384]{2,1,0:T(8,128)(2,1)} %broadcast_in_dim.66), calls=%async_computation | async-start | bytes 786432 | tf_op jit(solution)/shard_map/all_to_all | solution.py:45
  37.1 2.5 %slice-start = ((bf16[16,164737]{1,0:T(8,128)(2,1)}), bf16[16,163840]{1,0:T(8,128)(2,1)S(1)}, s32[]{:S(2)}) async-start(bf16[16,164737]{1,0:T(8,128)(2,1)} %tile.19), calls=%async_computation.3 | async-start | bytes 10485760 | tf_op jit(solution)/shard_map/slice | solution.py:30
  54.9 1.5 %slice-start.1 = ((bf16[16,384]{1,0:T(8,128)(2,1)}), bf16[16,256]{1,0:T(8,128)(2,1)S(1)}, s32[]{:S(2)}) async-start(bf16[16,384]{1,0:T(8,128)(2,1)} %copy-done), calls=%async_computation.4 | async-start | bytes 16384 | tf_op jit(solution)/shard_map/slice | solution.py:58
  59.6 18.5 %all-to-all-start.1 = ((f32[16,40,256]{2,1,0:T(8,128)}), f32[16,40,256]{2,1,0:T(8,128)S(1)}, u32[]{:S(2)}, u32[]{:S(2)}) async-start(f32[16,40,256]{2,1,0:T(8,128)} %bitcast.7), calls=%async_computation.1 | async-start | bytes 1310720 | tf_op jit(solution)/shard_map/all_to_all | solution.py:89

commit v20 on v16

--- a/solution.py
+++ b/solution.py
@@ -90,8 +90,9 @@
     own_first = first[lax.axis_index("seg")]
     dense = jnp.zeros((chan_devices, OFFBINS, LAGS), jnp.float32)
     dense = lax.dynamic_update_slice(dense, part.reshape(depth, OFFBINS, LAGS), (own_first, 0, 0))
-    pieces = lax.all_to_all(dense, "chan", 0, 0, tiled=True)
-    summed = jnp.sum(pieces, axis=0, keepdims=True)
+    tiles = dense.reshape(chan_devices, OFFBINS * LAGS // 128, 128)
+    pieces = lax.all_to_all(tiles, "chan", 0, 0, tiled=True)
+    summed = jnp.sum(pieces, axis=0).reshape(1, OFFBINS, LAGS)
     flipped = jnp.flip(summed[:, :, 1:], axis=2)
     return summed + jnp.concatenate([jnp.zeros_like(summed[:, :, :1]), flipped], axis=2)
 

time: 102 us -> 102 us (level)
  no operation moved by 1% of the time
where the time goes in v20:
time: 102 us; the launch traced here: 101 us
  starting transfers between devices  25.7 us (25%)
  blocking collectives  22.4 us (22%)
  local copies, waits for them, and re-layouts  21.2 us (21%)
  waiting for transfers between devices  13.3 us (13%)
  other arithmetic  8.58 us (8%)
  matrix products  8.07 us (8%)
  between operations  2.16 us (2%)
    all_to_all x1, blocking collectives, shards(): pieces = lax.all_to_all(tiles, 'chan', 0, 0, tiled=True)  22.4 us
    all_to_all x1, starting transfers between devices, shards(): lax.all_to_all(copies, 'chan', 0, 0, tiled=True).reshape(-1, flat.shape[1])  18.5 us
    another operation x2, local copies, waits for them, and re-layouts, toeplitz(): tiled = jnp.tile(ring, (1, lag_count + 1))[:, :lag_count * (width - 1)]  11.9 us
    all_to_all x1, waiting for transfers between devices, shards(): part = jnp.sum(lax.all_to_all(stacked, 'seg', 0, 0, tiled=True), axis=0)  8.71 us
    all_to_all x1, starting transfers between devices, shards(): part = jnp.sum(lax.all_to_all(stacked, 'seg', 0, 0, tiled=True), axis=0)  7.25 us
    all_to_all x1, waiting for transfers between devices, shards(): lax.all_to_all(copies, 'chan', 0, 0, tiled=True).reshape(-1, flat.shape[1])  4.56 us
    unnamed x7, local copies, waits for them, and re-layouts  3.42 us
    dot_general x1, matrix products, shards(): jnp.einsum('it,jkt->ijk', near, kernel, preferred_element_type=jnp.float32)  3.27 us
  transfers between devices with their start and end apart: 2, of which 2 were waited for; matrix products, arithmetic and copies ran while one was open for 19% of the time, Pallas kernels for 0%

profile of v20, /device:TPU:1, one launch (start us, length us, event | category | flops | bytes accessed | tf_op | source)
XLA Modules:
  0.0 101.5 jit_solution(7801563641238792622)
XLA Ops:
  0.0 0.8 fusion.23
  0.8 0.7 convert_element_type.28
  1.5 0.8 fusion.30
  2.3 0.8 broadcast_in_dim.89
  3.1 18.5 %all-to-all-start = ((bf16[32,16,384]{2,1,0:T(8,128)(2,1)}), bf16[32,16,384]{2,1,0:T(8,128)(2,1)S(1)}, u32[]{:S(2)}, u32[]{:S(2)}) async-start(bf16[32,16,384]{2,1,0:T(8,128)(2,1)} %broadcast_in_dim.89), calls=%async_computation | async-start | bytes 786432 | tf_op jit(solution)/shard_map/all_to_all | solution.py:45
  21.9 1.2 %slice.33 = s32[1,1]{1,0:T(1,128)} slice(s32[16,512]{1,0:T(8,128)} %param.6), slice={[0:1], [0:1]} | slice | bytes 8 | tf_op jit(solution)/shard_map/slice | solution.py:69
  23.1 0.8 multiply_add_fusion
  24.1 0.7 fusion.34
  25.2 3.1 %tile.18 = bf16[16,257,641]{2,1,0:T(8,128)(2,1)} broadcast(bf16[16,641]{1,0:T(8,128)(2,1)S(1)} %pad_maximum_fusion), dimensions={0,2} | broadcast | bytes 5292096 | tf_op jit(solution)/shard_map/tile | solution.py:30
  28.3 8.7 %tile.19 = bf16[16,164737]{1,0:T(8,128)(2,1)} reshape(bf16[16,257,641]{2,1,0:T(8,128)(2,1)} %tile.18) | data formatting | bytes 10543168 | tf_op jit(solution)/shard_map/tile | solution.py:30
  37.0 2.5 %slice-done = bf16[16,163840]{1,0:T(8,128)(2,1)S(1)} async-done(((bf16[16,164737]{1,0:T(8,128)(2,1)}), bf16[16,163840]{1,0:T(8,128)(2,1)S(1)}, s32[]{:S(2)}) %slice-start) | async-done | bytes 5242904 | tf_op jit(solution)/shard_map/slice | solution.py:30
  39.5 3.2 %copy.7 = bf16[2,8,256,640]{3,2,1,0:T(8,128)(2,1)} copy(bf16[2,8,256,640]{3,1,2,0:T(8,128)(2,1)S(1)} %bitcast.18) | data formatting | bytes 10485760
  42.7 4.6 %all-to-all-done = bf16[32,16,384]{2,1,0:T(8,128)(2,1)S(1)} async-done(((bf16[32,16,384]{2,1,0:T(8,128)(2,1)}), bf16[32,16,384]{2,1,0:T(8,128)(2,1)S(1)}, u32[]{:S(2)}, u32[]{:S(2)}) %all-to-all-start) | async-done | bytes 393248 | tf_op jit(solution)/shard_map/all_to_all | solution.py:45
  47.2 0.3 fusion.18
  47.6 3.3 %fusion.14 = f32[272,16,256]{2,0,1:T(8,128)S(1)} fusion(bf16[16,256,640]{2,1,0:T(8,128)(2,1)} %bitcast.19, bf16[272,384]{1,0:T(8,128)(2,1)S(1)} %fusion.18), kind=kOutput, calls=%fused_computation.17 | convolution fusion | flops 855638016 | bytes 7811072 | tf_op jit(solution)/shard_map/it,jkt->ijk/dot_general | solution.py:56
  50.9 2.4 %reduce-precision_convert_fusion = (bf16[4352,256]{1,0:T(8,128)(2,1)S(1)}, bf16[4352,256]{1,0:T(8,128)(2,1)}) fusion(f32[272,16,256]{2,0,1:T(8,128)S(1)} %fusion.14), kind=kLoop, calls=%fused_computation.4 | loop fusion | flops 4456448 | bytes 8912896 | tf_op jit(solution)/shard_map/convert.2
  53.6 1.6 %fusion = f32[640,2]{0,1:T(2,128)S(1)} fusion(bf16[4352]{0:T(1024)(128)(2,1)S(1)} %broadcast_in_dim.86, s32[4352]{0:T(1024)S(1)} %eq.49, s32[640]{0:T(1024)S(1)} %add.120, bf16[4352,1]{0,1:T(2,128)(2,1)S(1)} %get-tuple-element.8, bf16[4352,1]{0,1:T(2,128)(2,1)S(1)} %get-tuple-element.7), kind=kOutput, calls=%fused_computation.1 | convolution fusion | flops 16746496 | bytes 51200 | tf_op jit(solution)/shard_map/dot_general | solution.py:83
  55.2 3.1 %fusion.1 = f32[640,512]{1,0:T(8,128)S(1)} fusion(bf16[4352]{0:T(1024)(128)(2,1)S(1)} %broadcast_in_dim.86, s32[4352]{0:T(1024)S(1)} %eq.49, s32[640]{0:T(1024)S(1)} %add.120, bf16[4352,256]{1,0:T(8,128)(2,1)S(1)} %copy-done, bf16[4352,256]{1,0:T(8,128)(2,1)S(1)} %get-tuple-element.5), kind=kOutput, calls=%fused_computation.2 | convolution fusion | flops 2866610176 | bytes 5795840 | tf_op jit(solution)/shard_map/dot_general | solution.py:80
  58.3 1.0 fusion.17
  59.3 7.2 %all-to-all-start.1 = ((f32[16,40,256]{2,1,0:T(8,128)}), f32[16,40,256]{2,1,0:T(8,128)S(1)}, u32[]{:S(2)}, u32[]{:S(2)}) async-start(f32[16,40,256]{2,1,0:T(8,128)} %bitcast.7), calls=%async_computation.1 | async-start | bytes 1310720 | tf_op jit(solution)/shard_map/all_to_all | solution.py:89
  66.5 0.6 dynamic_slice.11
  69.1 8.7 %all-to-all-done.1 = f32[16,40,256]{2,1,0:T(8,128)S(1)} async-done(((f32[16,40,256]{2,1,0:T(8,128)}), f32[16,40,256]{2,1,0:T(8,128)S(1)}, u32[]{:S(2)}, u32[]{:S(2)}) %all-to-all-start.1) | async-done | bytes 655392 | tf_op jit(solution)/shard_map/all_to_all | solution.py:89
  78.0 22.4 %all_to_all.15 = f32[32,4,128]{2,1,0:T(4,128)S(1)} all-to-all(f32[32,4,128]{2,1,0:T(4,128)S(1)} %reshape.256), channel_id=1, replica_groups=mesh['chan'=32,'seg'=16] {'chan'}, dimensions={0} | all-to-all | bytes 131072 | tf_op jit(solution)/shard_map/all_to_all | solution.py:94
  100.8 0.7 pad_add_fusion
  (39 shorter events, 1.8 us)
Async XLA Ops:
  2.3 34.7 %copy-start.1 = (bf16[16,384]{1,0:T(8,128)(2,1)}, bf16[16,384]{1,0:T(8,128)(2,1)S(1)}, u32[]{:S(2)}) copy-start(bf16[16,384]{1,0:T(8,128)(2,1)S(1)} %fusion.30) | copy-start | bytes 36868
  3.1 44.2 %all-to-all-start = ((bf16[32,16,384]{2,1,0:T(8,128)(2,1)}), bf16[32,16,384]{2,1,0:T(8,128)(2,1)S(1)}, u32[]{:S(2)}, u32[]{:S(2)}) async-start(bf16[32,16,384]{2,1,0:T(8,128)(2,1)} %broadcast_in_dim.89), calls=%async_computation | async-start | bytes 786432 | tf_op jit(solution)/shard_map/all_to_all | solution.py:45
  37.0 2.5 %slice-start = ((bf16[16,164737]{1,0:T(8,128)(2,1)}), bf16[16,163840]{1,0:T(8,128)(2,1)S(1)}, s32[]{:S(2)}) async-start(bf16[16,164737]{1,0:T(8,128)(2,1)} %tile.19), calls=%async_computation.3 | async-start | bytes 10485760 | tf_op jit(solution)/shard_map/slice | solution.py:30
  50.9 2.4 %slice-start.1 = ((bf16[16,384]{1,0:T(8,128)(2,1)}), bf16[16,256]{1,0:T(8,128)(2,1)S(1)}, s32[]{:S(2)}) async-start(bf16[16,384]{1,0:T(8,128)(2,1)} %copy-done.1), calls=%async_computation.4 | async-start | bytes 16384 | tf_op jit(solution)/shard_map/slice | solution.py:58
  53.5 1.7 %copy-start = (bf16[4352,256]{1,0:T(8,128)(2,1)S(1)}, bf16[4352,256]{1,0:T(8,128)(2,1)}, u32[]{:S(2)}) copy-start(bf16[4352,256]{1,0:T(8,128)(2,1)} %get-tuple-element.6) | copy-start | bytes 6684676
  59.3 18.5 %all-to-all-start.1 = ((f32[16,40,256]{2,1,0:T(8,128)}), f32[16,40,256]{2,1,0:T(8,128)S(1)}, u32[]{:S(2)}, u32[]{:S(2)}) async-start(f32[16,40,256]{2,1,0:T(8,128)} %bitcast.7), calls=%async_computation.1 | async-start | bytes 1310720 | tf_op jit(solution)/shard_map/all_to_all | solution.py:89

commit v21 on v15

--- a/solution.py
+++ b/solution.py
@@ -40,7 +40,7 @@
     kernel = toeplitz(normed, LAGS)
     first_row = lax.axis_index("chan") * chan_count
     own_rows = first_row + jnp.arange(chan_count, dtype=jnp.int32)[None, :]
-    flat = lax.optimization_barrier(normed.reshape(chan_count, -1))
+    flat = normed.reshape(chan_count, -1)
     copies = jnp.broadcast_to(flat[None], (chan_devices,) + flat.shape)
     piece = lax.all_to_all(copies, "chan", 0, 0, tiled=True).reshape(-1, flat.shape[1])
     row_count = piece.shape[0]

time: 102 us -> 102 us (level)
    unnamed x5 -> x3, local copies, waits for them, and re-layouts: 4.3 us -> 4.3 us
where the time goes in v21:
time: 102 us; the launch traced here: 101 us
  starting transfers between devices  25.7 us (25%)
  blocking collectives  22.4 us (22%)
  local copies, waits for them, and re-layouts  22.2 us (22%)
  waiting for transfers between devices  13.3 us (13%)
  matrix products  8.08 us (8%)
  other arithmetic  7.41 us (7%)
  between operations  2.14 us (2%)
    all_to_all x1, blocking collectives, shards(): pieces = lax.all_to_all(dense, 'chan', 0, 0, tiled=True)  22.4 us
    all_to_all x1, starting transfers between devices, shards(): lax.all_to_all(copies, 'chan', 0, 0, tiled=True).reshape(-1, flat.shape[1])  18.5 us
    another operation x2, local copies, waits for them, and re-layouts, toeplitz(): tiled = jnp.tile(ring, (1, lag_count + 1))[:, :lag_count * (width - 1)]  11.9 us
    all_to_all x1, waiting for transfers between devices, shards(): part = jnp.sum(lax.all_to_all(stacked, 'seg', 0, 0, tiled=True), axis=0)  8.71 us
    all_to_all x1, starting transfers between devices, shards(): part = jnp.sum(lax.all_to_all(stacked, 'seg', 0, 0, tiled=True), axis=0)  7.25 us
    all_to_all x1, waiting for transfers between devices, shards(): lax.all_to_all(copies, 'chan', 0, 0, tiled=True).reshape(-1, flat.shape[1])  4.57 us
    unnamed x3, local copies, waits for them, and re-layouts  4.3 us
    dot_general x1, matrix products, shards(): jnp.einsum('it,jkt->ijk', near, kernel, preferred_element_type=jnp.float32)  3.24 us
  transfers between devices with their start and end apart: 2, of which 2 were waited for; matrix products, arithmetic and copies ran while one was open for 19% of the time, Pallas kernels for 0%

profile of v21, /device:TPU:1, one launch (start us, length us, event | category | flops | bytes accessed | tf_op | source)
XLA Modules:
  0.0 101.2 jit_solution(12134720660603609513)
XLA Ops:
  0.0 0.8 fusion.22
  0.8 0.7 convert_element_type.28
  1.5 0.8 fusion.29
  2.3 0.8 broadcast_in_dim.71
  3.1 18.5 %all-to-all-start = ((bf16[32,16,384]{2,1,0:T(8,128)(2,1)}), bf16[32,16,384]{2,1,0:T(8,128)(2,1)S(1)}, u32[]{:S(2)}, u32[]{:S(2)}) async-start(bf16[32,16,384]{2,1,0:T(8,128)(2,1)} %broadcast_in_dim.71), calls=%async_computation | async-start | bytes 786432 | tf_op jit(solution)/shard_map/all_to_all | solution.py:45
  21.9 1.2 %slice.33 = s32[1,1]{1,0:T(1,128)} slice(s32[16,512]{1,0:T(8,128)} %param.6), slice={[0:1], [0:1]} | slice | bytes 8 | tf_op jit(solution)/shard_map/slice | solution.py:69
  23.1 0.8 multiply_add_fusion
  24.0 0.7 fusion.32
  25.2 3.1 %tile.18 = bf16[16,257,641]{2,1,0:T(8,128)(2,1)} broadcast(bf16[16,641]{1,0:T(8,128)(2,1)S(1)} %pad_maximum_fusion), dimensions={0,2} | broadcast | bytes 5292096 | tf_op jit(solution)/shard_map/tile | solution.py:30
  28.3 8.7 %tile.19 = bf16[16,164737]{1,0:T(8,128)(2,1)} reshape(bf16[16,257,641]{2,1,0:T(8,128)(2,1)} %tile.18) | data formatting | bytes 10543168 | tf_op jit(solution)/shard_map/tile | solution.py:30
  37.0 2.5 %slice-done = bf16[16,163840]{1,0:T(8,128)(2,1)S(1)} async-done(((bf16[16,164737]{1,0:T(8,128)(2,1)}), bf16[16,163840]{1,0:T(8,128)(2,1)S(1)}, s32[]{:S(2)}) %slice-start) | async-done | bytes 5242904 | tf_op jit(solution)/shard_map/slice | solution.py:30
  39.5 3.2 %copy.19 = bf16[2,8,256,640]{3,2,1,0:T(8,128)(2,1)} copy(bf16[2,8,256,640]{3,1,2,0:T(8,128)(2,1)S(1)} %bitcast.19) | data formatting | bytes 10485760
  42.7 4.6 %all-to-all-done = bf16[32,16,384]{2,1,0:T(8,128)(2,1)S(1)} async-done(((bf16[32,16,384]{2,1,0:T(8,128)(2,1)}), bf16[32,16,384]{2,1,0:T(8,128)(2,1)S(1)}, u32[]{:S(2)}, u32[]{:S(2)}) %all-to-all-start) | async-done | bytes 393248 | tf_op jit(solution)/shard_map/all_to_all | solution.py:45
  47.6 3.2 %fusion.14 = f32[272,16,256]{2,0,1:T(8,128)S(1)} fusion(bf16[16,256,640]{2,1,0:T(8,128)(2,1)} %bitcast.20, bf16[272,384]{1,0:T(8,128)(2,1)S(1)} %fusion.17), kind=kOutput, calls=%fused_computation.17 | convolution fusion | flops 855638016 | bytes 7811072 | tf_op jit(solution)/shard_map/it,jkt->ijk/dot_general | solution.py:56
  50.8 1.0 reduce-precision_convert_fusion
  51.8 3.1 %fusion.1 = f32[640,512]{1,0:T(8,128)S(1)} fusion(bf16[4352]{0:T(1024)(128)(2,1)S(1)} %broadcast_in_dim.67, s32[4352]{0:T(1024)S(1)} %eq.38, s32[640]{0:T(1024)S(1)} %add.115, bf16[4352,256]{1,0:T(8,128)(2,1)S(1)} %get-tuple-element.6, bf16[4352,256]{1,0:T(8,128)(2,1)S(1)} %get-tuple-element.5), kind=kOutput, calls=%fused_computation.2 | convolution fusion | flops 2866610176 | bytes 5795840 | tf_op jit(solution)/shard_map/dot_general | solution.py:80
  55.2 0.9 reverse
  56.7 1.6 %fusion = f32[640,2]{1,0:T(8,128)S(1)} fusion(bf16[4352]{0:T(1024)(128)(2,1)S(1)} %broadcast_in_dim.67, s32[4352]{0:T(1024)S(1)} %eq.38, s32[640]{0:T(1024)S(1)} %add.115, bf16[4352,1]{0,1:T(2,128)(2,1)S(1)} %get-tuple-element.8, bf16[4352,1]{0,1:T(2,128)(2,1)S(1)} %get-tuple-element.7), kind=kOutput, calls=%fused_computation.1 | convolution fusion | flops 16746496 | bytes 51200 | tf_op jit(solution)/shard_map/dot_general | solution.py:83
  58.5 1.1 %fusion.16 = f32[640,256]{1,0:T(8,128)} fusion(f32[640,255]{1,0:T(8,128)S(1)} %slice.60, f32[640,1]{1,0:T(8,128)S(1)} %slice_add_fusion.1, f32[640,512]{1,0:T(8,128)S(1)} %fusion.1), kind=kLoop, calls=%fused_computation.23 | loop fusion | flops 655360 | bytes 2621440 | tf_op jit(solution)/shard_map/mul | solution.py:88
  59.6 7.2 %all-to-all-start.1 = ((f32[16,40,256]{2,1,0:T(8,128)}), f32[16,40,256]{2,1,0:T(8,128)S(1)}, u32[]{:S(2)}, u32[]{:S(2)}) async-start(f32[16,40,256]{2,1,0:T(8,128)} %bitcast.7), calls=%async_computation.1 | async-start | bytes 1310720 | tf_op jit(solution)/shard_map/all_to_all | solution.py:89
  66.8 0.6 dynamic_slice.11
  69.3 8.7 %all-to-all-done.1 = f32[16,40,256]{2,1,0:T(8,128)S(1)} async-done(((f32[16,40,256]{2,1,0:T(8,128)}), f32[16,40,256]{2,1,0:T(8,128)S(1)}, u32[]{:S(2)}, u32[]{:S(2)}) %all-to-all-start.1) | async-done | bytes 655392 | tf_op jit(solution)/shard_map/all_to_all | solution.py:89
  78.2 22.4 %all_to_all.15 = f32[32,2,256]{2,1,0:T(2,128)S(1)} all-to-all(f32[32,2,256]{2,1,0:T(2,128)S(1)} %constant_dynamic-update-slice_fusion), channel_id=1, replica_groups=mesh['chan'=32,'seg'=16] {'chan'}, dimensions={0} | all-to-all | bytes 131072 | tf_op jit(solution)/shard_map/all_to_all | solution.py:93
  100.6 0.6 reduce_sum.29
  (30 shorter events, 2.3 us)
Async XLA Ops:
  3.1 44.2 %all-to-all-start = ((bf16[32,16,384]{2,1,0:T(8,128)(2,1)}), bf16[32,16,384]{2,1,0:T(8,128)(2,1)S(1)}, u32[]{:S(2)}, u32[]{:S(2)}) async-start(bf16[32,16,384]{2,1,0:T(8,128)(2,1)} %broadcast_in_dim.71), calls=%async_computation | async-start | bytes 786432 | tf_op jit(solution)/shard_map/all_to_all | solution.py:45
  37.0 2.5 %slice-start = ((bf16[16,164737]{1,0:T(8,128)(2,1)}), bf16[16,163840]{1,0:T(8,128)(2,1)S(1)}, s32[]{:S(2)}) async-start(bf16[16,164737]{1,0:T(8,128)(2,1)} %tile.19), calls=%async_computation.3 | async-start | bytes 10485760 | tf_op jit(solution)/shard_map/slice | solution.py:30
  59.6 18.5 %all-to-all-start.1 = ((f32[16,40,256]{2,1,0:T(8,128)}), f32[16,40,256]{2,1,0:T(8,128)S(1)}, u32[]{:S(2)}, u32[]{:S(2)}) async-start(f32[16,40,256]{2,1,0:T(8,128)} %bitcast.7), calls=%async_computation.1 | async-start | bytes 1310720 | tf_op jit(solution)/shard_map/all_to_all | solution.py:89

commit v22 on v16

--- a/solution.py
+++ b/solution.py
@@ -40,7 +40,7 @@
     kernel = toeplitz(normed, LAGS)
     first_row = lax.axis_index("chan") * chan_count
     own_rows = first_row + jnp.arange(chan_count, dtype=jnp.int32)[None, :]
-    flat = lax.optimization_barrier(normed.reshape(chan_count, -1))
+    flat = normed.reshape(chan_count, -1)
     copies = jnp.broadcast_to(flat[None], (chan_devices,) + flat.shape)
     piece = lax.all_to_all(copies, "chan", 0, 0, tiled=True).reshape(-1, flat.shape[1])
     row_count = piece.shape[0]

time: 102 us -> 102 us (level)
    unnamed x7 -> x5, local copies, waits for them, and re-layouts: 3.42 us -> 3.43 us
where the time goes in v22:
time: 102 us; the launch traced here: 101 us
  starting transfers between devices  25.7 us (25%)
  blocking collectives  22.5 us (22%)
  local copies, waits for them, and re-layouts  21.1 us (21%)
  waiting for transfers between devices  13.3 us (13%)
  other arithmetic  8.58 us (8%)
  matrix products  8.07 us (8%)
  between operations  2.13 us (2%)
    all_to_all x1, blocking collectives, shards(): pieces = lax.all_to_all(dense, 'chan', 0, 0, tiled=True)  22.5 us
    all_to_all x1, starting transfers between devices, shards(): lax.all_to_all(copies, 'chan', 0, 0, tiled=True).reshape(-1, flat.shape[1])  18.5 us
    another operation x2, local copies, waits for them, and re-layouts, toeplitz(): tiled = jnp.tile(ring, (1, lag_count + 1))[:, :lag_count * (width - 1)]  11.9 us
    all_to_all x1, waiting for transfers between devices, shards(): part = jnp.sum(lax.all_to_all(stacked, 'seg', 0, 0, tiled=True), axis=0)  8.71 us
    all_to_all x1, starting transfers between devices, shards(): part = jnp.sum(lax.all_to_all(stacked, 'seg', 0, 0, tiled=True), axis=0)  7.25 us
    all_to_all x1, waiting for transfers between devices, shards(): lax.all_to_all(copies, 'chan', 0, 0, tiled=True).reshape(-1, flat.shape[1])  4.55 us
    unnamed x5, local copies, waits for them, and re-layouts  3.43 us
    dot_general x1, matrix products, shards(): jnp.einsum('it,jkt->ijk', near, kernel, preferred_element_type=jnp.float32)  3.27 us
  transfers between devices with their start and end apart: 2, of which 2 were waited for; matrix products, arithmetic and copies ran while one was open for 19% of the time, Pallas kernels for 0%

profile of v22, /device:TPU:1, one launch (start us, length us, event | category | flops | bytes accessed | tf_op | source)
XLA Modules:
  0.0 101.4 jit_solution(7784609083701460701)
XLA Ops:
  0.0 0.8 fusion.23
  0.8 0.7 convert_element_type.28
  1.5 0.8 fusion.30
  2.3 0.8 broadcast_in_dim.94
  3.1 18.5 %all-to-all-start = ((bf16[32,16,384]{2,1,0:T(8,128)(2,1)}), bf16[32,16,384]{2,1,0:T(8,128)(2,1)S(1)}, u32[]{:S(2)}, u32[]{:S(2)}) async-start(bf16[32,16,384]{2,1,0:T(8,128)(2,1)} %broadcast_in_dim.94), calls=%async_computation | async-start | bytes 786432 | tf_op jit(solution)/shard_map/all_to_all | solution.py:45
  21.9 1.2 %slice.33 = s32[1,1]{1,0:T(1,128)} slice(s32[16,512]{1,0:T(8,128)} %param.6), slice={[0:1], [0:1]} | slice | bytes 8 | tf_op jit(solution)/shard_map/slice | solution.py:69
  23.1 0.8 multiply_add_fusion
  24.0 0.7 fusion.34
  25.2 3.1 %tile.18 = bf16[16,257,641]{2,1,0:T(8,128)(2,1)} broadcast(bf16[16,641]{1,0:T(8,128)(2,1)S(1)} %pad_maximum_fusion), dimensions={0,2} | broadcast | bytes 5292096 | tf_op jit(solution)/shard_map/tile | solution.py:30
  28.3 8.7 %tile.19 = bf16[16,164737]{1,0:T(8,128)(2,1)} reshape(bf16[16,257,641]{2,1,0:T(8,128)(2,1)} %tile.18) | data formatting | bytes 10543168 | tf_op jit(solution)/shard_map/tile | solution.py:30
  37.0 2.5 %slice-done = bf16[16,163840]{1,0:T(8,128)(2,1)S(1)} async-done(((bf16[16,164737]{1,0:T(8,128)(2,1)}), bf16[16,163840]{1,0:T(8,128)(2,1)S(1)}, s32[]{:S(2)}) %slice-start) | async-done | bytes 5242904 | tf_op jit(solution)/shard_map/slice | solution.py:30
  39.5 3.2 %copy.8 = bf16[2,8,256,640]{3,2,1,0:T(8,128)(2,1)} copy(bf16[2,8,256,640]{3,1,2,0:T(8,128)(2,1)S(1)} %bitcast.20) | data formatting | bytes 10485760
  42.7 4.5 %all-to-all-done = bf16[32,16,384]{2,1,0:T(8,128)(2,1)S(1)} async-done(((bf16[32,16,384]{2,1,0:T(8,128)(2,1)}), bf16[32,16,384]{2,1,0:T(8,128)(2,1)S(1)}, u32[]{:S(2)}, u32[]{:S(2)}) %all-to-all-start) | async-done | bytes 393248 | tf_op jit(solution)/shard_map/all_to_all | solution.py:45
  47.2 0.3 fusion.18
  47.6 3.3 %fusion.14 = f32[272,16,256]{2,0,1:T(8,128)S(1)} fusion(bf16[16,256,640]{2,1,0:T(8,128)(2,1)} %bitcast.21, bf16[272,384]{1,0:T(8,128)(2,1)S(1)} %fusion.18), kind=kOutput, calls=%fused_computation.17 | convolution fusion | flops 855638016 | bytes 7811072 | tf_op jit(solution)/shard_map/it,jkt->ijk/dot_general | solution.py:56
  50.8 2.4 %reduce-precision_convert_fusion = (bf16[4352,256]{1,0:T(8,128)(2,1)S(1)}, bf16[4352,256]{1,0:T(8,128)(2,1)}) fusion(f32[272,16,256]{2,0,1:T(8,128)S(1)} %fusion.14), kind=kLoop, calls=%fused_computation.4 | loop fusion | flops 4456448 | bytes 8912896 | tf_op jit(solution)/shard_map/convert.2
  53.5 1.6 %fusion = f32[640,2]{0,1:T(2,128)S(1)} fusion(bf16[4352]{0:T(1024)(128)(2,1)S(1)} %broadcast_in_dim.90, s32[4352]{0:T(1024)S(1)} %eq.49, s32[640]{0:T(1024)S(1)} %add.120, bf16[4352,1]{0,1:T(2,128)(2,1)S(1)} %get-tuple-element.8, bf16[4352,1]{0,1:T(2,128)(2,1)S(1)} %get-tuple-element.7), kind=kOutput, calls=%fused_computation.1 | convolution fusion | flops 16746496 | bytes 51200 | tf_op jit(solution)/shard_map/dot_general | solution.py:83
  55.2 3.1 %fusion.1 = f32[640,512]{1,0:T(8,128)S(1)} fusion(bf16[4352]{0:T(1024)(128)(2,1)S(1)} %broadcast_in_dim.90, s32[4352]{0:T(1024)S(1)} %eq.49, s32[640]{0:T(1024)S(1)} %add.120, bf16[4352,256]{1,0:T(8,128)(2,1)S(1)} %copy-done, bf16[4352,256]{1,0:T(8,128)(2,1)S(1)} %get-tuple-element.5), kind=kOutput, calls=%fused_computation.2 | convolution fusion | flops 2866610176 | bytes 5795840 | tf_op jit(solution)/shard_map/dot_general | solution.py:80
  58.3 1.0 fusion.17
  59.3 7.2 %all-to-all-start.1 = ((f32[16,40,256]{2,1,0:T(8,128)}), f32[16,40,256]{2,1,0:T(8,128)S(1)}, u32[]{:S(2)}, u32[]{:S(2)}) async-start(f32[16,40,256]{2,1,0:T(8,128)} %bitcast.7), calls=%async_computation.1 | async-start | bytes 1310720 | tf_op jit(solution)/shard_map/all_to_all | solution.py:89
  66.5 0.6 dynamic_slice.11
  69.0 8.7 %all-to-all-done.1 = f32[16,40,256]{2,1,0:T(8,128)S(1)} async-done(((f32[16,40,256]{2,1,0:T(8,128)}), f32[16,40,256]{2,1,0:T(8,128)S(1)}, u32[]{:S(2)}, u32[]{:S(2)}) %all-to-all-start.1) | async-done | bytes 655392 | tf_op jit(solution)/shard_map/all_to_all | solution.py:89
  77.9 22.5 %all_to_all.15 = f32[32,2,256]{2,1,0:T(2,128)S(1)} all-to-all(f32[32,2,256]{2,1,0:T(2,128)S(1)} %constant_dynamic-update-slice_fusion), channel_id=1, replica_groups=mesh['chan'=32,'seg'=16] {'chan'}, dimensions={0} | all-to-all | bytes 131072 | tf_op jit(solution)/shard_map/all_to_all | solution.py:93
  100.7 0.7 pad_add_fusion
  (33 shorter events, 1.7 us)
Async XLA Ops:
  3.1 44.2 %all-to-all-start = ((bf16[32,16,384]{2,1,0:T(8,128)(2,1)}), bf16[32,16,384]{2,1,0:T(8,128)(2,1)S(1)}, u32[]{:S(2)}, u32[]{:S(2)}) async-start(bf16[32,16,384]{2,1,0:T(8,128)(2,1)} %broadcast_in_dim.94), calls=%async_computation | async-start | bytes 786432 | tf_op jit(solution)/shard_map/all_to_all | solution.py:45
  37.0 2.5 %slice-start = ((bf16[16,164737]{1,0:T(8,128)(2,1)}), bf16[16,163840]{1,0:T(8,128)(2,1)S(1)}, s32[]{:S(2)}) async-start(bf16[16,164737]{1,0:T(8,128)(2,1)} %tile.19), calls=%async_computation.3 | async-start | bytes 10485760 | tf_op jit(solution)/shard_map/slice | solution.py:30
  53.5 1.7 %copy-start = (bf16[4352,256]{1,0:T(8,128)(2,1)S(1)}, bf16[4352,256]{1,0:T(8,128)(2,1)}, u32[]{:S(2)}) copy-start(bf16[4352,256]{1,0:T(8,128)(2,1)} %get-tuple-element.6) | copy-start | bytes 6684676
  59.3 18.5 %all-to-all-start.1 = ((f32[16,40,256]{2,1,0:T(8,128)}), f32[16,40,256]{2,1,0:T(8,128)S(1)}, u32[]{:S(2)}, u32[]{:S(2)}) async-start(f32[16,40,256]{2,1,0:T(8,128)} %bitcast.7), calls=%async_computation.1 | async-start | bytes 1310720 | tf_op jit(solution)/shard_map/all_to_all | solution.py:89
